TPU v7x, 256 devices: a whole 4x4x8 slice. The times are simulated.
256 devices in a mesh: gx: 64 (over y, z, core), gz: 4 (over x).
Axes of the slice: x: 4, y: 4, z: 8, core: 2. Of those that a mesh axis runs over, the one named last changes fastest.
Arguments:
- field: float32 [4, 4, 512, 8192], P(None, 'gz', None, 'gx'), may hold values from -6 to 6
- drop_cell: int32 [1048576], P(('gx', 'gz')), may hold values from 0 to 65535
- drop_plane: int32 [1048576], P(('gx', 'gz')), may hold values from 0 to 3
- drop_rate: float32 [2, 1048576], P(None, ('gx', 'gz')), may hold values from -8 to 8
- diffusivity: float32 [4], replicated, may hold values from 0.25 to 4
- wall_eigen: float32 [512], replicated, may hold values from 0.05 to 2
- basis_part: float32 [512, 512], replicated, may hold values from -0.125 to 0.125
- dual_part: float32 [512, 512], replicated, may hold values from -0.125 to 0.125
- bulk_shift: float32 [1], replicated, may hold values from 2.2 to 2.8
Outputs:
- new_field: float32 [4, 4, 512, 8192], P(None, 'gz', None, 'gx')
All inputs are finite; a program needn't handle non-finite values.
Results may differ from a plain program's by a relative error of at most 0.0001.
Values sent between devices are 32-bit elements; how exact they have to be, the bound alone decides.
No kernel may reach another device: no remote copies, remote signals or barrier semaphores. Data moves between devices by JAX's collectives and lax.ppermute only.
A program may use at most 64 MiB of HBM per device.

v0:
```python
import math

import jax
import jax.numpy as jnp
from jax import lax
from jax.sharding import PartitionSpec as P


def partner(array, axis, apart):
    return lax.ppermute(array, axis, [(i, i ^ 1 << apart) for i in range(lax.axis_size(axis))])


def phase_tables(length):
    counter = jnp.arange(length, dtype=jnp.int32)
    product = counter[:, None] * counter[None, :] % length
    angle = 2.0 * math.pi / length * product.astype(jnp.float32)
    return (jnp.cos(angle), jnp.sin(angle))


def along_last(values, table):
    return jnp.einsum("fzyj,jm->fzym", values, table, precision=lax.Precision.HIGHEST)


def crank_factor(diffusivity, eigen_rows, mode_index, total_cells):
    folded = jnp.minimum(mode_index, total_cells - mode_index).astype(jnp.float32)
    wavenumber = 2.0 * math.pi / total_cells * folded
    growth = diffusivity[:, None, None] * (
        eigen_rows[None, :, None] + wavenumber[None, None, :] ** 2
    )
    return (1.0 - growth) / (1.0 + growth)


def travel_phase(bulk_shift, mode_index, total_cells):
    signed = jnp.where(2 * mode_index >= total_cells, mode_index - total_cells, mode_index).astype(
        jnp.float32
    )
    travel = 2.0 * math.pi / total_cells * signed * bulk_shift[0]
    return (jnp.cos(travel), jnp.sin(travel))


def turn_modes(spec_real, spec_imag, damping, cos_travel, sin_travel):
    new_real = damping * (spec_real * cos_travel + spec_imag * sin_travel)
    new_imag = damping * (spec_imag * cos_travel - spec_real * sin_travel)
    return (new_real, new_imag)


def per_device(
    field,
    drop_cell,
    drop_plane,
    drop_rate,
    diffusivity,
    wall_eigen,
    basis_part,
    dual_part,
    bulk_shift,
):
    field_count, plane_count, row_count, slab_width = field.shape
    gx_count = lax.axis_size("gx")
    gz_count = lax.axis_size("gz")
    total_cells = slab_width * gx_count
    plane_cells = row_count * slab_width
    flat_cell = drop_plane * plane_cells + drop_cell
    partial_value = jnp.stack(
        [
            jax.ops.segment_sum(
                drop_rate[component], flat_cell, num_segments=plane_count * gz_count * plane_cells
            )
            for component in range(2)
        ]
    )
    partial_value = partial_value.reshape(2, plane_count * gz_count, row_count, slab_width)
    source = lax.psum_scatter(partial_value, "gz", scatter_dimension=1, tiled=True)
    right_side = jnp.concatenate([field[:2], field[2:] + source], axis=0)
    identity = jnp.eye(row_count, dtype=jnp.float32)
    projected = jnp.einsum(
        "ay,fzyx->fzax", identity + dual_part, right_side, precision=lax.Precision.HIGHEST
    )
    position = lax.axis_index("gx")
    bit_total = gx_count.bit_length() - 1
    real_part = projected
    imag_part = jnp.zeros_like(projected)
    for section_bit in range(bit_total - 1, -1, -1):
        half_span = 1 << section_bit
        other_real, other_imag = partner((real_part, imag_part), "gx", section_bit)
        upper_side = position // half_span % 2 == 1
        angle = -math.pi / half_span * (position % half_span).astype(jnp.float32)
        cosine = jnp.cos(angle)
        sine = jnp.sin(angle)
        diff_real = other_real - real_part
        diff_imag = other_imag - imag_part
        new_real = jnp.where(
            upper_side, diff_real * cosine - diff_imag * sine, real_part + other_real
        )
        new_imag = jnp.where(
            upper_side, diff_real * sine + diff_imag * cosine, imag_part + other_imag
        )
        real_part, imag_part = (new_real, new_imag)
    reversed_index = jnp.zeros((), jnp.int32)
    for bit_number in range(bit_total):
        reversed_index = reversed_index + position // (1 << bit_number) % 2 * (
            1 << bit_total - 1 - bit_number
        )
    columns = jnp.arange(slab_width, dtype=jnp.int32)
    twist = (
        2.0 * math.pi / total_cells * (reversed_index * columns % total_cells).astype(jnp.float32)
    )
    cos_twist = jnp.cos(twist)
    sin_twist = jnp.sin(twist)
    shifted_real = real_part * cos_twist + imag_part * sin_twist
    shifted_imag = imag_part * cos_twist - real_part * sin_twist
    cos_table, sin_table = phase_tables(slab_width)
    spec_real = along_last(shifted_real, cos_table) + along_last(shifted_imag, sin_table)
    spec_imag = along_last(shifted_imag, cos_table) - along_last(shifted_real, sin_table)
    mode_index = reversed_index + gx_count * columns
    damping = crank_factor(diffusivity, wall_eigen, mode_index, total_cells)[:, None]
    cos_travel, sin_travel = travel_phase(bulk_shift, mode_index, total_cells)
    spec_real, spec_imag = turn_modes(spec_real, spec_imag, damping, cos_travel, sin_travel)
    back_real = along_last(spec_real, cos_table) - along_last(spec_imag, sin_table)
    back_imag = along_last(spec_imag, cos_table) + along_last(spec_real, sin_table)
    real_part = back_real * cos_twist - back_imag * sin_twist
    imag_part = back_real * sin_twist + back_imag * cos_twist
    for section_bit in range(bit_total):
        half_span = 1 << section_bit
        other_real, other_imag = partner((real_part, imag_part), "gx", section_bit)
        upper_side = position // half_span % 2 == 1
        angle = math.pi / half_span * (position % half_span).astype(jnp.float32)
        cosine = jnp.cos(angle)
        sine = jnp.sin(angle)
        mine_real = real_part * cosine - imag_part * sine
        mine_imag = real_part * sine + imag_part * cosine
        turned_real = other_real * cosine - other_imag * sine
        turned_imag = other_real * sine + other_imag * cosine
        new_real = jnp.where(upper_side, other_real - mine_real, real_part + turned_real)
        new_imag = jnp.where(upper_side, other_imag - mine_imag, imag_part + turned_imag)
        real_part, imag_part = (new_real, new_imag)
    filtered = real_part / total_cells
    return jnp.einsum(
        "ya,fzax->fzyx", identity + basis_part, filtered, precision=lax.Precision.HIGHEST
    )


def solution(mesh):
    in_specs = (
        P(None, "gz", None, "gx"),
        P(("gx", "gz")),
        P(("gx", "gz")),
        P(None, ("gx", "gz")),
        P(),
        P(),
        P(),
        P(),
        P(),
    )
    out_specs = P(None, "gz", None, "gx")
    return jax.shard_map(
        per_device, mesh=mesh, in_specs=in_specs, out_specs=out_specs, check_vma=False
    )
```

profile of v0, /device:TPU:1, one launch (start us, length us, event | category | flops | bytes accessed | tf_op | source)
XLA Modules:
  0.0 796.0 jit_solution(8399179134907437658)
XLA Ops:
  8.1 22.2 %scatter_custom_fusion = f32[262144]{0:T(1024)S(1)} fusion(s32[4096]{0:T(1024)S(1)} %multiply_add_fusion.3, f32[4096]{0:T(1024)S(1)} %bitcast.72, f32[]{:T(128)} %constant.263.clone.1), kind=kCustom, calls=%fused_computation.72 | custom fusion | flops 4096 | bytes 1048580 | tf_op jit(solution)/shard_map/scatter-add | solution.py:66
  30.7 22.2 %scatter_custom_fusion.1 = f32[262144]{0:T(1024)S(1)} fusion(s32[4096]{0:T(1024)S(1)} %multiply_add_fusion.3, f32[4096]{0:T(1024)S(1)} %bitcast.71, f32[]{:T(128)} %constant.263.clone.1), kind=kCustom, calls=%fused_computation.70 | custom fusion | flops 4096 | bytes 1048580 | tf_op jit(solution)/shard_map/scatter-add | solution.py:66
  55.9 3.7 collective-permute-start.1
  60.1 30.9 %reduce-scatter.2.cloned.1.call-done = f32[2,1,512,128]{2,3,0,1:T(8,128)} async-done(((f32[2,4,512,128]{2,3,0,1:T(8,128)}), f32[2,1,512,128]{2,3,0,1:T(8,128)}) %reduce-scatter.2.cloned.1.call-update) | async-done | bytes 524304 | tf_op jit(solution)/shard_map/reduce_scatter | solution.py:73
  94.0 2.8 collective-permute-start
  97.0 22.8 %collective-permute-done = f32[4,1,512,128]{2,3,0,1:T(8,128)} collective-permute-done((f32[4,1,512,128]{2,3,0,1:T(8,128)S(1)}, f32[4,1,512,128]{2,3,0,1:T(8,128)}, u32[]{:S(2)}, u32[]{:S(2)}) %collective-permute-start) | collective-permute-done | bytes 1048608 | tf_op jit(solution)/shard_map/ppermute | solution.py:10
  123.5 21.6 %collective-permute-done.2 = f32[4,1,512,128]{2,3,0,1:T(8,128)S(1)} collective-permute-done((f32[4,1,512,128]{2,3,0,1:T(8,128)S(1)}, f32[4,1,512,128]{2,3,0,1:T(8,128)S(1)}, u32[]{:S(2)}, u32[]{:S(2)}) %collective-permute-start.2) | collective-permute-done | bytes 1048608 | tf_op jit(solution)/shard_map/ppermute | solution.py:10
  146.0 21.6 %collective-permute-done.3 = f32[4,1,512,128]{2,3,0,1:T(8,128)} collective-permute-done((f32[4,1,512,128]{2,3,0,1:T(8,128)S(1)}, f32[4,1,512,128]{2,3,0,1:T(8,128)}, u32[]{:S(2)}, u32[]{:S(2)}) %collective-permute-start.3) | collective-permute-done | bytes 1048608 | tf_op jit(solution)/shard_map/ppermute | solution.py:10
  170.0 5.5 collective-permute-start.4
  175.8 30.3 %collective-permute-done.4 = f32[4,1,512,128]{2,3,0,1:T(8,128)S(1)} collective-permute-done((f32[4,1,512,128]{2,3,0,1:T(8,128)S(1)}, f32[4,1,512,128]{2,3,0,1:T(8,128)S(1)}, u32[]{:S(2)}, u32[]{:S(2)}) %collective-permute-start.4) | collective-permute-done | bytes 1048608 | tf_op jit(solution)/shard_map/ppermute | solution.py:10
  207.1 45.0 %collective-permute-done.5 = f32[4,1,512,128]{2,3,0,1:T(8,128)} collective-permute-done((f32[4,1,512,128]{2,3,0,1:T(8,128)S(1)}, f32[4,1,512,128]{2,3,0,1:T(8,128)}, u32[]{:S(2)}, u32[]{:S(2)}) %collective-permute-start.5) | collective-permute-done | bytes 1048608 | tf_op jit(solution)/shard_map/ppermute | solution.py:10
  252.1 3.0 add_select_fusion.15
  255.1 17.1 %collective-permute-start.6 = (f32[4,1,512,128]{2,3,0,1:T(8,128)S(1)}, f32[4,1,512,128]{2,3,0,1:T(8,128)S(1)}, u32[]{:S(2)}, u32[]{:S(2)}) collective-permute-start(f32[4,1,512,128]{2,3,0,1:T(8,128)S(1)} %get-tuple-element.21), channel_id=1, source_target_pairs={{0,16},{4,20},{8,24},{12,28},{16,0},{20,4},{24,8},{28,12},{32,48},... | collective-permute-start | bytes 3145736 | tf_op jit(solution)/shard_map/ppermute | solution.py:10
  272.9 66.6 %collective-permute-done.6 = f32[4,1,512,128]{2,3,0,1:T(8,128)S(1)} collective-permute-done((f32[4,1,512,128]{2,3,0,1:T(8,128)S(1)}, f32[4,1,512,128]{2,3,0,1:T(8,128)S(1)}, u32[]{:S(2)}, u32[]{:S(2)}) %collective-permute-start.6) | collective-permute-done | bytes 1048608 | tf_op jit(solution)/shard_map/ppermute | solution.py:10
  340.5 21.6 %collective-permute-done.7 = f32[4,1,512,128]{2,3,0,1:T(8,128)} collective-permute-done((f32[4,1,512,128]{2,3,0,1:T(8,128)}, f32[4,1,512,128]{2,3,0,1:T(8,128)}, u32[]{:S(2)}, u32[]{:S(2)}) %collective-permute-start.7) | collective-permute-done | bytes 1048608 | tf_op jit(solution)/shard_map/ppermute | solution.py:10
  366.2 22.6 %collective-permute-done.8 = f32[4,1,512,128]{2,3,0,1:T(8,128)S(1)} collective-permute-done((f32[4,1,512,128]{2,3,0,1:T(8,128)S(1)}, f32[4,1,512,128]{2,3,0,1:T(8,128)S(1)}, u32[]{:S(2)}, u32[]{:S(2)}) %collective-permute-start.8) | collective-permute-done | bytes 1048608 | tf_op jit(solution)/shard_map/ppermute | solution.py:10
  389.8 21.6 %collective-permute-done.9 = f32[4,1,512,128]{2,3,0,1:T(8,128)} collective-permute-done((f32[4,1,512,128]{2,3,0,1:T(8,128)S(1)}, f32[4,1,512,128]{2,3,0,1:T(8,128)}, u32[]{:S(2)}, u32[]{:S(2)}) %collective-permute-start.9) | collective-permute-done | bytes 1048608 | tf_op jit(solution)/shard_map/ppermute | solution.py:10
  442.8 22.7 %collective-permute-done.14 = f32[4,1,512,128]{2,3,0,1:T(8,128)S(1)} collective-permute-done((f32[4,1,512,128]{2,3,0,1:T(8,128)S(1)}, f32[4,1,512,128]{2,3,0,1:T(8,128)S(1)}, u32[]{:S(2)}, u32[]{:S(2)}) %collective-permute-start.14) | collective-permute-done | bytes 1048608 | tf_op jit(solution)/shard_map/ppermute | solution.py:10
  466.5 21.6 %collective-permute-done.15 = f32[4,1,512,128]{2,3,0,1:T(8,128)} collective-permute-done((f32[4,1,512,128]{2,3,0,1:T(8,128)S(1)}, f32[4,1,512,128]{2,3,0,1:T(8,128)}, u32[]{:S(2)}, u32[]{:S(2)}) %collective-permute-start.15) | collective-permute-done | bytes 1048608 | tf_op jit(solution)/shard_map/ppermute | solution.py:10
  488.1 3.1 add_select_fusion.6
  493.8 68.3 %collective-permute-done.16 = f32[4,1,512,128]{2,3,0,1:T(8,128)S(1)} collective-permute-done((f32[4,1,512,128]{2,3,0,1:T(8,128)}, f32[4,1,512,128]{2,3,0,1:T(8,128)S(1)}, u32[]{:S(2)}, u32[]{:S(2)}) %collective-permute-start.16) | collective-permute-done | bytes 1048608 | tf_op jit(solution)/shard_map/ppermute | solution.py:10
  563.1 21.6 %collective-permute-done.17 = f32[4,1,512,128]{2,3,0,1:T(8,128)} collective-permute-done((f32[4,1,512,128]{2,3,0,1:T(8,128)S(1)}, f32[4,1,512,128]{2,3,0,1:T(8,128)}, u32[]{:S(2)}, u32[]{:S(2)}) %collective-permute-start.17) | collective-permute-done | bytes 1048608 | tf_op jit(solution)/shard_map/ppermute | solution.py:10
  588.3 4.3 collective-permute-start.19
  592.8 66.7 %collective-permute-done.18 = f32[4,1,512,128]{2,3,0,1:T(8,128)S(1)} collective-permute-done((f32[4,1,512,128]{2,3,0,1:T(8,128)S(1)}, f32[4,1,512,128]{2,3,0,1:T(8,128)S(1)}, u32[]{:S(2)}, u32[]{:S(2)}) %collective-permute-start.18) | collective-permute-done | bytes 1048608 | tf_op jit(solution)/shard_map/ppermute | solution.py:10
  660.4 21.6 %collective-permute-done.19 = f32[4,1,512,128]{2,3,0,1:T(8,128)} collective-permute-done((f32[4,1,512,128]{2,3,0,1:T(8,128)S(1)}, f32[4,1,512,128]{2,3,0,1:T(8,128)}, u32[]{:S(2)}, u32[]{:S(2)}) %collective-permute-start.19) | collective-permute-done | bytes 1048608 | tf_op jit(solution)/shard_map/ppermute | solution.py:10
  682.0 3.1 add_select_fusion.2
  687.0 22.5 %collective-permute-done.20 = f32[4,1,512,128]{2,3,0,1:T(8,128)S(1)} collective-permute-done((f32[4,1,512,128]{2,3,0,1:T(8,128)}, f32[4,1,512,128]{2,3,0,1:T(8,128)S(1)}, u32[]{:S(2)}, u32[]{:S(2)}) %collective-permute-start.20) | collective-permute-done | bytes 1048608 | tf_op jit(solution)/shard_map/ppermute | solution.py:10
  710.5 21.6 %collective-permute-done.21 = f32[4,1,512,128]{2,3,0,1:T(8,128)} collective-permute-done((f32[4,1,512,128]{2,3,0,1:T(8,128)S(1)}, f32[4,1,512,128]{2,3,0,1:T(8,128)}, u32[]{:S(2)}, u32[]{:S(2)}) %collective-permute-start.21) | collective-permute-done | bytes 1048608 | tf_op jit(solution)/shard_map/ppermute | solution.py:10
  734.6 4.0 collective-permute-start.22
  738.9 21.9 %collective-permute-done.22 = f32[4,1,512,128]{2,3,0,1:T(8,128)S(1)} collective-permute-done((f32[4,1,512,128]{2,3,0,1:T(8,128)S(1)}, f32[4,1,512,128]{2,3,0,1:T(8,128)S(1)}, u32[]{:S(2)}, u32[]{:S(2)}) %collective-permute-start.22) | collective-permute-done | bytes 1048608 | tf_op jit(solution)/shard_map/ppermute | solution.py:10
  760.8 22.6 %collective-permute-done.23 = f32[4,1,512,128]{2,3,0,1:T(8,128)} collective-permute-done((f32[4,1,512,128]{2,3,0,1:T(8,128)S(1)}, f32[4,1,512,128]{2,3,0,1:T(8,128)}, u32[]{:S(2)}, u32[]{:S(2)}) %collective-permute-start.23) | collective-permute-done | bytes 1048608 | tf_op jit(solution)/shard_map/ppermute | solution.py:10
  783.3 4.1 convolution_bitcast_fusion
  (87 shorter events, 68.8 us)
Async XLA Ops:
  6.5 84.5 %reduce-scatter.2.cloned.1.call-start = ((), (), s32[]{:S(2)}) async-start(), calls=%async_computation.1 | async-start | bytes 2621440 | tf_op jit(solution)/shard_map/reduce_scatter | solution.py:73
  54.8 4.9 copy-start.4
  55.9 41.1 %collective-permute-start.1 = (f32[4,1,512,128]{2,3,0,1:T(8,128)}, f32[4,1,512,128]{2,3,0,1:T(8,128)}, u32[]{:S(2)}, u32[]{:S(2)}) collective-permute-start(f32[4,1,512,128]{2,3,0,1:T(8,128)} %broadcast_in_dim.5), channel_id=1, source_target_pairs={{0,128},{4,132},{8,136},{12,140},{16,144},{20,148},{24,152},{28,15... | collective-permute-start | bytes 3145736 | tf_op jit(solution)/shard_map/ppermute | solution.py:10
  59.7 32.4 %copy-start.3 = (f32[512,512]{1,0:T(8,128)S(1)}, f32[512,512]{1,0:T(8,128)}, u32[]{:S(2)}) copy-start(f32[512,512]{1,0:T(8,128)} %param.16) | copy-start | bytes 3145732
  94.0 25.8 %collective-permute-start = (f32[4,1,512,128]{2,3,0,1:T(8,128)S(1)}, f32[4,1,512,128]{2,3,0,1:T(8,128)}, u32[]{:S(2)}, u32[]{:S(2)}) collective-permute-start(f32[4,1,512,128]{2,3,0,1:T(8,128)S(1)} %convolution_bitcast_fusion.1), channel_id=1, source_target_pairs={{0,128},{4,132},{8,136},{12,140},{16,144},{20,148},{24,152},{28,15... | collective-permute-start | bytes 3145736 | tf_op jit(solution)/shard_map/ppermute | solution.py:10
  121.8 23.3 %copy-start.1 = (f32[4,1,512,128]{2,3,0,1:T(8,128)}, f32[4,1,512,128]{2,3,0,1:T(8,128)S(1)}, u32[]{:S(2)}) copy-start(f32[4,1,512,128]{2,3,0,1:T(8,128)S(1)} %get-tuple-element.26) | copy-start | bytes 3145732
  121.8 23.3 %collective-permute-start.2 = (f32[4,1,512,128]{2,3,0,1:T(8,128)S(1)}, f32[4,1,512,128]{2,3,0,1:T(8,128)S(1)}, u32[]{:S(2)}, u32[]{:S(2)}) collective-permute-start(f32[4,1,512,128]{2,3,0,1:T(8,128)S(1)} %get-tuple-element.25), channel_id=1, source_target_pairs={{0,64},{4,68},{8,72},{12,76},{16,80},{20,84},{24,88},{28,92},{32,9... | collective-permute-start | bytes 3145736 | tf_op jit(solution)/shard_map/ppermute | solution.py:10
  123.1 44.6 %collective-permute-start.3 = (f32[4,1,512,128]{2,3,0,1:T(8,128)S(1)}, f32[4,1,512,128]{2,3,0,1:T(8,128)}, u32[]{:S(2)}, u32[]{:S(2)}) collective-permute-start(f32[4,1,512,128]{2,3,0,1:T(8,128)S(1)} %get-tuple-element.26), channel_id=1, source_target_pairs={{0,64},{4,68},{8,72},{12,76},{16,80},{20,84},{24,88},{28,92},{32,9... | collective-permute-start | bytes 3145736 | tf_op jit(solution)/shard_map/ppermute | solution.py:10
  170.0 36.1 %collective-permute-start.4 = (f32[4,1,512,128]{2,3,0,1:T(8,128)S(1)}, f32[4,1,512,128]{2,3,0,1:T(8,128)S(1)}, u32[]{:S(2)}, u32[]{:S(2)}) collective-permute-start(f32[4,1,512,128]{2,3,0,1:T(8,128)S(1)} %get-tuple-element.23), channel_id=1, source_target_pairs={{0,32},{4,36},{8,40},{12,44},{16,48},{20,52},{24,56},{28,60},{32,0... | collective-permute-start | bytes 3145736 | tf_op jit(solution)/shard_map/ppermute | solution.py:10
  175.5 76.6 %collective-permute-start.5 = (f32[4,1,512,128]{2,3,0,1:T(8,128)S(1)}, f32[4,1,512,128]{2,3,0,1:T(8,128)}, u32[]{:S(2)}, u32[]{:S(2)}) collective-permute-start(f32[4,1,512,128]{2,3,0,1:T(8,128)S(1)} %get-tuple-element.24), channel_id=1, source_target_pairs={{0,32},{4,36},{8,40},{12,44},{16,48},{20,52},{24,56},{28,60},{32,0... | collective-permute-start | bytes 3145736 | tf_op jit(solution)/shard_map/ppermute | solution.py:10
  255.1 84.4 %collective-permute-start.6 = (f32[4,1,512,128]{2,3,0,1:T(8,128)S(1)}, f32[4,1,512,128]{2,3,0,1:T(8,128)S(1)}, u32[]{:S(2)}, u32[]{:S(2)}) collective-permute-start(f32[4,1,512,128]{2,3,0,1:T(8,128)S(1)} %get-tuple-element.21), channel_id=1, source_target_pairs={{0,16},{4,20},{8,24},{12,28},{16,0},{20,4},{24,8},{28,12},{32,48},... | collective-permute-start | bytes 3145736 | tf_op jit(solution)/shard_map/ppermute | solution.py:10
  272.2 89.9 %collective-permute-start.7 = (f32[4,1,512,128]{2,3,0,1:T(8,128)}, f32[4,1,512,128]{2,3,0,1:T(8,128)}, u32[]{:S(2)}, u32[]{:S(2)}) collective-permute-start(f32[4,1,512,128]{2,3,0,1:T(8,128)} %get-tuple-element.22), channel_id=1, source_target_pairs={{0,16},{4,20},{8,24},{12,28},{16,0},{20,4},{24,8},{28,12},{32,48},... | collective-permute-start | bytes 3145736 | tf_op jit(solution)/shard_map/ppermute | solution.py:10
  364.4 24.4 %copy-start = (f32[4,1,512,128]{2,3,0,1:T(8,128)}, f32[4,1,512,128]{2,3,0,1:T(8,128)S(1)}, u32[]{:S(2)}) copy-start(f32[4,1,512,128]{2,3,0,1:T(8,128)S(1)} %get-tuple-element.20) | copy-start | bytes 3145732
  364.4 24.3 %collective-permute-start.8 = (f32[4,1,512,128]{2,3,0,1:T(8,128)S(1)}, f32[4,1,512,128]{2,3,0,1:T(8,128)S(1)}, u32[]{:S(2)}, u32[]{:S(2)}) collective-permute-start(f32[4,1,512,128]{2,3,0,1:T(8,128)S(1)} %get-tuple-element.19), channel_id=1, source_target_pairs={{0,8},{4,12},{8,0},{12,4},{16,24},{20,28},{24,16},{28,20},{32,40},... | collective-permute-start | bytes 3145736 | tf_op jit(solution)/shard_map/ppermute | solution.py:10
  364.5 46.8 %collective-permute-start.9 = (f32[4,1,512,128]{2,3,0,1:T(8,128)S(1)}, f32[4,1,512,128]{2,3,0,1:T(8,128)}, u32[]{:S(2)}, u32[]{:S(2)}) collective-permute-start(f32[4,1,512,128]{2,3,0,1:T(8,128)S(1)} %get-tuple-element.20), channel_id=1, source_target_pairs={{0,8},{4,12},{8,0},{12,4},{16,24},{20,28},{24,16},{28,20},{32,40},... | collective-permute-start | bytes 3145736 | tf_op jit(solution)/shard_map/ppermute | solution.py:10
  366.2 50.1 %copy-start.13 = (f32[512]{0:T(512)S(1)}, f32[512]{0:T(512)}, u32[]{:S(2)}) copy-start(f32[512]{0:T(512)} %param.14) | copy-start | bytes 6148
  413.7 3.7 collective-permute-start.10
  415.2 3.9 collective-permute-start.11
  427.1 2.1 copy-start.14
  436.3 2.7 collective-permute-start.12
  436.8 3.8 collective-permute-start.13
  441.1 24.5 %collective-permute-start.14 = (f32[4,1,512,128]{2,3,0,1:T(8,128)S(1)}, f32[4,1,512,128]{2,3,0,1:T(8,128)S(1)}, u32[]{:S(2)}, u32[]{:S(2)}) collective-permute-start(f32[4,1,512,128]{2,3,0,1:T(8,128)S(1)} %get-tuple-element.14), channel_id=1, source_target_pairs={{0,8},{4,12},{8,0},{12,4},{16,24},{20,28},{24,16},{28,20},{32,40},... | collective-permute-start | bytes 3145736 | tf_op jit(solution)/shard_map/ppermute | solution.py:10
  441.2 46.9 %collective-permute-start.15 = (f32[4,1,512,128]{2,3,0,1:T(8,128)S(1)}, f32[4,1,512,128]{2,3,0,1:T(8,128)}, u32[]{:S(2)}, u32[]{:S(2)}) collective-permute-start(f32[4,1,512,128]{2,3,0,1:T(8,128)S(1)} %get-tuple-element.13), channel_id=1, source_target_pairs={{0,8},{4,12},{8,0},{12,4},{16,24},{20,28},{24,16},{28,20},{32,40},... | collective-permute-start | bytes 3145736 | tf_op jit(solution)/shard_map/ppermute | solution.py:10
  491.3 70.9 %collective-permute-start.16 = (f32[4,1,512,128]{2,3,0,1:T(8,128)}, f32[4,1,512,128]{2,3,0,1:T(8,128)S(1)}, u32[]{:S(2)}, u32[]{:S(2)}) collective-permute-start(f32[4,1,512,128]{2,3,0,1:T(8,128)} %get-tuple-element.12), channel_id=1, source_target_pairs={{0,16},{4,20},{8,24},{12,28},{16,0},{20,4},{24,8},{28,12},{32,48},... | collective-permute-start | bytes 3145736 | tf_op jit(solution)/shard_map/ppermute | solution.py:10
  491.3 93.4 %collective-permute-start.17 = (f32[4,1,512,128]{2,3,0,1:T(8,128)S(1)}, f32[4,1,512,128]{2,3,0,1:T(8,128)}, u32[]{:S(2)}, u32[]{:S(2)}) collective-permute-start(f32[4,1,512,128]{2,3,0,1:T(8,128)S(1)} %get-tuple-element.11), channel_id=1, source_target_pairs={{0,16},{4,20},{8,24},{12,28},{16,0},{20,4},{24,8},{28,12},{32,48},... | collective-permute-start | bytes 3145736 | tf_op jit(solution)/shard_map/ppermute | solution.py:10
  587.2 72.3 %collective-permute-start.18 = (f32[4,1,512,128]{2,3,0,1:T(8,128)S(1)}, f32[4,1,512,128]{2,3,0,1:T(8,128)S(1)}, u32[]{:S(2)}, u32[]{:S(2)}) collective-permute-start(f32[4,1,512,128]{2,3,0,1:T(8,128)S(1)} %get-tuple-element.10), channel_id=1, source_target_pairs={{0,32},{4,36},{8,40},{12,44},{16,48},{20,52},{24,56},{28,60},{32,0... | collective-permute-start | bytes 3145736 | tf_op jit(solution)/shard_map/ppermute | solution.py:10
  588.3 93.7 %collective-permute-start.19 = (f32[4,1,512,128]{2,3,0,1:T(8,128)S(1)}, f32[4,1,512,128]{2,3,0,1:T(8,128)}, u32[]{:S(2)}, u32[]{:S(2)}) collective-permute-start(f32[4,1,512,128]{2,3,0,1:T(8,128)S(1)} %get-tuple-element.9), channel_id=1, source_target_pairs={{0,32},{4,36},{8,40},{12,44},{16,48},{20,52},{24,56},{28,60},{32,0... | collective-permute-start | bytes 3145736 | tf_op jit(solution)/shard_map/ppermute | solution.py:10
  685.2 24.4 %collective-permute-start.20 = (f32[4,1,512,128]{2,3,0,1:T(8,128)}, f32[4,1,512,128]{2,3,0,1:T(8,128)S(1)}, u32[]{:S(2)}, u32[]{:S(2)}) collective-permute-start(f32[4,1,512,128]{2,3,0,1:T(8,128)} %get-tuple-element.8), channel_id=1, source_target_pairs={{0,64},{4,68},{8,72},{12,76},{16,80},{20,84},{24,88},{28,92},{32,9... | collective-permute-start | bytes 3145736 | tf_op jit(solution)/shard_map/ppermute | solution.py:10
  686.2 45.9 %collective-permute-start.21 = (f32[4,1,512,128]{2,3,0,1:T(8,128)S(1)}, f32[4,1,512,128]{2,3,0,1:T(8,128)}, u32[]{:S(2)}, u32[]{:S(2)}) collective-permute-start(f32[4,1,512,128]{2,3,0,1:T(8,128)S(1)} %get-tuple-element.7), channel_id=1, source_target_pairs={{0,64},{4,68},{8,72},{12,76},{16,80},{20,84},{24,88},{28,92},{32,9... | collective-permute-start | bytes 3145736 | tf_op jit(solution)/shard_map/ppermute | solution.py:10
  734.6 26.2 %copy-start.2 = (f32[4,1,512,128]{2,3,0,1:T(8,128)}, f32[4,1,512,128]{2,3,0,1:T(8,128)S(1)}, u32[]{:S(2)}) copy-start(f32[4,1,512,128]{2,3,0,1:T(8,128)S(1)} %get-tuple-element.6) | copy-start | bytes 3145732
  734.6 26.2 %collective-permute-start.22 = (f32[4,1,512,128]{2,3,0,1:T(8,128)S(1)}, f32[4,1,512,128]{2,3,0,1:T(8,128)S(1)}, u32[]{:S(2)}, u32[]{:S(2)}) collective-permute-start(f32[4,1,512,128]{2,3,0,1:T(8,128)S(1)} %get-tuple-element.6), channel_id=1, source_target_pairs={{0,128},{4,132},{8,136},{12,140},{16,144},{20,148},{24,152},{28,15... | collective-permute-start | bytes 3145736 | tf_op jit(solution)/shard_map/ppermute | solution.py:10
  738.6 44.7 %collective-permute-start.23 = (f32[4,1,512,128]{2,3,0,1:T(8,128)S(1)}, f32[4,1,512,128]{2,3,0,1:T(8,128)}, u32[]{:S(2)}, u32[]{:S(2)}) collective-permute-start(f32[4,1,512,128]{2,3,0,1:T(8,128)S(1)} %get-tuple-element.5), channel_id=1, source_target_pairs={{0,128},{4,132},{8,136},{12,140},{16,144},{20,148},{24,152},{28,15... | collective-permute-start | bytes 3145736 | tf_op jit(solution)/shard_map/ppermute | solution.py:10
  (8 other events, 7.8 us)
Sparse Core Ops, SparseCore 0:
  54.9 36.0 reduce-scatter.1
where the time goes:
time: 805 us; the launch traced here: 796 us
  waiting for transfers between devices  622 us (77%)
  other arithmetic  73.6 us (9%)
  starting transfers between devices  50.3 us (6%)
  matrix products  21.3 us (3%)
  between operations  16.4 us (2%)
  local copies, waits for them, and re-layouts  12.3 us (2%)
    ppermute x24, waiting for transfers between devices, partner(): lax.ppermute(array, axis, [(i, i ^ 1 << apart) for i in range(lax.axis_si...  591 us
    ppermute x24, starting transfers between devices, partner(): lax.ppermute(array, axis, [(i, i ^ 1 << apart) for i in range(lax.axis_si...  50.3 us
    scatter-add x2, other arithmetic, per_device(): jax.ops.segment_sum(drop_rate[component], flat_cell, num_segments=plane_c...  44.3 us
    reduce_scatter x1, waiting for transfers between devices, per_device(): lax.psum_scatter(partial_value, 'gz', scatter_dimension=1, tiled=True)  30.9 us
  transfers between devices with their start and end apart: 25, of which 24 were waited for; matrix products, arithmetic and copies ran while one was open for 1% of the time, Pallas kernels for 0%

commit v1 on v0

v1 whole, which is shorter than its diff:
```python
import math

import jax
import jax.numpy as jnp
from jax import lax
from jax.sharding import PartitionSpec as P

HI = lax.Precision.HIGHEST


def phase(numer, length):
    angle = 2.0 * math.pi / length * (numer % length).astype(jnp.float32)
    return jnp.cos(angle), jnp.sin(angle)


def per_device(
    field,
    drop_cell,
    drop_plane,
    drop_rate,
    diffusivity,
    wall_eigen,
    basis_part,
    dual_part,
    bulk_shift,
):
    field_count, plane_count, row_count, slab_width = field.shape
    gx_count = lax.axis_size("gx")
    gz_count = lax.axis_size("gz")
    total_cells = slab_width * gx_count
    plane_cells = row_count * slab_width
    rows_here = row_count // gx_count

    flat_cell = drop_plane * plane_cells + drop_cell
    partial_value = jnp.stack(
        [
            jax.ops.segment_sum(
                drop_rate[component], flat_cell, num_segments=plane_count * gz_count * plane_cells
            )
            for component in range(2)
        ]
    )
    partial_value = partial_value.reshape(2, plane_count * gz_count, row_count, slab_width)
    source = lax.psum_scatter(partial_value, "gz", scatter_dimension=1, tiled=True)
    right_side = jnp.concatenate([field[:2], field[2:] + source], axis=0)[:, 0]
    identity = jnp.eye(row_count, dtype=jnp.float32)
    projected = jnp.einsum("ay,fyx->fax", identity + dual_part, right_side, precision=HI)

    spread = lax.all_to_all(projected, "gx", 1, 1, tiled=True)
    spread = spread.reshape(field_count, gx_count, rows_here, slab_width)

    d_index = jnp.arange(gx_count, dtype=jnp.int32)
    j_index = jnp.arange(slab_width, dtype=jnp.int32)
    c64, s64 = phase(d_index[:, None] * d_index[None, :], gx_count)
    ct, st = phase(d_index[:, None] * j_index[None, :], total_cells)
    c128, s128 = phase(j_index[:, None] * j_index[None, :], slab_width)

    a_real = jnp.einsum("kd,fdaj->fkaj", c64, spread, precision=HI)
    a_imag = -jnp.einsum("kd,fdaj->fkaj", s64, spread, precision=HI)
    ct4 = ct[None, :, None, :]
    st4 = st[None, :, None, :]
    b_real = a_real * ct4 + a_imag * st4
    b_imag = a_imag * ct4 - a_real * st4
    joined = jnp.concatenate([b_real, b_imag], axis=-1)
    forward_table = jnp.concatenate(
        [jnp.concatenate([c128, -s128], axis=1), jnp.concatenate([s128, c128], axis=1)], axis=0
    )
    spec = jnp.einsum("fkaj,jm->fkam", joined, forward_table, precision=HI)
    spec_real = spec[..., :slab_width]
    spec_imag = spec[..., slab_width:]

    mode_index = d_index[:, None] + gx_count * j_index[None, :]
    folded = jnp.minimum(mode_index, total_cells - mode_index).astype(jnp.float32)
    wavenumber = 2.0 * math.pi / total_cells * folded
    position = lax.axis_index("gx")
    eigen_here = lax.dynamic_slice_in_dim(wall_eigen, position * rows_here, rows_here)
    growth = diffusivity[:, None, None, None] * (
        eigen_here[None, None, :, None] + (wavenumber**2)[None, :, None, :]
    )
    damping = (1.0 - growth) / (1.0 + growth)
    signed = jnp.where(2 * mode_index >= total_cells, mode_index - total_cells, mode_index).astype(
        jnp.float32
    )
    travel = 2.0 * math.pi / total_cells * signed * bulk_shift[0]
    cos_travel = jnp.cos(travel)[None, :, None, :]
    sin_travel = jnp.sin(travel)[None, :, None, :]
    factor_real = damping * cos_travel
    factor_imag = -damping * sin_travel
    turned_real = spec_real * factor_real - spec_imag * factor_imag
    turned_imag = spec_real * factor_imag + spec_imag * factor_real

    joined = jnp.concatenate([turned_real, turned_imag], axis=-1)
    inverse_table = jnp.concatenate(
        [jnp.concatenate([c128, s128], axis=1), jnp.concatenate([-s128, c128], axis=1)], axis=0
    )
    back = jnp.einsum("fkam,mj->fkaj", joined, inverse_table, precision=HI)
    back_real = back[..., :slab_width]
    back_imag = back[..., slab_width:]
    e_real = back_real * ct4 - back_imag * st4
    e_imag = back_real * st4 + back_imag * ct4
    filtered = (
        jnp.einsum("dk,fkaj->fdaj", c64, e_real, precision=HI)
        - jnp.einsum("dk,fkaj->fdaj", s64, e_imag, precision=HI)
    ) / total_cells

    filtered = filtered.reshape(field_count, row_count, slab_width)
    gathered = lax.all_to_all(filtered, "gx", 1, 1, tiled=True)
    result = jnp.einsum("ya,fax->fyx", identity + basis_part, gathered, precision=HI)
    return result[:, None]


def solution(mesh):
    in_specs = (
        P(None, "gz", None, "gx"),
        P(("gx", "gz")),
        P(("gx", "gz")),
        P(None, ("gx", "gz")),
        P(),
        P(),
        P(),
        P(),
        P(),
    )
    out_specs = P(None, "gz", None, "gx")
    return jax.shard_map(
        per_device, mesh=mesh, in_specs=in_specs, out_specs=out_specs, check_vma=False
    )
```

time: 805 us -> 194 us (0.24); the launches traced: 796 us -> 194 us
  waiting for transfers between devices: 622 us -> 60.6 us
  starting transfers between devices: 50.3 us -> 10.8 us
  blocking collectives: 0 us -> 34.5 us
  other arithmetic: 73.6 us -> 49.6 us
    ppermute x24 -> x0, waiting for transfers between devices: 591 us -> none  [partner(): lax.ppermute(array, axis, [(i, i ^ 1 << apart) for i in range(lax.axis_si...]
    ppermute x24 -> x0, starting transfers between devices: 50.3 us -> none  [partner(): lax.ppermute(array, axis, [(i, i ^ 1 << apart) for i in range(lax.axis_si...]
    all_to_all x0 -> x1, blocking collectives: none -> 34.5 us  [per_device(): gathered = lax.all_to_all(filtered, 'gx', 1, 1, tiled=True)]
    all_to_all x0 -> x1, waiting for transfers between devices: none -> 26 us  [per_device(): spread = lax.all_to_all(projected, 'gx', 1, 1, tiled=True)]
    select_n x11 -> x0, other arithmetic: 25.6 us -> none  [the longest x6 13.9 us: per_device(): jnp.where(upper_side, diff_real * cosine - diff_imag * sine, real_part +...]
    all_to_all x0 -> x1, starting transfers between devices: none -> 10.8 us  [per_device(): spread = lax.all_to_all(projected, 'gx', 1, 1, tiled=True)]
    dot_general x10 -> x8, matrix products: 21.3 us -> 16.2 us  [the longest x1 3.48 us: per_device(): jnp.einsum('ya,fax->fyx', identity + basis_part, gathered, precision=HI)]
  transfers between devices with their start and end apart: 25 -> 2, of which waited for: 24 -> 2; matrix products, arithmetic and copies ran while one was open for 1% -> 1% of each run, Pallas kernels for 0% -> 0%
where the time goes in v1:
time: 194 us
  waiting for transfers between devices  60.6 us (31%)
  other arithmetic  49.6 us (26%)
  blocking collectives  34.5 us (18%)
  matrix products  16.2 us (8%)
  between operations  14.3 us (7%)
  starting transfers between devices  10.8 us (6%)
  local copies, waits for them, and re-layouts  7.93 us (4%)
    scatter-add x2, other arithmetic, per_device(): jax.ops.segment_sum(drop_rate[component], flat_cell, num_segments=plane_c...  44.3 us
    all_to_all x1, blocking collectives, per_device(): gathered = lax.all_to_all(filtered, 'gx', 1, 1, tiled=True)  34.5 us
    reduce_scatter x1, waiting for transfers between devices, per_device(): lax.psum_scatter(partial_value, 'gz', scatter_dimension=1, tiled=True)  34.5 us
    all_to_all x1, waiting for transfers between devices, per_device(): spread = lax.all_to_all(projected, 'gx', 1, 1, tiled=True)  26 us
    all_to_all x1, starting transfers between devices, per_device(): spread = lax.all_to_all(projected, 'gx', 1, 1, tiled=True)  10.8 us
  transfers between devices with their start and end apart: 2, of which 2 were waited for; matrix products, arithmetic and copies ran while one was open for 1% of the time, Pallas kernels for 0%

profile of v1, /device:TPU:1, one launch (start us, length us, event | category | flops | bytes accessed | tf_op | source)
XLA Modules:
  0.0 194.0 jit_solution(14143660567578855916)
XLA Ops:
  6.5 0.9 fusion.106
  7.4 0.7 multiply_add_fusion.3
  8.1 22.2 %scatter_custom_fusion.1 = f32[262144]{0:T(1024)S(1)} fusion(s32[4096]{0:T(1024)S(1)} %multiply_add_fusion.3, f32[4096]{0:T(1024)S(1)} %bitcast.64, f32[]{:T(128)} %constant.56.clone.1), kind=kCustom, calls=%fused_computation.53 | custom fusion | flops 4096 | bytes 1048580 | tf_op jit(solution)/shard_map/scatter-add | solution.py:37
  30.3 0.3 copy.34
  30.7 22.2 %scatter_custom_fusion = f32[262144]{0:T(1024)S(1)} fusion(s32[4096]{0:T(1024)S(1)} %multiply_add_fusion.3, f32[4096]{0:T(1024)S(1)} %bitcast.63, f32[]{:T(128)} %constant.56.clone.1), kind=kCustom, calls=%fused_computation.55 | custom fusion | flops 4096 | bytes 1048580 | tf_op jit(solution)/shard_map/scatter-add | solution.py:37
  52.8 0.3 copy.33
  53.2 1.6 pad_maximum_fusion
  54.8 1.2 copy-done.2
  56.1 0.2 copy.52
  56.3 0.2 copy.53
  56.5 34.5 %reduce-scatter.2.cloned.1.call-done = f32[2,1,512,128]{2,3,0,1:T(8,128)} async-done(((f32[2,4,512,128]{2,3,0,1:T(8,128)}), f32[2,1,512,128]{2,3,0,1:T(8,128)}) %reduce-scatter.2.cloned.1.call-update) | async-done | bytes 524304 | tf_op jit(solution)/shard_map/reduce_scatter | solution.py:44
  91.0 1.1 add.144
  92.2 1.9 convolution_bitcast_fusion.2
  94.0 1.3 copy.35
  95.4 10.8 %all-to-all-start = ((f32[4,512,128]{2,0,1:T(4,128)}), f32[4,512,128]{2,0,1:T(4,128)S(1)}, u32[]{:S(2)}, u32[]{:S(2)}) async-start(f32[4,512,128]{2,0,1:T(4,128)} %copy.35), calls=%async_computation.1 | async-start | bytes 2097152 | tf_op jit(solution)/shard_map/all_to_all | solution.py:49
  106.8 0.8 dynamic_slice.3
  107.6 0.3 fusion.77
  108.0 0.3 fusion.69
  108.5 26.0 %all-to-all-done = f32[4,512,128]{2,0,1:T(4,128)S(1)} async-done(((f32[4,512,128]{2,0,1:T(4,128)}), f32[4,512,128]{2,0,1:T(4,128)S(1)}, u32[]{:S(2)}, u32[]{:S(2)}) %all-to-all-start) | async-done | bytes 1048608 | tf_op jit(solution)/shard_map/all_to_all | solution.py:49
  134.6 1.3 convolution_bitcast_fusion.1
  135.9 1.5 multiply_add_fusion.2
  137.4 0.2 pad_maximum_fusion.1
  137.6 2.9 %fusion.2 = f32[4,64,8,256]{3,2,1,0:T(8,128)S(1)} fusion(f32[4,64,8,256]{3,1,2,0:T(8,128)S(1)} %pad_maximum_fusion.1, f32[128,128]{1,0:T(8,128)S(1)} %get-tuple-element.19, f32[128,128]{1,0:T(8,128)S(1)} %get-tuple-element.18, f32[128,128]{1,0:T(8,128)S(1)} %fusion.77), kind=kOutput, calls=%fused_computation.7 | convolution fusion | flops 1610809344 | bytes 4390912 | tf_op jit(solution)/shard_map/fkaj,jm->fkam/dot_general | solution.py:68
  140.6 0.6 multiply_subtract_fusion.1
  141.3 2.3 %fusion = f32[4,64,8,256]{3,1,2,0:T(8,128)S(1)} fusion(f32[4,64,8,256]{3,2,1,0:T(8,128)S(1)} %pad_maximum_fusion.2, f32[128,128]{1,0:T(8,128)S(1)} %get-tuple-element.19, f32[128,128]{1,0:T(8,128)S(1)} %fusion.77, f32[128,128]{1,0:T(8,128)S(1)} %get-tuple-element.18), kind=kOutput, calls=%fused_computation.5 | convolution fusion | flops 1610809344 | bytes 4390912 | tf_op jit(solution)/shard_map/fkam,mj->fkaj/dot_general | solution.py:96
  143.5 1.3 fusion.18
  144.9 1.6 fusion.5
  146.5 0.6 copy.68
  147.1 0.7 copy.43
  147.8 34.5 %all_to_all.10 = f32[4,512,128]{2,0,1:T(4,128)S(1)} all-to-all(f32[4,512,128]{2,0,1:T(4,128)S(1)} %copy.43), channel_id=1, replica_groups=mesh['gx'=64,'gz'=4] {'gx'}, dimensions={1} | all-to-all | bytes 2097152 | tf_op jit(solution)/shard_map/all_to_all | solution.py:107
  182.3 3.5 %convolution_bitcast_fusion = f32[4,1,512,128]{2,3,0,1:T(8,128)S(1)} fusion(f32[512,512]{1,0:T(8,128)S(1)} %copy-done.1, f32[4,512,128]{2,0,1:T(4,128)S(1)} %all_to_all.10), kind=kOutput, calls=%fused_computation.13 | convolution fusion | flops 1611399168 | bytes 3145728 | tf_op jit(solution)/shard_map/ya,fax->fyx/dot_general | solution.py:108
  185.8 1.3 copy.45
  (16 shorter events, 0.7 us)
Async XLA Ops:
  6.5 84.5 %reduce-scatter.2.cloned.1.call-start = ((), (), s32[]{:S(2)}) async-start(), calls=%async_computation.3 | async-start | bytes 2621440 | tf_op jit(solution)/shard_map/reduce_scatter | solution.py:44
  54.8 1.2 copy-start.2
  56.1 36.1 %copy-start = (f32[512,512]{1,0:T(8,128)S(1)}, f32[512,512]{1,0:T(8,128)}, u32[]{:S(2)}) copy-start(f32[512,512]{1,0:T(8,128)} %param.16) | copy-start | bytes 3145732
  95.4 39.2 %all-to-all-start = ((f32[4,512,128]{2,0,1:T(4,128)}), f32[4,512,128]{2,0,1:T(4,128)S(1)}, u32[]{:S(2)}, u32[]{:S(2)}) async-start(f32[4,512,128]{2,0,1:T(4,128)} %copy.35), calls=%async_computation.1 | async-start | bytes 2097152 | tf_op jit(solution)/shard_map/all_to_all | solution.py:49
  137.6 3.0 %copy-start.3 = (f32[4]{0:T(128)S(1)}, f32[4]{0:T(128)}, u32[]{:S(2)}) copy-start(f32[4]{0:T(128)} %param.13) | copy-start | bytes 52
  147.1 35.2 %copy-start.1 = (f32[512,512]{1,0:T(8,128)S(1)}, f32[512,512]{1,0:T(8,128)}, u32[]{:S(2)}) copy-start(f32[512,512]{1,0:T(8,128)} %param.15) | copy-start | bytes 3145732
Sparse Core Ops, SparseCore 0:
  54.9 36.0 reduce-scatter.1

commit v2 on v1

--- a/solution.py
+++ b/solution.py
@@ -3,6 +3,8 @@
 import jax
 import jax.numpy as jnp
 from jax import lax
+from jax.experimental import pallas as pl
+from jax.experimental.pallas import tpu as pltpu
 from jax.sharding import PartitionSpec as P
 
 HI = lax.Precision.HIGHEST
@@ -11,6 +13,72 @@
 def phase(numer, length):
     angle = 2.0 * math.pi / length * (numer % length).astype(jnp.float32)
     return jnp.cos(angle), jnp.sin(angle)
+
+
+PIECES = 3
+CHUNK = 2048
+
+
+def source_kernel(row_ref, col_ref, piece_ref, out_ref):
+    step = pl.program_id(0)
+    row_count = out_ref.shape[0]
+    slab_width = out_ref.shape[1] // piece_ref.shape[0]
+    chunk = row_ref.shape[1]
+    rows = row_ref[...]
+    cols = col_ref[...]
+    row_hit = lax.broadcasted_iota(jnp.int32, (row_count, chunk), 0) == rows
+    lhs = jnp.where(row_hit, 1.0, 0.0).astype(jnp.bfloat16)
+    col_hit = lax.broadcasted_iota(jnp.int32, (slab_width, chunk), 0) == cols
+    pieces = piece_ref[...]
+    rhs = jnp.concatenate(
+        [jnp.where(col_hit, pieces[p : p + 1, :], 0.0) for p in range(pieces.shape[0])], axis=0
+    ).astype(jnp.bfloat16)
+    part = lax.dot_general(
+        lhs, rhs, (((1,), (1,)), ((), ())), preferred_element_type=jnp.float32
+    )
+
+    @pl.when(step == 0)
+    def _():
+        out_ref[...] = part
+
+    @pl.when(step > 0)
+    def _():
+        out_ref[...] += part
+
+
+def drop_source(cells, rates, row_count, slab_width):
+    drops = cells.shape[0]
+    pieces = []
+    rest = rates
+    for _ in range(PIECES):
+        piece = lax.reduce_precision(rest, exponent_bits=8, mantissa_bits=7)
+        pieces.append(piece)
+        rest = rest - piece
+    pieces = jnp.stack(pieces, axis=1).reshape(2 * PIECES, drops)
+    rows = (cells // slab_width).reshape(1, drops)
+    cols = (cells % slab_width).reshape(1, drops)
+    width = 2 * PIECES * slab_width
+    chunk = min(CHUNK, drops)
+    summed = pl.pallas_call(
+        source_kernel,
+        grid=(drops // chunk,),
+        in_specs=[
+            pl.BlockSpec((1, chunk), lambda i: (0, i)),
+            pl.BlockSpec((1, chunk), lambda i: (0, i)),
+            pl.BlockSpec((2 * PIECES, chunk), lambda i: (0, i)),
+        ],
+        out_specs=pl.BlockSpec((row_count, width), lambda i: (0, 0)),
+        out_shape=jax.ShapeDtypeStruct((row_count, width), jnp.float32),
+        compiler_params=pltpu.CompilerParams(vmem_limit_bytes=48 * 1024 * 1024),
+        cost_estimate=pl.CostEstimate(
+            flops=2 * row_count * width * drops, transcendentals=0, bytes_accessed=4 * row_count * width
+        ),
+    )(rows, cols, pieces)
+    summed = summed.reshape(row_count, 2, PIECES, slab_width)
+    total = summed[:, :, 0]
+    for p in range(1, PIECES):
+        total = total + summed[:, :, p]
+    return jnp.transpose(total, (1, 0, 2))
 
 
 def per_device(
@@ -31,18 +99,13 @@
     plane_cells = row_count * slab_width
     rows_here = row_count // gx_count
 
-    flat_cell = drop_plane * plane_cells + drop_cell
-    partial_value = jnp.stack(
-        [
-            jax.ops.segment_sum(
-                drop_rate[component], flat_cell, num_segments=plane_count * gz_count * plane_cells
-            )
-            for component in range(2)
-        ]
-    )
-    partial_value = partial_value.reshape(2, plane_count * gz_count, row_count, slab_width)
-    source = lax.psum_scatter(partial_value, "gz", scatter_dimension=1, tiled=True)
-    right_side = jnp.concatenate([field[:2], field[2:] + source], axis=0)[:, 0]
+    plane_here = lax.axis_index("gz")
+    cells = lax.all_gather(drop_cell, "gz", tiled=True)
+    planes = lax.all_gather(drop_plane, "gz", tiled=True)
+    rates = lax.all_gather(drop_rate, "gz", axis=1, tiled=True)
+    rates = jnp.where((planes == plane_here)[None, :], rates, 0.0)
+    source = drop_source(cells, rates, row_count, slab_width)
+    right_side = jnp.concatenate([field[:2], field[2:] + source[:, None]], axis=0)[:, 0]
     identity = jnp.eye(row_count, dtype=jnp.float32)
     projected = jnp.einsum("ay,fyx->fax", identity + dual_part, right_side, precision=HI)
 

time: 194 us -> 156 us (0.80)
  other arithmetic: 49.6 us -> 2.41 us
  waiting for transfers between devices: 60.6 us -> 26 us
  blocking collectives: 34.5 us -> 63.5 us
  Pallas kernels: 0 us -> 16.1 us
  between operations: 14.3 us -> 0.91 us
  starting transfers between devices: 10.8 us -> 21.1 us
    scatter-add x2 -> x0, other arithmetic: 44.3 us -> none  [per_device(): jax.ops.segment_sum(drop_rate[component], flat_cell, num_segments=plane_c...]
    reduce_scatter x1 -> x0, waiting for transfers between devices: 34.5 us -> none  [per_device(): lax.psum_scatter(partial_value, 'gz', scatter_dimension=1, tiled=True)]
    all_gather x0 -> x3, blocking collectives: none -> 28.9 us  [the longest x1 10.4 us: per_device(): cells = lax.all_gather(drop_cell, 'gz', tiled=True)]
    pallas_call x0 -> x1, Pallas kernels: none -> 16.1 us  [drop_source(): pl.pallas_call(source_kernel, grid=(drops // chunk,), in_specs=[pl.BlockS...]
    all_to_all x1, starting transfers between devices: 10.8 us -> 21.1 us  [per_device(): spread = lax.all_to_all(projected, 'gx', 1, 1, tiled=True)]
  transfers between devices with their start and end apart: 2 -> 1, of which waited for: 2 -> 1; matrix products, arithmetic and copies ran while one was open for 1% -> 1% of each run, Pallas kernels for 0% -> 0%
where the time goes in v2:
time: 156 us; the launch traced here: 155 us
  blocking collectives  63.5 us (41%)
  waiting for transfers between devices  26 us (17%)
  starting transfers between devices  21.1 us (14%)
  matrix products  16.2 us (10%)
  Pallas kernels  16.1 us (10%)
  local copies, waits for them, and re-layouts  9.28 us (6%)
  other arithmetic  2.41 us (2%)
    all_to_all x1, blocking collectives, per_device(): gathered = lax.all_to_all(filtered, 'gx', 1, 1, tiled=True)  34.6 us
    all_to_all x1, waiting for transfers between devices, per_device(): spread = lax.all_to_all(projected, 'gx', 1, 1, tiled=True)  26 us
    all_to_all x1, starting transfers between devices, per_device(): spread = lax.all_to_all(projected, 'gx', 1, 1, tiled=True)  21.1 us
    pallas_call x1, Pallas kernels, drop_source(): pl.pallas_call(source_kernel, grid=(drops // chunk,), in_specs=[pl.BlockS...  16.1 us
    all_gather x1, blocking collectives, per_device(): cells = lax.all_gather(drop_cell, 'gz', tiled=True)  10.4 us
    all_gather x1, blocking collectives, per_device(): rates = lax.all_gather(drop_rate, 'gz', axis=1, tiled=True)  9.32 us
    all_gather x1, blocking collectives, per_device(): planes = lax.all_gather(drop_plane, 'gz', tiled=True)  9.24 us
    dot_general x1, matrix products, per_device(): jnp.einsum('ya,fax->fyx', identity + basis_part, gathered, precision=HI)  3.48 us
  transfers between devices with their start and end apart: 1, of which 1 were waited for; matrix products, arithmetic and copies ran while one was open for 1% of the time, Pallas kernels for 0%

profile of v2, /device:TPU:1, one launch (start us, length us, event | category | flops | bytes accessed | tf_op | source)
XLA Modules:
  0.0 155.5 jit_solution(3192382455929676348)
XLA Ops:
  0.0 10.4 %all_gather.9 = s32[16384]{0:T(1024)S(1)} all-gather(s32[4096]{0:T(1024)} %param.10), channel_id=1, replica_groups=mesh['gx'=64,'gz'=4] {'gz'}, dimensions={0}, use_global_device_ids=true | all-gather | bytes 81920 | tf_op jit(solution)/shard_map/all_gather | solution.py:103
  10.4 9.2 %all_gather.10 = s32[16384]{0:T(1024)S(1)} all-gather(s32[4096]{0:T(1024)} %param.11), channel_id=1, replica_groups=mesh['gx'=64,'gz'=4] {'gz'}, dimensions={0}, use_global_device_ids=true | all-gather | bytes 81920 | tf_op jit(solution)/shard_map/all_gather | solution.py:104
  19.7 9.3 %all_gather.11 = f32[2,16384]{1,0:T(2,128)S(1)} all-gather(f32[2,4096]{1,0:T(2,128)} %param.12), channel_id=1, replica_groups=mesh['gx'=64,'gz'=4] {'gz'}, dimensions={1}, use_global_device_ids=true | all-gather | bytes 163840 | tf_op jit(solution)/shard_map/all_gather | solution.py:105
  29.2 0.2 pad_maximum_fusion.2
  29.3 0.3 copy.40
  29.8 16.1 %shard_map.91 = f32[512,768]{1,0:T(8,128)S(1)} custom-call(s32[1,16384]{1,0:T(1,128)S(1)} %bitcast.90, s32[1,16384]{1,0:T(1,128)S(1)} %bitcast.89, f32[6,16384]{1,0:T(8,128)S(1)} %reshape.143.piece_ref), custom_call_target="tpu_custom_call" | custom-call | flops 12884901888 | bytes 1572864 | tf_op jit(solution)/shard_map/pallas_call | solution.py:62
  45.9 0.5 copy.41
  46.4 1.3 fusion.109
  47.6 1.0 copy.62
  48.6 0.2 copy.63
  48.9 0.2 fusion.30
  49.1 0.8 copy-done
  49.9 0.3 copy-done.1
  50.2 1.9 %convolution_bitcast_fusion.2 = f32[4,512,128]{1,2,0:T(8,128)S(1)} fusion(f32[512,512]{1,0:T(8,128)S(1)} %copy-done.1, f32[2,1,512,128]{2,3,0,1:T(8,128)S(1)} %fusion.30, f32[2,1,512,128]{2,3,0,1:T(8,128)S(1)} %copy-done), kind=kOutput, calls=%fused_computation.17 | convolution fusion | flops 1611661312 | bytes 3145728 | tf_op jit(solution)/shard_map/ay,fyx->fax/dot_general | solution.py:110
  52.1 1.3 copy.45
  53.4 21.1 %all-to-all-start = ((f32[4,512,128]{2,0,1:T(4,128)}), f32[4,512,128]{2,0,1:T(4,128)S(1)}, u32[]{:S(2)}, u32[]{:S(2)}) async-start(f32[4,512,128]{2,0,1:T(4,128)} %copy.45), calls=%async_computation | async-start | bytes 2097152 | tf_op jit(solution)/shard_map/all_to_all | solution.py:112
  75.2 0.8 dynamic_slice.3
  75.9 0.3 fusion.81
  76.3 0.3 fusion.73
  76.9 26.0 %all-to-all-done = f32[4,512,128]{2,0,1:T(4,128)S(1)} async-done(((f32[4,512,128]{2,0,1:T(4,128)}), f32[4,512,128]{2,0,1:T(4,128)S(1)}, u32[]{:S(2)}, u32[]{:S(2)}) %all-to-all-start) | async-done | bytes 1048608 | tf_op jit(solution)/shard_map/all_to_all | solution.py:112
  103.0 1.2 convolution_bitcast_fusion.1
  104.2 1.5 multiply_add_fusion.2
  105.9 2.9 %fusion.2 = f32[4,64,8,256]{3,2,1,0:T(8,128)S(1)} fusion(f32[4,64,8,256]{3,1,2,0:T(8,128)S(1)} %pad_maximum_fusion, f32[128,128]{1,0:T(8,128)S(1)} %get-tuple-element.22, f32[128,128]{1,0:T(8,128)S(1)} %get-tuple-element.21, f32[128,128]{1,0:T(8,128)S(1)} %fusion.81), kind=kOutput, calls=%fused_computation.4 | convolution fusion | flops 1610809344 | bytes 4390912 | tf_op jit(solution)/shard_map/fkaj,jm->fkam/dot_general | solution.py:131
  108.9 0.6 multiply_subtract_fusion.1
  109.6 2.3 %fusion = f32[4,64,8,256]{3,1,2,0:T(8,128)S(1)} fusion(f32[4,64,8,256]{3,2,1,0:T(8,128)S(1)} %pad_maximum_fusion.1, f32[128,128]{1,0:T(8,128)S(1)} %get-tuple-element.22, f32[128,128]{1,0:T(8,128)S(1)} %fusion.81, f32[128,128]{1,0:T(8,128)S(1)} %get-tuple-element.21), kind=kOutput, calls=%fused_computation.2 | convolution fusion | flops 1610809344 | bytes 4390912 | tf_op jit(solution)/shard_map/fkam,mj->fkaj/dot_general | solution.py:159
  111.9 1.3 fusion.18
  113.2 1.6 %fusion.5 = f32[4,64,8,128]{3,1,2,0:T(8,128)S(1)} fusion(f32[4,8,128,64]{2,3,1,0:T(8,128)S(1)} %fusion.18, f32[4,64,8,256]{3,1,2,0:T(8,128)S(1)} %fusion, f32[64,128]{1,0:T(8,128)S(1)} %get-tuple-element.19, f32[64,128]{1,0:T(8,128)S(1)} %get-tuple-element.20), kind=kOutput, calls=%fused_computation.13 | convolution fusion | flops 202694656 | bytes 4259840 | tf_op jit(solution)/shard_map/dk,fkaj->fdaj/dot_general | solution.py:166
  114.8 0.6 copy.81
  115.4 0.7 copy.53
  116.1 34.6 %all_to_all.10 = f32[4,512,128]{2,0,1:T(4,128)S(1)} all-to-all(f32[4,512,128]{2,0,1:T(4,128)S(1)} %copy.53), channel_id=1, replica_groups=mesh['gx'=64,'gz'=4] {'gx'}, dimensions={1} | all-to-all | bytes 2097152 | tf_op jit(solution)/shard_map/all_to_all | solution.py:170
  150.7 3.5 %convolution_bitcast_fusion = f32[4,1,512,128]{2,3,0,1:T(8,128)S(1)} fusion(f32[512,512]{1,0:T(8,128)S(1)} %copy-done.2, f32[4,512,128]{2,0,1:T(4,128)S(1)} %all_to_all.10), kind=kOutput, calls=%fused_computation.10 | convolution fusion | flops 1611399168 | bytes 3145728 | tf_op jit(solution)/shard_map/ya,fax->fyx/dot_general | solution.py:171
  154.2 1.3 copy.55
  (17 shorter events, 1.2 us)
Async XLA Ops:
  48.8 1.0 copy-start
  48.9 1.4 copy-start.1
  53.4 49.5 %all-to-all-start = ((f32[4,512,128]{2,0,1:T(4,128)}), f32[4,512,128]{2,0,1:T(4,128)S(1)}, u32[]{:S(2)}, u32[]{:S(2)}) async-start(f32[4,512,128]{2,0,1:T(4,128)} %copy.45), calls=%async_computation | async-start | bytes 2097152 | tf_op jit(solution)/shard_map/all_to_all | solution.py:112
  105.9 3.0 %copy-start.3 = (f32[4]{0:T(128)S(1)}, f32[4]{0:T(128)}, u32[]{:S(2)}) copy-start(f32[4]{0:T(128)} %param.13) | copy-start | bytes 52
  115.4 35.3 %copy-start.2 = (f32[512,512]{1,0:T(8,128)S(1)}, f32[512,512]{1,0:T(8,128)}, u32[]{:S(2)}) copy-start(f32[512,512]{1,0:T(8,128)} %param.15) | copy-start | bytes 3145732

commit v3 on v2

--- a/solution.py
+++ b/solution.py
@@ -100,10 +100,18 @@
     rows_here = row_count // gx_count
 
     plane_here = lax.axis_index("gz")
-    cells = lax.all_gather(drop_cell, "gz", tiled=True)
-    planes = lax.all_gather(drop_plane, "gz", tiled=True)
-    rates = lax.all_gather(drop_rate, "gz", axis=1, tiled=True)
-    rates = jnp.where((planes == plane_here)[None, :], rates, 0.0)
+    packed = jnp.concatenate(
+        [(drop_plane * plane_cells + drop_cell).astype(jnp.float32)[None, :], drop_rate], axis=0
+    )
+    shares = [packed] + [
+        lax.ppermute(packed, "gz", [(i, (i + shift) % gz_count) for i in range(gz_count)])
+        for shift in range(1, gz_count)
+    ]
+    packed = jnp.concatenate(shares, axis=1)
+    keys = packed[0].astype(jnp.int32)
+    cells = keys % plane_cells
+    planes = keys // plane_cells
+    rates = jnp.where((planes == plane_here)[None, :], packed[1:], 0.0)
     source = drop_source(cells, rates, row_count, slab_width)
     right_side = jnp.concatenate([field[:2], field[2:] + source[:, None]], axis=0)[:, 0]
     identity = jnp.eye(row_count, dtype=jnp.float32)

time: 156 us -> 129 us (0.83)
  blocking collectives: 63.5 us -> 34.6 us
  other arithmetic: 2.41 us -> 6.29 us
  starting transfers between devices: 21.1 us -> 18.4 us
    all_gather x3 -> x0, blocking collectives: 28.9 us -> none  [the longest x1 10.4 us: per_device(): cells = lax.all_gather(drop_cell, 'gz', tiled=True)]
    all_to_all x1, starting transfers between devices: 21.1 us -> 13.9 us  [per_device(): spread = lax.all_to_all(projected, 'gx', 1, 1, tiled=True)]
    ppermute x0 -> x3, starting transfers between devices: none -> 4.51 us  [per_device(): lax.ppermute(packed, 'gz', [(i, (i + shift) % gz_count) for i in range(gz...]
  transfers between devices with their start and end apart: 1 -> 4, of which waited for: 1 -> 3; matrix products, arithmetic and copies ran while one was open for 1% -> 4% of each run, Pallas kernels for 0% -> 0%
where the time goes in v3:
time: 129 us
  blocking collectives  34.6 us (27%)
  waiting for transfers between devices  26.9 us (21%)
  starting transfers between devices  18.4 us (14%)
  matrix products  16.2 us (13%)
  Pallas kernels  16.1 us (12%)
  local copies, waits for them, and re-layouts  9.08 us (7%)
  other arithmetic  6.29 us (5%)
    all_to_all x1, blocking collectives, per_device(): gathered = lax.all_to_all(filtered, 'gx', 1, 1, tiled=True)  34.6 us
    all_to_all x1, waiting for transfers between devices, per_device(): spread = lax.all_to_all(projected, 'gx', 1, 1, tiled=True)  26 us
    pallas_call x1, Pallas kernels, drop_source(): pl.pallas_call(source_kernel, grid=(drops // chunk,), in_specs=[pl.BlockS...  16.1 us
    all_to_all x1, starting transfers between devices, per_device(): spread = lax.all_to_all(projected, 'gx', 1, 1, tiled=True)  13.9 us
    ppermute x3, starting transfers between devices, per_device(): lax.ppermute(packed, 'gz', [(i, (i + shift) % gz_count) for i in range(gz...  4.51 us
    dot_general x1, matrix products, per_device(): jnp.einsum('ya,fax->fyx', identity + basis_part, gathered, precision=HI)  3.48 us
    dot_general x1, matrix products, per_device(): spec = jnp.einsum('fkaj,jm->fkam', joined, forward_table, precision=HI)  2.94 us
  transfers between devices with their start and end apart: 4, of which 3 were waited for; matrix products, arithmetic and copies ran while one was open for 4% of the time, Pallas kernels for 0%

profile of v3, /device:TPU:1, one launch (start us, length us, event | category | flops | bytes accessed | tf_op | source)
XLA Modules:
  0.0 128.5 jit_solution(3710307707555874078)
XLA Ops:
  0.0 0.7 add_convert_fusion
  0.7 0.8 pad_maximum_fusion.13
  1.5 3.4 %collective-permute-start.2 = (f32[3,4096]{1,0:T(4,128)S(1)}, f32[3,4096]{1,0:T(4,128)S(1)}, u32[]{:S(2)}, u32[]{:S(2)}) collective-permute-start(f32[3,4096]{1,0:T(4,128)S(1)} %pad_maximum_fusion.13), channel_id=1, source_target_pairs={{0,3},{1,0},{2,1},{3,2},{4,7},{5,4},{6,5},{7,6},{8,11},{9,8},{10,9... | collective-permute-start | bytes 147464 | tf_op jit(solution)/shard_map/ppermute | solution.py:107
  4.9 0.5 collective-permute-start.1
  5.5 0.6 collective-permute-start
  6.1 1.3 fusion.109
  7.3 1.0 copy.62
  8.3 1.0 copy.63
  9.6 0.7 collective-permute-done
  10.3 0.5 compare_reduce_fusion
  10.8 0.3 and_select_fusion.1
  11.1 0.3 and_select_fusion.2.row_ref
  12.4 16.1 %shard_map.91 = f32[512,768]{1,0:T(8,128)S(1)} custom-call(s32[1,16384]{1,0:T(1,128)S(1)} %and_select_fusion.2.row_ref, s32[1,16384]{1,0:T(1,128)S(1)} %get-tuple-element.9.col_ref, f32[6,16384]{1,0:T(8,128)S(1)} %reshape.136.piece_ref), custom_call_target="tpu_custom_call" | custom-call | flops 12884901888 | bytes 1572864 | tf_op jit(solution)/shard_map/pallas_call | solution.py:62
  28.4 0.5 copy.41
  28.9 1.4 %fusion.30 = f32[2,1,512,128]{2,3,0,1:T(8,128)S(1)} fusion(f32[2,1,512,128]{2,3,0,1:T(8,128)} %copy.63, f32[512,2,3,128]{0,3,2,1:T(8,128)S(1)} %bitcast.90), kind=kLoop, calls=%fused_computation.49 | loop fusion | flops 393216 | bytes 2621440 | tf_op jit(solution)/shard_map/add | solution.py:116
  30.5 1.9 %convolution_bitcast_fusion.2 = f32[4,512,128]{1,2,0:T(8,128)S(1)} fusion(f32[512,512]{1,0:T(8,128)S(1)} %copy-done.1, f32[2,1,512,128]{2,3,0,1:T(8,128)S(1)} %fusion.30, f32[2,1,512,128]{2,3,0,1:T(8,128)S(1)} %copy-done), kind=kOutput, calls=%fused_computation.17 | convolution fusion | flops 1611661312 | bytes 3145728 | tf_op jit(solution)/shard_map/ay,fyx->fax/dot_general | solution.py:118
  32.3 1.3 %copy.45 = f32[4,512,128]{2,0,1:T(4,128)} copy(f32[4,512,128]{1,2,0:T(8,128)S(1)} %convolution_bitcast_fusion.2) | data formatting | bytes 2097152 | tf_op jit(solution)/shard_map/ay,fyx->fax/transpose | solution.py:118
  33.6 13.9 %all-to-all-start = ((f32[4,512,128]{2,0,1:T(4,128)}), f32[4,512,128]{2,0,1:T(4,128)S(1)}, u32[]{:S(2)}, u32[]{:S(2)}) async-start(f32[4,512,128]{2,0,1:T(4,128)} %copy.45), calls=%async_computation | async-start | bytes 2097152 | tf_op jit(solution)/shard_map/all_to_all | solution.py:120
  48.2 0.8 dynamic_slice.3
  49.9 26.0 %all-to-all-done = f32[4,512,128]{2,0,1:T(4,128)S(1)} async-done(((f32[4,512,128]{2,0,1:T(4,128)}), f32[4,512,128]{2,0,1:T(4,128)S(1)}, u32[]{:S(2)}, u32[]{:S(2)}) %all-to-all-start) | async-done | bytes 1048608 | tf_op jit(solution)/shard_map/all_to_all | solution.py:120
  76.0 1.3 convolution_bitcast_fusion.1
  77.3 1.5 %multiply_add_fusion.2 = (f32[4,64,8,128]{3,1,2,0:T(8,128)S(1)}, f32[4,64,8,128]{3,1,2,0:T(8,128)S(1)}) fusion(f32[4,64,8,128]{3,1,2,0:T(8,128)S(1)} %convolution_bitcast_fusion.1, f32[64,128]{1,0:T(8,128)S(1)} %get-tuple-element.22, f32[64,128]{1,0:T(8,128)S(1)} %get-tuple-element.23, f32[4,64,8,128]{3,2,1,0:T(8,128)S(1)} %bitcast.89), kind=kOutput, calls=%fused_computation.38 | convolution fusion | flops 203218944 | bytes 4259840 | tf_op jit(solution)/shard_map/kd,fdaj->fkaj/dot_general | solution.py:130
  79.0 2.9 %fusion.2 = f32[4,64,8,256]{3,2,1,0:T(8,128)S(1)} fusion(f32[4,64,8,256]{3,1,2,0:T(8,128)S(1)} %pad_maximum_fusion, f32[128,128]{1,0:T(8,128)S(1)} %get-tuple-element.25, f32[128,128]{1,0:T(8,128)S(1)} %get-tuple-element.24, f32[128,128]{1,0:T(8,128)S(1)} %fusion.80), kind=kOutput, calls=%fused_computation.4 | convolution fusion | flops 1610809344 | bytes 4390912 | tf_op jit(solution)/shard_map/fkaj,jm->fkam/dot_general | solution.py:139
  81.9 0.6 multiply_subtract_fusion.1
  82.7 2.3 %fusion = f32[4,64,8,256]{3,1,2,0:T(8,128)S(1)} fusion(f32[4,64,8,256]{3,2,1,0:T(8,128)S(1)} %pad_maximum_fusion.1, f32[128,128]{1,0:T(8,128)S(1)} %get-tuple-element.25, f32[128,128]{1,0:T(8,128)S(1)} %fusion.80, f32[128,128]{1,0:T(8,128)S(1)} %get-tuple-element.24), kind=kOutput, calls=%fused_computation.2 | convolution fusion | flops 1610809344 | bytes 4390912 | tf_op jit(solution)/shard_map/fkam,mj->fkaj/dot_general | solution.py:167
  84.9 1.3 %fusion.18 = f32[4,8,128,64]{2,3,1,0:T(8,128)S(1)} fusion(f32[4,64,8,256]{3,1,2,0:T(8,128)S(1)} %fusion, f32[64,128]{1,0:T(8,128)S(1)} %get-tuple-element.22, f32[64,128]{1,0:T(8,128)S(1)} %get-tuple-element.23), kind=kOutput, calls=%fused_computation.30 | convolution fusion | flops 202170368 | bytes 3211264 | tf_op jit(solution)/shard_map/dk,fkaj->fdaj/dot_general | solution.py:173
  86.3 1.6 %fusion.5 = f32[4,64,8,128]{3,1,2,0:T(8,128)S(1)} fusion(f32[4,8,128,64]{2,3,1,0:T(8,128)S(1)} %fusion.18, f32[4,64,8,256]{3,1,2,0:T(8,128)S(1)} %fusion, f32[64,128]{1,0:T(8,128)S(1)} %get-tuple-element.22, f32[64,128]{1,0:T(8,128)S(1)} %get-tuple-element.23), kind=kOutput, calls=%fused_computation.13 | convolution fusion | flops 202694656 | bytes 4259840 | tf_op jit(solution)/shard_map/dk,fkaj->fdaj/dot_general | solution.py:174
  87.9 0.6 copy.81
  88.5 0.7 copy.53
  89.2 34.6 %all_to_all.10 = f32[4,512,128]{2,0,1:T(4,128)S(1)} all-to-all(f32[4,512,128]{2,0,1:T(4,128)S(1)} %copy.53), channel_id=1, replica_groups=mesh['gx'=64,'gz'=4] {'gx'}, dimensions={1} | all-to-all | bytes 2097152 | tf_op jit(solution)/shard_map/all_to_all | solution.py:178
  123.7 3.5 %convolution_bitcast_fusion = f32[4,1,512,128]{2,3,0,1:T(8,128)S(1)} fusion(f32[512,512]{1,0:T(8,128)S(1)} %copy-done.2, f32[4,512,128]{2,0,1:T(4,128)S(1)} %all_to_all.10), kind=kOutput, calls=%fused_computation.10 | convolution fusion | flops 1611399168 | bytes 3145728 | tf_op jit(solution)/shard_map/ya,fax->fyx/dot_general | solution.py:179
  127.2 1.3 %copy.55 = f32[4,1,512,128]{3,2,1,0:T(8,128)} copy(f32[4,1,512,128]{2,3,0,1:T(8,128)S(1)} %convolution_bitcast_fusion) | data formatting | bytes 2097152 | tf_op jit(solution)/shard_map/broadcast_in_dim | solution.py:180
  (26 shorter events, 2.6 us)
Async XLA Ops:
  1.5 8.7 %copy-start.3 = (f32[2,4096]{1,0:T(2,128)S(1)}, f32[2,4096]{1,0:T(2,128)}, u32[]{:S(2)}) copy-start(f32[2,4096]{1,0:T(2,128)} %param.12) | copy-start | bytes 98308
  1.5 7.8 %collective-permute-start.2 = (f32[3,4096]{1,0:T(4,128)S(1)}, f32[3,4096]{1,0:T(4,128)S(1)}, u32[]{:S(2)}, u32[]{:S(2)}) collective-permute-start(f32[3,4096]{1,0:T(4,128)S(1)} %pad_maximum_fusion.13), channel_id=1, source_target_pairs={{0,3},{1,0},{2,1},{3,2},{4,7},{5,4},{6,5},{7,6},{8,11},{9,8},{10,9... | collective-permute-start | bytes 147464 | tf_op jit(solution)/shard_map/ppermute | solution.py:107
  4.9 4.7 %collective-permute-start.1 = (f32[3,4096]{1,0:T(4,128)S(1)}, f32[3,4096]{1,0:T(4,128)S(1)}, u32[]{:S(2)}, u32[]{:S(2)}) collective-permute-start(f32[3,4096]{1,0:T(4,128)S(1)} %pad_maximum_fusion.13), channel_id=1, source_target_pairs={{0,2},{1,3},{2,0},{3,1},{4,6},{5,7},{6,4},{7,5},{8,10},{9,11},{10,... | collective-permute-start | bytes 147464 | tf_op jit(solution)/shard_map/ppermute | solution.py:107
  5.5 4.8 %collective-permute-start = (f32[3,4096]{1,0:T(4,128)S(1)}, f32[3,4096]{1,0:T(4,128)S(1)}, u32[]{:S(2)}, u32[]{:S(2)}) collective-permute-start(f32[3,4096]{1,0:T(4,128)S(1)} %pad_maximum_fusion.13), channel_id=1, source_target_pairs={{0,1},{1,2},{2,3},{3,0},{4,5},{5,6},{6,7},{7,4},{8,9},{9,10},{10,1... | collective-permute-start | bytes 147464 | tf_op jit(solution)/shard_map/ppermute | solution.py:107
  28.9 1.4 %copy-start = (f32[2,1,512,128]{2,3,0,1:T(8,128)S(1)}, f32[2,1,512,128]{2,3,0,1:T(8,128)}, u32[]{:S(2)}) copy-start(f32[2,1,512,128]{2,3,0,1:T(8,128)} %copy.62) | copy-start | bytes 1572868
  28.9 1.5 %copy-start.1 = (f32[512,512]{1,0:T(8,128)S(1)}, f32[512,512]{1,0:T(8,128)}, u32[]{:S(2)}) copy-start(f32[512,512]{1,0:T(8,128)} %param.16) | copy-start | bytes 3145732
  33.6 42.3 %all-to-all-start = ((f32[4,512,128]{2,0,1:T(4,128)}), f32[4,512,128]{2,0,1:T(4,128)S(1)}, u32[]{:S(2)}, u32[]{:S(2)}) async-start(f32[4,512,128]{2,0,1:T(4,128)} %copy.45), calls=%async_computation | async-start | bytes 2097152 | tf_op jit(solution)/shard_map/all_to_all | solution.py:120
  79.0 3.0 %copy-start.4 = (f32[4]{0:T(128)S(1)}, f32[4]{0:T(128)}, u32[]{:S(2)}) copy-start(f32[4]{0:T(128)} %param.13) | copy-start | bytes 52
  88.5 35.3 %copy-start.2 = (f32[512,512]{1,0:T(8,128)S(1)}, f32[512,512]{1,0:T(8,128)}, u32[]{:S(2)}) copy-start(f32[512,512]{1,0:T(8,128)} %param.15) | copy-start | bytes 3145732

commit v4 on v3

--- a/solution.py
+++ b/solution.py
@@ -113,18 +113,47 @@
     planes = keys // plane_cells
     rates = jnp.where((planes == plane_here)[None, :], packed[1:], 0.0)
     source = drop_source(cells, rates, row_count, slab_width)
-    right_side = jnp.concatenate([field[:2], field[2:] + source[:, None]], axis=0)[:, 0]
     identity = jnp.eye(row_count, dtype=jnp.float32)
-    projected = jnp.einsum("ay,fyx->fax", identity + dual_part, right_side, precision=HI)
-
-    spread = lax.all_to_all(projected, "gx", 1, 1, tiled=True)
-    spread = spread.reshape(field_count, gx_count, rows_here, slab_width)
-
+    dual_full = identity + dual_part
+    basis_full = identity + basis_part
+    position = lax.axis_index("gx")
+    eigen_here = lax.dynamic_slice_in_dim(wall_eigen, position * rows_here, rows_here)
+    tables = dft_tables(gx_count, slab_width)
+
+    calm = filter_group(field[:2, 0], dual_full, basis_full, diffusivity[:2], eigen_here, bulk_shift, tables)
+    fed = filter_group(
+        field[2:, 0] + source, dual_full, basis_full, diffusivity[2:], eigen_here, bulk_shift, tables
+    )
+    return jnp.concatenate([calm, fed], axis=0)[:, None]
+
+
+def dft_tables(gx_count, slab_width):
+    total_cells = gx_count * slab_width
     d_index = jnp.arange(gx_count, dtype=jnp.int32)
     j_index = jnp.arange(slab_width, dtype=jnp.int32)
     c64, s64 = phase(d_index[:, None] * d_index[None, :], gx_count)
     ct, st = phase(d_index[:, None] * j_index[None, :], total_cells)
     c128, s128 = phase(j_index[:, None] * j_index[None, :], slab_width)
+    forward_table = jnp.concatenate(
+        [jnp.concatenate([c128, -s128], axis=1), jnp.concatenate([s128, c128], axis=1)], axis=0
+    )
+    inverse_table = jnp.concatenate(
+        [jnp.concatenate([c128, s128], axis=1), jnp.concatenate([-s128, c128], axis=1)], axis=0
+    )
+    mode_index = d_index[:, None] + gx_count * j_index[None, :]
+    return c64, s64, ct, st, forward_table, inverse_table, mode_index
+
+
+def filter_group(right_side, dual_full, basis_full, diffusivity, eigen_here, bulk_shift, tables):
+    c64, s64, ct, st, forward_table, inverse_table, mode_index = tables
+    field_count, row_count, slab_width = right_side.shape
+    gx_count = c64.shape[0]
+    rows_here = row_count // gx_count
+    total_cells = gx_count * slab_width
+    projected = jnp.einsum("ay,fyx->fax", dual_full, right_side, precision=HI)
+
+    spread = lax.all_to_all(projected, "gx", 1, 1, tiled=True)
+    spread = spread.reshape(field_count, gx_count, rows_here, slab_width)
 
     a_real = jnp.einsum("kd,fdaj->fkaj", c64, spread, precision=HI)
     a_imag = -jnp.einsum("kd,fdaj->fkaj", s64, spread, precision=HI)
@@ -133,18 +162,12 @@
     b_real = a_real * ct4 + a_imag * st4
     b_imag = a_imag * ct4 - a_real * st4
     joined = jnp.concatenate([b_real, b_imag], axis=-1)
-    forward_table = jnp.concatenate(
-        [jnp.concatenate([c128, -s128], axis=1), jnp.concatenate([s128, c128], axis=1)], axis=0
-    )
     spec = jnp.einsum("fkaj,jm->fkam", joined, forward_table, precision=HI)
     spec_real = spec[..., :slab_width]
     spec_imag = spec[..., slab_width:]
 
-    mode_index = d_index[:, None] + gx_count * j_index[None, :]
     folded = jnp.minimum(mode_index, total_cells - mode_index).astype(jnp.float32)
     wavenumber = 2.0 * math.pi / total_cells * folded
-    position = lax.axis_index("gx")
-    eigen_here = lax.dynamic_slice_in_dim(wall_eigen, position * rows_here, rows_here)
     growth = diffusivity[:, None, None, None] * (
         eigen_here[None, None, :, None] + (wavenumber**2)[None, :, None, :]
     )
@@ -161,9 +184,6 @@
     turned_imag = spec_real * factor_imag + spec_imag * factor_real
 
     joined = jnp.concatenate([turned_real, turned_imag], axis=-1)
-    inverse_table = jnp.concatenate(
-        [jnp.concatenate([c128, s128], axis=1), jnp.concatenate([-s128, c128], axis=1)], axis=0
-    )
     back = jnp.einsum("fkam,mj->fkaj", joined, inverse_table, precision=HI)
     back_real = back[..., :slab_width]
     back_imag = back[..., slab_width:]
@@ -176,8 +196,7 @@
 
     filtered = filtered.reshape(field_count, row_count, slab_width)
     gathered = lax.all_to_all(filtered, "gx", 1, 1, tiled=True)
-    result = jnp.einsum("ya,fax->fyx", identity + basis_part, gathered, precision=HI)
-    return result[:, None]
+    return jnp.einsum("ya,fax->fyx", basis_full, gathered, precision=HI)
 
 
 def solution(mesh):

time: 129 us -> 140 us (1.085)
  blocking collectives: 34.6 us -> 0 us
  starting transfers between devices: 18.4 us -> 42.1 us
  waiting for transfers between devices: 26.9 us -> 43.6 us
  matrix products: 16.2 us -> 20.2 us
  local copies, waits for them, and re-layouts: 9.08 us -> 10.8 us
    all_to_all x1 -> x0, blocking collectives: 34.6 us -> none  [per_device(): gathered = lax.all_to_all(filtered, 'gx', 1, 1, tiled=True)]
    all_to_all x1 -> x4, starting transfers between devices: 13.9 us -> 36.4 us  [the longest x2 23.8 us: filter_group(): spread = lax.all_to_all(projected, 'gx', 1, 1, tiled=True)]
    all_to_all x1 -> x4, waiting for transfers between devices: 26 us -> 43.6 us  [the longest x2 28.4 us: filter_group(): gathered = lax.all_to_all(filtered, 'gx', 1, 1, tiled=True)]
    dot_general x8 -> x16, matrix products: 16.2 us -> 20.2 us  [the longest x2 4.84 us: filter_group(): projected = jnp.einsum('ay,fyx->fax', dual_full, right_side, precision=HI)]
    unnamed x12 -> x11, local copies, waits for them, and re-layouts: 2.16 us -> 0.23 us
    reshape x1 -> x2, local copies, waits for them, and re-layouts: 0.68 us -> 2.41 us  [filter_group(): filtered = filtered.reshape(field_count, row_count, slab_width)]
  transfers between devices with their start and end apart: 4 -> 7, of which waited for: 3 -> 3; matrix products, arithmetic and copies ran while one was open for 4% -> 15% of each run, Pallas kernels for 0% -> 12%
where the time goes in v4:
time: 140 us; the launch traced here: 139 us
  waiting for transfers between devices  43.6 us (31%)
  starting transfers between devices  42.1 us (30%)
  matrix products  20.2 us (14%)
  Pallas kernels  16.1 us (12%)
  local copies, waits for them, and re-layouts  10.8 us (8%)
  other arithmetic  5.14 us (4%)
    all_to_all x2, waiting for transfers between devices, filter_group(): gathered = lax.all_to_all(filtered, 'gx', 1, 1, tiled=True)  28.4 us
    all_to_all x2, starting transfers between devices, filter_group(): spread = lax.all_to_all(projected, 'gx', 1, 1, tiled=True)  23.8 us
    pallas_call x1, Pallas kernels, drop_source(): pl.pallas_call(source_kernel, grid=(drops // chunk,), in_specs=[pl.BlockS...  16.1 us
    all_to_all x2, waiting for transfers between devices, filter_group(): spread = lax.all_to_all(projected, 'gx', 1, 1, tiled=True)  15.2 us
    all_to_all x2, starting transfers between devices, filter_group(): gathered = lax.all_to_all(filtered, 'gx', 1, 1, tiled=True)  12.6 us
    ppermute x3, starting transfers between devices, per_device(): lax.ppermute(packed, 'gz', [(i, (i + shift) % gz_count) for i in range(gz...  5.72 us
    dot_general x2, matrix products, filter_group(): projected = jnp.einsum('ay,fyx->fax', dual_full, right_side, precision=HI)  4.84 us
    dot_general x2, matrix products, filter_group(): return jnp.einsum('ya,fax->fyx', basis_full, gathered, precision=HI)  3.75 us
  transfers between devices with their start and end apart: 7, of which 3 were waited for; matrix products, arithmetic and copies ran while one was open for 15% of the time, Pallas kernels for 12%

profile of v4, /device:TPU:1, one launch (start us, length us, event | category | flops | bytes accessed | tf_op | source)
XLA Modules:
  0.0 138.9 jit_solution(7111424279232552409)
XLA Ops:
  0.7 0.8 pad_maximum_fusion.13
  1.5 2.1 %collective-permute-start = (f32[3,4096]{1,0:T(4,128)S(1)}, f32[3,4096]{1,0:T(4,128)S(1)}, u32[]{:S(2)}, u32[]{:S(2)}) collective-permute-start(f32[3,4096]{1,0:T(4,128)S(1)} %pad_maximum_fusion.13), channel_id=1, source_target_pairs={{0,1},{1,2},{2,3},{3,0},{4,5},{5,6},{6,7},{7,4},{8,9},{9,10},{10,1... | collective-permute-start | bytes 147464 | tf_op jit(solution)/shard_map/ppermute | solution.py:107
  3.7 2.5 %collective-permute-start.1 = (f32[3,4096]{1,0:T(4,128)S(1)}, f32[3,4096]{1,0:T(4,128)S(1)}, u32[]{:S(2)}, u32[]{:S(2)}) collective-permute-start(f32[3,4096]{1,0:T(4,128)S(1)} %pad_maximum_fusion.13), channel_id=1, source_target_pairs={{0,2},{1,3},{2,0},{3,1},{4,6},{5,7},{6,4},{7,5},{8,10},{9,11},{10,... | collective-permute-start | bytes 147464 | tf_op jit(solution)/shard_map/ppermute | solution.py:107
  6.1 1.2 collective-permute-start.2
  7.3 2.4 %convolution_bitcast_fusion.5 = f32[2,512,128]{2,1,0:T(8,128)S(1)} fusion(f32[512,512]{1,0:T(8,128)} %param.16, f32[4,1,512,128]{3,2,0,1:T(8,128)} %bitcast.110), kind=kOutput, calls=%fused_computation.11 | convolution fusion | flops 806092800 | bytes 2097152 | tf_op jit(solution)/shard_map/ay,fyx->fax/dot_general | solution.py:153
  9.6 1.2 copy.70
  10.8 13.5 %all-to-all-start = ((f32[2,512,128]{2,0,1:T(2,128)}), f32[2,512,128]{2,0,1:T(2,128)}, u32[]{:S(2)}, u32[]{:S(2)}) async-start(f32[2,512,128]{2,0,1:T(2,128)} %copy.70), calls=%async_computation | async-start | bytes 1048576 | tf_op jit(solution)/shard_map/all_to_all | solution.py:155
  29.0 16.1 %shard_map.91 = f32[512,768]{1,0:T(8,128)S(1)} custom-call(s32[1,16384]{1,0:T(1,128)S(1)} %and_select_fusion.2.row_ref, s32[1,16384]{1,0:T(1,128)S(1)} %get-tuple-element.9.col_ref, f32[6,16384]{1,0:T(8,128)S(1)} %reshape.145.piece_ref), custom_call_target="tpu_custom_call" | custom-call | flops 12884901888 | bytes 1572864 | tf_op jit(solution)/shard_map/pallas_call | solution.py:62
  45.1 1.6 %copy.82 = f32[512,768]{0,1:T(8,128)} copy(f32[512,768]{1,0:T(8,128)S(1)} %shard_map.91) | data formatting | bytes 3145728 | tf_op jit(solution)/shard_map/pallas_call | solution.py:62
  46.7 2.5 %convolution_bitcast_fusion.2 = f32[2,512,128]{1,2,0:T(8,128)S(1)} fusion(f32[512,512]{1,0:T(8,128)S(1)} %copy-done, f32[512,2,3,128]{0,3,2,1:T(8,128)} %bitcast.107, f32[2,1,512,128]{2,3,0,1:T(8,128)S(1)} %copy.102), kind=kOutput, calls=%fused_computation.6 | convolution fusion | flops 806486016 | bytes 3670016 | tf_op jit(solution)/shard_map/ay,fyx->fax/dot_general | solution.py:153
  49.2 1.0 copy.83
  50.2 10.3 %all-to-all-start.2 = ((f32[2,512,128]{2,0,1:T(2,128)}), f32[2,512,128]{2,0,1:T(2,128)S(1)}, u32[]{:S(2)}, u32[]{:S(2)}) async-start(f32[2,512,128]{2,0,1:T(2,128)} %copy.83), calls=%async_computation.2 | async-start | bytes 1048576 | tf_op jit(solution)/shard_map/all_to_all | solution.py:155
  60.9 1.1 copy.132
  62.7 15.2 %all-to-all-done.2 = f32[2,512,128]{2,0,1:T(2,128)S(1)} async-done(((f32[2,512,128]{2,0,1:T(2,128)}), f32[2,512,128]{2,0,1:T(2,128)S(1)}, u32[]{:S(2)}, u32[]{:S(2)}) %all-to-all-start.2) | async-done | bytes 524320 | tf_op jit(solution)/shard_map/all_to_all | solution.py:155
  79.4 0.9 multiply_add_fusion.5
  80.5 1.5 %fusion.12 = f32[2,64,8,256]{3,2,1,0:T(8,128)S(1)} fusion(f32[2,64,8,256]{3,1,2,0:T(8,128)S(1)} %get-tuple-element.31, f32[128,128]{1,0:T(8,128)S(1)} %get-tuple-element.33, f32[128,128]{1,0:T(8,128)S(1)} %get-tuple-element.32, f32[128,128]{1,0:T(8,128)S(1)} %fusion.109), kind=kOutput, calls=%fused_computation.29 | convolution fusion | flops 805502976 | bytes 2293760 | tf_op jit(solution)/shard_map/fkaj,jm->fkam/dot_general | solution.py:165
  82.0 1.5 %fusion.14 = f32[2,64,8,256]{3,2,1,0:T(8,128)S(1)} fusion(f32[2,64,8,256]{3,1,2,0:T(8,128)S(1)} %get-tuple-element.30, f32[128,128]{1,0:T(8,128)S(1)} %get-tuple-element.33, f32[128,128]{1,0:T(8,128)S(1)} %get-tuple-element.32, f32[128,128]{1,0:T(8,128)S(1)} %fusion.109), kind=kOutput, calls=%fused_computation.31 | convolution fusion | flops 805502976 | bytes 2293760 | tf_op jit(solution)/shard_map/fkaj,jm->fkam/dot_general | solution.py:165
  84.2 1.2 fusion.10
  85.3 0.8 fusion.39
  86.1 0.8 fusion.5
  87.2 1.2 copy.78
  88.4 6.3 %all-to-all-start.1 = ((f32[2,512,128]{2,0,1:T(2,128)}), f32[2,512,128]{2,0,1:T(2,128)S(1)}, u32[]{:S(2)}, u32[]{:S(2)}) async-start(f32[2,512,128]{2,0,1:T(2,128)} %copy.78), calls=%async_computation.1 | async-start | bytes 1048576 | tf_op jit(solution)/shard_map/all_to_all | solution.py:198
  94.8 1.2 fusion.8
  96.0 0.8 fusion.32
  96.8 0.8 fusion.3
  97.9 1.2 copy.91
  99.1 13.0 %all-to-all-done.1 = f32[2,512,128]{2,0,1:T(2,128)S(1)} async-done(((f32[2,512,128]{2,0,1:T(2,128)}), f32[2,512,128]{2,0,1:T(2,128)S(1)}, u32[]{:S(2)}, u32[]{:S(2)}) %all-to-all-start.1) | async-done | bytes 524320 | tf_op jit(solution)/shard_map/all_to_all | solution.py:198
  112.0 6.3 %all-to-all-start.3 = ((f32[2,512,128]{2,0,1:T(2,128)}), f32[2,512,128]{2,0,1:T(2,128)S(1)}, u32[]{:S(2)}, u32[]{:S(2)}) async-start(f32[2,512,128]{2,0,1:T(2,128)} %copy.91), calls=%async_computation.3 | async-start | bytes 1048576 | tf_op jit(solution)/shard_map/all_to_all | solution.py:198
  118.3 1.9 %convolution_bitcast_fusion.3 = f32[2,512,128]{1,2,0:T(8,128)S(1)} fusion(f32[512,512]{1,0:T(8,128)S(1)} %copy-done.1, f32[2,512,128]{2,0,1:T(2,128)S(1)} %all-to-all-done.1), kind=kOutput, calls=%fused_computation.7 | convolution fusion | flops 806092800 | bytes 2097152 | tf_op jit(solution)/shard_map/ya,fax->fyx/dot_general | solution.py:199
  120.2 15.4 %all-to-all-done.3 = f32[2,512,128]{2,0,1:T(2,128)S(1)} async-done(((f32[2,512,128]{2,0,1:T(2,128)}), f32[2,512,128]{2,0,1:T(2,128)S(1)}, u32[]{:S(2)}, u32[]{:S(2)}) %all-to-all-start.3) | async-done | bytes 524320 | tf_op jit(solution)/shard_map/all_to_all | solution.py:198
  135.7 1.9 %convolution_bitcast_fusion = f32[2,512,128]{1,2,0:T(8,128)S(1)} fusion(f32[512,512]{1,0:T(8,128)S(1)} %copy-done.1, f32[2,512,128]{2,0,1:T(2,128)S(1)} %all-to-all-done.3), kind=kOutput, calls=%fused_computation.2 | convolution fusion | flops 806092800 | bytes 2097152 | tf_op jit(solution)/shard_map/ya,fax->fyx/dot_general | solution.py:199
  137.6 1.3 copy.93
  (45 shorter events, 8.8 us)
Async XLA Ops:
  1.5 25.3 %collective-permute-start = (f32[3,4096]{1,0:T(4,128)S(1)}, f32[3,4096]{1,0:T(4,128)S(1)}, u32[]{:S(2)}, u32[]{:S(2)}) collective-permute-start(f32[3,4096]{1,0:T(4,128)S(1)} %pad_maximum_fusion.13), channel_id=1, source_target_pairs={{0,1},{1,2},{2,3},{3,0},{4,5},{5,6},{6,7},{7,4},{8,9},{9,10},{10,1... | collective-permute-start | bytes 147464 | tf_op jit(solution)/shard_map/ppermute | solution.py:107
  3.7 23.2 %collective-permute-start.1 = (f32[3,4096]{1,0:T(4,128)S(1)}, f32[3,4096]{1,0:T(4,128)S(1)}, u32[]{:S(2)}, u32[]{:S(2)}) collective-permute-start(f32[3,4096]{1,0:T(4,128)S(1)} %pad_maximum_fusion.13), channel_id=1, source_target_pairs={{0,2},{1,3},{2,0},{3,1},{4,6},{5,7},{6,4},{7,5},{8,10},{9,11},{10,... | collective-permute-start | bytes 147464 | tf_op jit(solution)/shard_map/ppermute | solution.py:107
  6.1 20.7 %collective-permute-start.2 = (f32[3,4096]{1,0:T(4,128)S(1)}, f32[3,4096]{1,0:T(4,128)S(1)}, u32[]{:S(2)}, u32[]{:S(2)}) collective-permute-start(f32[3,4096]{1,0:T(4,128)S(1)} %pad_maximum_fusion.13), channel_id=1, source_target_pairs={{0,3},{1,0},{2,1},{3,2},{4,7},{5,4},{6,5},{7,6},{8,11},{9,8},{10,9... | collective-permute-start | bytes 147464 | tf_op jit(solution)/shard_map/ppermute | solution.py:107
  9.6 15.5 %copy-start.2 = (f32[4,1,512,128]{3,2,1,0:T(8,128)S(1)}, f32[4,1,512,128]{3,2,1,0:T(8,128)}, u32[]{:S(2)}) copy-start(f32[4,1,512,128]{3,2,1,0:T(8,128)} %param.9) | copy-start | bytes 3145732
  10.8 16.0 %copy-start.3 = (f32[2,4096]{1,0:T(2,128)S(1)}, f32[2,4096]{1,0:T(2,128)}, u32[]{:S(2)}) copy-start(f32[2,4096]{1,0:T(2,128)} %param.12) | copy-start | bytes 98308
  10.8 39.4 %all-to-all-start = ((f32[2,512,128]{2,0,1:T(2,128)}), f32[2,512,128]{2,0,1:T(2,128)}, u32[]{:S(2)}, u32[]{:S(2)}) async-start(f32[2,512,128]{2,0,1:T(2,128)} %copy.70), calls=%async_computation | async-start | bytes 1048576 | tf_op jit(solution)/shard_map/all_to_all | solution.py:155
  45.0 1.6 %copy-start = (f32[512,512]{1,0:T(8,128)S(1)}, f32[512,512]{1,0:T(8,128)}, u32[]{:S(2)}) copy-start(f32[512,512]{1,0:T(8,128)} %param.16) | copy-start | bytes 3145732
  49.2 11.4 %copy-start.4 = (f32[4]{0:T(128)S(1)}, f32[4]{0:T(128)}, u32[]{:S(2)}) copy-start(f32[4]{0:T(128)} %param.13) | copy-start | bytes 52
  50.2 27.6 %all-to-all-start.2 = ((f32[2,512,128]{2,0,1:T(2,128)}), f32[2,512,128]{2,0,1:T(2,128)S(1)}, u32[]{:S(2)}, u32[]{:S(2)}) async-start(f32[2,512,128]{2,0,1:T(2,128)} %copy.83), calls=%async_computation.2 | async-start | bytes 1048576 | tf_op jit(solution)/shard_map/all_to_all | solution.py:155
  88.4 23.6 %all-to-all-start.1 = ((f32[2,512,128]{2,0,1:T(2,128)}), f32[2,512,128]{2,0,1:T(2,128)S(1)}, u32[]{:S(2)}, u32[]{:S(2)}) async-start(f32[2,512,128]{2,0,1:T(2,128)} %copy.78), calls=%async_computation.1 | async-start | bytes 1048576 | tf_op jit(solution)/shard_map/all_to_all | solution.py:198
  97.5 20.8 %copy-start.1 = (f32[512,512]{1,0:T(8,128)S(1)}, f32[512,512]{1,0:T(8,128)}, u32[]{:S(2)}) copy-start(f32[512,512]{1,0:T(8,128)} %param.15) | copy-start | bytes 3145732
  112.0 23.6 %all-to-all-start.3 = ((f32[2,512,128]{2,0,1:T(2,128)}), f32[2,512,128]{2,0,1:T(2,128)S(1)}, u32[]{:S(2)}, u32[]{:S(2)}) async-start(f32[2,512,128]{2,0,1:T(2,128)} %copy.91), calls=%async_computation.3 | async-start | bytes 1048576 | tf_op jit(solution)/shard_map/all_to_all | solution.py:198

commit v5 on v3

--- a/solution.py
+++ b/solution.py
@@ -7,7 +7,7 @@
 from jax.experimental.pallas import tpu as pltpu
 from jax.sharding import PartitionSpec as P
 
-HI = lax.Precision.HIGHEST
+HI = lax.Precision.HIGH
 
 
 def phase(numer, length):

time: 129 us -> 122 us (0.946)
  matrix products: 16.2 us -> 9.63 us
    dot_general x1, matrix products: 3.48 us -> 1.86 us  [per_device(): jnp.einsum('ya,fax->fyx', identity + basis_part, gathered, precision=HI)]
where the time goes in v5:
time: 122 us
  blocking collectives  34.5 us (28%)
  waiting for transfers between devices  27.1 us (22%)
  starting transfers between devices  18.3 us (15%)
  Pallas kernels  16.1 us (13%)
  matrix products  9.63 us (8%)
  local copies, waits for them, and re-layouts  9.08 us (7%)
  other arithmetic  6.29 us (5%)
    all_to_all x1, blocking collectives, per_device(): gathered = lax.all_to_all(filtered, 'gx', 1, 1, tiled=True)  34.5 us
    all_to_all x1, waiting for transfers between devices, per_device(): spread = lax.all_to_all(projected, 'gx', 1, 1, tiled=True)  26.2 us
    pallas_call x1, Pallas kernels, drop_source(): pl.pallas_call(source_kernel, grid=(drops // chunk,), in_specs=[pl.BlockS...  16.1 us
    all_to_all x1, starting transfers between devices, per_device(): spread = lax.all_to_all(projected, 'gx', 1, 1, tiled=True)  13.8 us
    ppermute x3, starting transfers between devices, per_device(): lax.ppermute(packed, 'gz', [(i, (i + shift) % gz_count) for i in range(gz...  4.51 us
  transfers between devices with their start and end apart: 4, of which 3 were waited for; matrix products, arithmetic and copies ran while one was open for 4% of the time, Pallas kernels for 0%

profile of v5, /device:TPU:1, one launch (start us, length us, event | category | flops | bytes accessed | tf_op | source)
XLA Modules:
  0.0 121.9 jit_solution(8626420302805076476)
XLA Ops:
  0.0 0.7 add_convert_fusion
  0.7 0.8 pad_maximum_fusion.13
  1.5 3.4 %collective-permute-start.2 = (f32[3,4096]{1,0:T(4,128)S(1)}, f32[3,4096]{1,0:T(4,128)S(1)}, u32[]{:S(2)}, u32[]{:S(2)}) collective-permute-start(f32[3,4096]{1,0:T(4,128)S(1)} %pad_maximum_fusion.13), channel_id=1, source_target_pairs={{0,3},{1,0},{2,1},{3,2},{4,7},{5,4},{6,5},{7,6},{8,11},{9,8},{10,9... | collective-permute-start | bytes 147464 | tf_op jit(solution)/shard_map/ppermute | solution.py:107
  4.9 0.5 collective-permute-start.1
  5.5 0.6 collective-permute-start
  6.1 1.3 %fusion.109 = (f32[2,1,512,128]{3,2,1,0:T(8,128)S(1)}, f32[2,1,512,128]{3,2,1,0:T(8,128)S(1)}) fusion(f32[4,1,512,128]{3,2,1,0:T(8,128)} %param.9), kind=kLoop, calls=%fused_computation.165 | loop fusion | bytes 2097152 | tf_op jit(solution)/shard_map/slice | solution.py:116
  7.3 1.0 copy.62
  8.3 1.0 copy.63
  9.6 0.7 collective-permute-done
  10.3 0.5 compare_reduce_fusion
  10.8 0.3 and_select_fusion.1
  11.1 0.3 and_select_fusion.2.row_ref
  12.4 16.1 %shard_map.91 = f32[512,768]{1,0:T(8,128)S(1)} custom-call(s32[1,16384]{1,0:T(1,128)S(1)} %and_select_fusion.2.row_ref, s32[1,16384]{1,0:T(1,128)S(1)} %get-tuple-element.9.col_ref, f32[6,16384]{1,0:T(8,128)S(1)} %reshape.136.piece_ref), custom_call_target="tpu_custom_call" | custom-call | flops 12884901888 | bytes 1572864 | tf_op jit(solution)/shard_map/pallas_call | solution.py:62
  28.4 0.5 copy.41
  28.9 1.4 %fusion.30 = f32[2,1,512,128]{2,3,0,1:T(8,128)S(1)} fusion(f32[2,1,512,128]{2,3,0,1:T(8,128)} %copy.63, f32[512,2,3,128]{0,3,2,1:T(8,128)S(1)} %bitcast.90), kind=kLoop, calls=%fused_computation.49 | loop fusion | flops 393216 | bytes 2621440 | tf_op jit(solution)/shard_map/add | solution.py:116
  30.5 1.0 convolution_bitcast_fusion.2
  31.5 1.3 %copy.45 = f32[4,512,128]{2,0,1:T(4,128)} copy(f32[4,512,128]{1,2,0:T(8,128)S(1)} %convolution_bitcast_fusion.2) | data formatting | bytes 2097152 | tf_op jit(solution)/shard_map/ay,fyx->fax/transpose | solution.py:118
  32.8 13.8 %all-to-all-start = ((f32[4,512,128]{2,0,1:T(4,128)}), f32[4,512,128]{2,0,1:T(4,128)S(1)}, u32[]{:S(2)}, u32[]{:S(2)}) async-start(f32[4,512,128]{2,0,1:T(4,128)} %copy.45), calls=%async_computation | async-start | bytes 2097152 | tf_op jit(solution)/shard_map/all_to_all | solution.py:120
  47.2 0.8 dynamic_slice.3
  48.9 26.2 %all-to-all-done = f32[4,512,128]{2,0,1:T(4,128)S(1)} async-done(((f32[4,512,128]{2,0,1:T(4,128)}), f32[4,512,128]{2,0,1:T(4,128)S(1)}, u32[]{:S(2)}, u32[]{:S(2)}) %all-to-all-start) | async-done | bytes 1048608 | tf_op jit(solution)/shard_map/all_to_all | solution.py:120
  75.2 0.7 convolution_bitcast_fusion.1
  75.9 1.0 multiply_add_fusion.2
  77.1 2.0 %fusion.2 = f32[4,64,8,256]{3,2,1,0:T(8,128)S(1)} fusion(f32[4,64,8,256]{3,1,2,0:T(8,128)S(1)} %pad_maximum_fusion, f32[128,128]{1,0:T(8,128)S(1)} %get-tuple-element.25, f32[128,128]{1,0:T(8,128)S(1)} %get-tuple-element.24, f32[128,128]{1,0:T(8,128)S(1)} %fusion.80), kind=kOutput, calls=%fused_computation.4 | convolution fusion | flops 805502976 | bytes 4390912 | tf_op jit(solution)/shard_map/fkaj,jm->fkam/dot_general | solution.py:139
  79.1 0.6 multiply_subtract_fusion.1
  79.8 1.5 %fusion = f32[4,64,8,256]{3,1,2,0:T(8,128)S(1)} fusion(f32[4,64,8,256]{3,2,1,0:T(8,128)S(1)} %pad_maximum_fusion.1, f32[128,128]{1,0:T(8,128)S(1)} %get-tuple-element.25, f32[128,128]{1,0:T(8,128)S(1)} %fusion.80, f32[128,128]{1,0:T(8,128)S(1)} %get-tuple-element.24), kind=kOutput, calls=%fused_computation.2 | convolution fusion | flops 805502976 | bytes 4390912 | tf_op jit(solution)/shard_map/fkam,mj->fkaj/dot_general | solution.py:167
  81.3 0.7 fusion.18
  82.1 0.8 fusion.5
  82.9 0.6 copy.81
  83.5 0.7 copy.53
  84.2 34.5 %all_to_all.10 = f32[4,512,128]{2,0,1:T(4,128)S(1)} all-to-all(f32[4,512,128]{2,0,1:T(4,128)S(1)} %copy.53), channel_id=1, replica_groups=mesh['gx'=64,'gz'=4] {'gx'}, dimensions={1} | all-to-all | bytes 2097152 | tf_op jit(solution)/shard_map/all_to_all | solution.py:178
  118.8 1.9 %convolution_bitcast_fusion = f32[4,1,512,128]{2,3,0,1:T(8,128)S(1)} fusion(f32[512,512]{1,0:T(8,128)S(1)} %copy-done.2, f32[4,512,128]{2,0,1:T(4,128)S(1)} %all_to_all.10), kind=kOutput, calls=%fused_computation.10 | convolution fusion | flops 806092800 | bytes 3145728 | tf_op jit(solution)/shard_map/ya,fax->fyx/dot_general | solution.py:179
  120.6 1.3 %copy.55 = f32[4,1,512,128]{3,2,1,0:T(8,128)} copy(f32[4,1,512,128]{2,3,0,1:T(8,128)S(1)} %convolution_bitcast_fusion) | data formatting | bytes 2097152 | tf_op jit(solution)/shard_map/broadcast_in_dim | solution.py:180
  (26 shorter events, 2.6 us)
Async XLA Ops:
  1.5 8.7 %copy-start.3 = (f32[2,4096]{1,0:T(2,128)S(1)}, f32[2,4096]{1,0:T(2,128)}, u32[]{:S(2)}) copy-start(f32[2,4096]{1,0:T(2,128)} %param.12) | copy-start | bytes 98308
  1.5 7.8 %collective-permute-start.2 = (f32[3,4096]{1,0:T(4,128)S(1)}, f32[3,4096]{1,0:T(4,128)S(1)}, u32[]{:S(2)}, u32[]{:S(2)}) collective-permute-start(f32[3,4096]{1,0:T(4,128)S(1)} %pad_maximum_fusion.13), channel_id=1, source_target_pairs={{0,3},{1,0},{2,1},{3,2},{4,7},{5,4},{6,5},{7,6},{8,11},{9,8},{10,9... | collective-permute-start | bytes 147464 | tf_op jit(solution)/shard_map/ppermute | solution.py:107
  4.9 4.7 %collective-permute-start.1 = (f32[3,4096]{1,0:T(4,128)S(1)}, f32[3,4096]{1,0:T(4,128)S(1)}, u32[]{:S(2)}, u32[]{:S(2)}) collective-permute-start(f32[3,4096]{1,0:T(4,128)S(1)} %pad_maximum_fusion.13), channel_id=1, source_target_pairs={{0,2},{1,3},{2,0},{3,1},{4,6},{5,7},{6,4},{7,5},{8,10},{9,11},{10,... | collective-permute-start | bytes 147464 | tf_op jit(solution)/shard_map/ppermute | solution.py:107
  5.5 4.8 %collective-permute-start = (f32[3,4096]{1,0:T(4,128)S(1)}, f32[3,4096]{1,0:T(4,128)S(1)}, u32[]{:S(2)}, u32[]{:S(2)}) collective-permute-start(f32[3,4096]{1,0:T(4,128)S(1)} %pad_maximum_fusion.13), channel_id=1, source_target_pairs={{0,1},{1,2},{2,3},{3,0},{4,5},{5,6},{6,7},{7,4},{8,9},{9,10},{10,1... | collective-permute-start | bytes 147464 | tf_op jit(solution)/shard_map/ppermute | solution.py:107
  28.9 1.4 %copy-start = (f32[2,1,512,128]{2,3,0,1:T(8,128)S(1)}, f32[2,1,512,128]{2,3,0,1:T(8,128)}, u32[]{:S(2)}) copy-start(f32[2,1,512,128]{2,3,0,1:T(8,128)} %copy.62) | copy-start | bytes 1572868
  28.9 1.5 %copy-start.1 = (f32[512,512]{1,0:T(8,128)S(1)}, f32[512,512]{1,0:T(8,128)}, u32[]{:S(2)}) copy-start(f32[512,512]{1,0:T(8,128)} %param.16) | copy-start | bytes 3145732
  32.8 42.3 %all-to-all-start = ((f32[4,512,128]{2,0,1:T(4,128)}), f32[4,512,128]{2,0,1:T(4,128)S(1)}, u32[]{:S(2)}, u32[]{:S(2)}) async-start(f32[4,512,128]{2,0,1:T(4,128)} %copy.45), calls=%async_computation | async-start | bytes 2097152 | tf_op jit(solution)/shard_map/all_to_all | solution.py:120
  77.1 2.1 %copy-start.4 = (f32[4]{0:T(128)S(1)}, f32[4]{0:T(128)}, u32[]{:S(2)}) copy-start(f32[4]{0:T(128)} %param.13) | copy-start | bytes 52
  83.5 35.2 %copy-start.2 = (f32[512,512]{1,0:T(8,128)S(1)}, f32[512,512]{1,0:T(8,128)}, u32[]{:S(2)}) copy-start(f32[512,512]{1,0:T(8,128)} %param.15) | copy-start | bytes 3145732

commit v6 on v5

--- a/solution.py
+++ b/solution.py
@@ -15,7 +15,7 @@
     return jnp.cos(angle), jnp.sin(angle)
 
 
-PIECES = 3
+PIECES = 2
 CHUNK = 2048
 
 

time: 122 us -> 121 us (level)
  Pallas kernels: 16.1 us -> 11 us
  local copies, waits for them, and re-layouts: 9.08 us -> 12.1 us
  waiting for transfers between devices: 27.1 us -> 28.7 us
  other arithmetic: 6.29 us -> 4.95 us
    pallas_call x1, Pallas kernels: 16.1 us -> 11 us  [drop_source(): pl.pallas_call(source_kernel, grid=(drops // chunk,), in_specs=[pl.BlockS...]
    slice x0 -> x1, local copies, waits for them, and re-layouts: none -> 1.6 us  [drop_source(): total = total + summed[:, :, p]]
    ppermute x3, waiting for transfers between devices: 0.92 us -> 2.49 us  [per_device(): lax.ppermute(packed, 'gz', [(i, (i + shift) % gz_count) for i in range(gz...]
    unnamed x12, local copies, waits for them, and re-layouts: 2.16 us -> 3.39 us
    add x1, other arithmetic: 1.37 us -> 0.15 us  [per_device(): field[2:] + source[:, None]]
  transfers between devices with their start and end apart: 4 -> 4, of which waited for: 3 -> 3; matrix products, arithmetic and copies ran while one was open for 4% -> 3% of each run, Pallas kernels for 0% -> 0%
where the time goes in v6:
time: 121 us; the launch traced here: 120 us
  blocking collectives  34.5 us (29%)
  waiting for transfers between devices  28.7 us (24%)
  starting transfers between devices  18.3 us (15%)
  local copies, waits for them, and re-layouts  12.1 us (10%)
  Pallas kernels  11 us (9%)
  matrix products  9.63 us (8%)
  other arithmetic  4.95 us (4%)
    all_to_all x1, blocking collectives, per_device(): gathered = lax.all_to_all(filtered, 'gx', 1, 1, tiled=True)  34.5 us
    all_to_all x1, waiting for transfers between devices, per_device(): spread = lax.all_to_all(projected, 'gx', 1, 1, tiled=True)  26.2 us
    all_to_all x1, starting transfers between devices, per_device(): spread = lax.all_to_all(projected, 'gx', 1, 1, tiled=True)  13.8 us
    pallas_call x1, Pallas kernels, drop_source(): pl.pallas_call(source_kernel, grid=(drops // chunk,), in_specs=[pl.BlockS...  11 us
    ppermute x3, starting transfers between devices, per_device(): lax.ppermute(packed, 'gz', [(i, (i + shift) % gz_count) for i in range(gz...  4.51 us
    unnamed x12, local copies, waits for them, and re-layouts  3.39 us
    ppermute x3, waiting for transfers between devices, per_device(): lax.ppermute(packed, 'gz', [(i, (i + shift) % gz_count) for i in range(gz...  2.49 us
  transfers between devices with their start and end apart: 4, of which 3 were waited for; matrix products, arithmetic and copies ran while one was open for 3% of the time, Pallas kernels for 0%

profile of v6, /device:TPU:1, one launch (start us, length us, event | category | flops | bytes accessed | tf_op | source)
XLA Modules:
  0.0 120.2 jit_solution(4962739992040986085)
XLA Ops:
  0.0 0.7 add_convert_fusion
  0.7 0.8 pad_maximum_fusion.13
  1.5 3.4 %collective-permute-start.2 = (f32[3,4096]{1,0:T(4,128)S(1)}, f32[3,4096]{1,0:T(4,128)S(1)}, u32[]{:S(2)}, u32[]{:S(2)}) collective-permute-start(f32[3,4096]{1,0:T(4,128)S(1)} %pad_maximum_fusion.13), channel_id=1, source_target_pairs={{0,3},{1,0},{2,1},{3,2},{4,7},{5,4},{6,5},{7,6},{8,11},{9,8},{10,9... | collective-permute-start | bytes 147464 | tf_op jit(solution)/shard_map/ppermute | solution.py:107
  4.9 0.5 collective-permute-start.1
  5.5 0.6 collective-permute-start
  6.1 1.3 %fusion.105 = (f32[2,1,512,128]{3,2,1,0:T(8,128)S(1)}, f32[2,1,512,128]{3,2,1,0:T(8,128)S(1)}) fusion(f32[4,1,512,128]{3,2,1,0:T(8,128)} %param.9), kind=kLoop, calls=%fused_computation.157 | loop fusion | bytes 2097152 | tf_op jit(solution)/shard_map/slice | solution.py:116
  7.8 1.8 %collective-permute-done.1 = f32[3,4096]{1,0:T(4,128)S(1)} collective-permute-done((f32[3,4096]{1,0:T(4,128)S(1)}, f32[3,4096]{1,0:T(4,128)S(1)}, u32[]{:S(2)}, u32[]{:S(2)}) %collective-permute-start.1) | collective-permute-done | bytes 49184 | tf_op jit(solution)/shard_map/ppermute | solution.py:107
  9.6 0.7 collective-permute-done
  10.3 0.5 compare_reduce_fusion
  12.2 11.0 %shard_map.91 = f32[512,512]{1,0:T(8,128)S(1)} custom-call(s32[1,16384]{1,0:T(1,128)S(1)} %and_select_fusion.2.row_ref, s32[1,16384]{1,0:T(1,128)S(1)} %get-tuple-element.9.col_ref, f32[4,16384]{1,0:T(4,128)S(1)} %reshape.135.piece_ref), custom_call_target="tpu_custom_call" | custom-call | flops 8589934592 | bytes 1048576 | tf_op jit(solution)/shard_map/pallas_call | solution.py:62
  23.3 0.7 reshape.136
  24.0 1.6 %fusion.106 = (f32[512,2,1,128]{3,2,1,0:T(1,128)}, f32[512,2,1,128]{3,2,1,0:T(1,128)S(1)}) fusion(f32[512,2,2,128]{3,2,1,0:T(2,128)S(1)} %reshape.136), kind=kLoop, calls=%fused_computation.158 | loop fusion | bytes 2097152 | tf_op jit(solution)/shard_map/slice | solution.py:80
  25.6 1.2 %copy.60 = f32[512,2,1,128]{0,3,1,2:T(8,128)S(1)} copy(f32[512,2,1,128]{3,2,1,0:T(1,128)} %get-tuple-element.17) | data formatting | bytes 1048576
  26.8 0.7 copy.59
  27.7 1.1 copy-done
  28.7 1.0 convolution_bitcast_fusion.2
  29.7 1.3 %copy.40 = f32[4,512,128]{2,0,1:T(4,128)} copy(f32[4,512,128]{1,2,0:T(8,128)S(1)} %convolution_bitcast_fusion.2) | data formatting | bytes 2097152 | tf_op jit(solution)/shard_map/ay,fyx->fax/transpose | solution.py:118
  31.1 13.8 %all-to-all-start = ((f32[4,512,128]{2,0,1:T(4,128)}), f32[4,512,128]{2,0,1:T(4,128)S(1)}, u32[]{:S(2)}, u32[]{:S(2)}) async-start(f32[4,512,128]{2,0,1:T(4,128)} %copy.40), calls=%async_computation | async-start | bytes 2097152 | tf_op jit(solution)/shard_map/all_to_all | solution.py:120
  45.5 0.8 dynamic_slice.3
  47.2 26.2 %all-to-all-done = f32[4,512,128]{2,0,1:T(4,128)S(1)} async-done(((f32[4,512,128]{2,0,1:T(4,128)}), f32[4,512,128]{2,0,1:T(4,128)S(1)}, u32[]{:S(2)}, u32[]{:S(2)}) %all-to-all-start) | async-done | bytes 1048608 | tf_op jit(solution)/shard_map/all_to_all | solution.py:120
  73.4 0.7 convolution_bitcast_fusion.1
  74.2 1.0 multiply_add_fusion.2
  75.3 2.0 %fusion.2 = f32[4,64,8,256]{3,2,1,0:T(8,128)S(1)} fusion(f32[4,64,8,256]{3,1,2,0:T(8,128)S(1)} %pad_maximum_fusion, f32[128,128]{1,0:T(8,128)S(1)} %get-tuple-element.25, f32[128,128]{1,0:T(8,128)S(1)} %get-tuple-element.24, f32[128,128]{1,0:T(8,128)S(1)} %fusion.76), kind=kOutput, calls=%fused_computation.4 | convolution fusion | flops 805502976 | bytes 4390912 | tf_op jit(solution)/shard_map/fkaj,jm->fkam/dot_general | solution.py:139
  77.4 0.6 multiply_subtract_fusion.1
  78.1 1.5 %fusion = f32[4,64,8,256]{3,1,2,0:T(8,128)S(1)} fusion(f32[4,64,8,256]{3,2,1,0:T(8,128)S(1)} %pad_maximum_fusion.1, f32[128,128]{1,0:T(8,128)S(1)} %get-tuple-element.25, f32[128,128]{1,0:T(8,128)S(1)} %fusion.76, f32[128,128]{1,0:T(8,128)S(1)} %get-tuple-element.24), kind=kOutput, calls=%fused_computation.2 | convolution fusion | flops 805502976 | bytes 4390912 | tf_op jit(solution)/shard_map/fkam,mj->fkaj/dot_general | solution.py:167
  79.6 0.7 fusion.18
  80.4 0.8 fusion.5
  81.2 0.6 copy.75
  81.8 0.7 copy.48
  82.5 34.5 %all_to_all.10 = f32[4,512,128]{2,0,1:T(4,128)S(1)} all-to-all(f32[4,512,128]{2,0,1:T(4,128)S(1)} %copy.48), channel_id=1, replica_groups=mesh['gx'=64,'gz'=4] {'gx'}, dimensions={1} | all-to-all | bytes 2097152 | tf_op jit(solution)/shard_map/all_to_all | solution.py:178
  117.0 1.9 %convolution_bitcast_fusion = f32[4,1,512,128]{2,3,0,1:T(8,128)S(1)} fusion(f32[512,512]{1,0:T(8,128)S(1)} %copy-done.1, f32[4,512,128]{2,0,1:T(4,128)S(1)} %all_to_all.10), kind=kOutput, calls=%fused_computation.10 | convolution fusion | flops 806092800 | bytes 3145728 | tf_op jit(solution)/shard_map/ya,fax->fyx/dot_general | solution.py:179
  118.9 1.3 %copy.50 = f32[4,1,512,128]{3,2,1,0:T(8,128)} copy(f32[4,1,512,128]{2,3,0,1:T(8,128)S(1)} %convolution_bitcast_fusion) | data formatting | bytes 2097152 | tf_op jit(solution)/shard_map/broadcast_in_dim | solution.py:180
  (27 shorter events, 3.2 us)
Async XLA Ops:
  1.5 8.7 %copy-start.2 = (f32[2,4096]{1,0:T(2,128)S(1)}, f32[2,4096]{1,0:T(2,128)}, u32[]{:S(2)}) copy-start(f32[2,4096]{1,0:T(2,128)} %param.12) | copy-start | bytes 98308
  1.5 6.2 %collective-permute-start.2 = (f32[3,4096]{1,0:T(4,128)S(1)}, f32[3,4096]{1,0:T(4,128)S(1)}, u32[]{:S(2)}, u32[]{:S(2)}) collective-permute-start(f32[3,4096]{1,0:T(4,128)S(1)} %pad_maximum_fusion.13), channel_id=1, source_target_pairs={{0,3},{1,0},{2,1},{3,2},{4,7},{5,4},{6,5},{7,6},{8,11},{9,8},{10,9... | collective-permute-start | bytes 147464 | tf_op jit(solution)/shard_map/ppermute | solution.py:107
  4.9 4.7 %collective-permute-start.1 = (f32[3,4096]{1,0:T(4,128)S(1)}, f32[3,4096]{1,0:T(4,128)S(1)}, u32[]{:S(2)}, u32[]{:S(2)}) collective-permute-start(f32[3,4096]{1,0:T(4,128)S(1)} %pad_maximum_fusion.13), channel_id=1, source_target_pairs={{0,2},{1,3},{2,0},{3,1},{4,6},{5,7},{6,4},{7,5},{8,10},{9,11},{10,... | collective-permute-start | bytes 147464 | tf_op jit(solution)/shard_map/ppermute | solution.py:107
  5.5 4.8 %collective-permute-start = (f32[3,4096]{1,0:T(4,128)S(1)}, f32[3,4096]{1,0:T(4,128)S(1)}, u32[]{:S(2)}, u32[]{:S(2)}) collective-permute-start(f32[3,4096]{1,0:T(4,128)S(1)} %pad_maximum_fusion.13), channel_id=1, source_target_pairs={{0,1},{1,2},{2,3},{3,0},{4,5},{5,6},{6,7},{7,4},{8,9},{9,10},{10,1... | collective-permute-start | bytes 147464 | tf_op jit(solution)/shard_map/ppermute | solution.py:107
  27.5 1.2 %copy-start = (f32[512,512]{1,0:T(8,128)S(1)}, f32[512,512]{1,0:T(8,128)}, u32[]{:S(2)}) copy-start(f32[512,512]{1,0:T(8,128)} %param.16) | copy-start | bytes 3145732
  31.1 42.3 %all-to-all-start = ((f32[4,512,128]{2,0,1:T(4,128)}), f32[4,512,128]{2,0,1:T(4,128)S(1)}, u32[]{:S(2)}, u32[]{:S(2)}) async-start(f32[4,512,128]{2,0,1:T(4,128)} %copy.40), calls=%async_computation | async-start | bytes 2097152 | tf_op jit(solution)/shard_map/all_to_all | solution.py:120
  75.3 2.1 %copy-start.3 = (f32[4]{0:T(128)S(1)}, f32[4]{0:T(128)}, u32[]{:S(2)}) copy-start(f32[4]{0:T(128)} %param.13) | copy-start | bytes 52
  81.8 35.2 %copy-start.1 = (f32[512,512]{1,0:T(8,128)S(1)}, f32[512,512]{1,0:T(8,128)}, u32[]{:S(2)}) copy-start(f32[512,512]{1,0:T(8,128)} %param.15) | copy-start | bytes 3145732

commit v7 on v6

--- a/solution.py
+++ b/solution.py
@@ -113,11 +113,13 @@
     planes = keys // plane_cells
     rates = jnp.where((planes == plane_here)[None, :], packed[1:], 0.0)
     source = drop_source(cells, rates, row_count, slab_width)
-    right_side = jnp.concatenate([field[:2], field[2:] + source[:, None]], axis=0)[:, 0]
     identity = jnp.eye(row_count, dtype=jnp.float32)
-    projected = jnp.einsum("ay,fyx->fax", identity + dual_part, right_side, precision=HI)
-
-    spread = lax.all_to_all(projected, "gx", 1, 1, tiled=True)
+    dual_full = identity + dual_part
+    calm = jnp.einsum("ay,fyx->fax", dual_full, field[:2, 0], precision=HI)
+    calm = lax.all_to_all(calm, "gx", 1, 1, tiled=True)
+    fed = jnp.einsum("ay,fyx->fax", dual_full, field[2:, 0] + source, precision=HI)
+    fed = lax.all_to_all(fed, "gx", 1, 1, tiled=True)
+    spread = jnp.concatenate([calm, fed], axis=0)
     spread = spread.reshape(field_count, gx_count, rows_here, slab_width)
 
     d_index = jnp.arange(gx_count, dtype=jnp.int32)

time: 121 us -> 115 us (0.950)
  waiting for transfers between devices: 28.7 us -> 14 us
  starting transfers between devices: 18.3 us -> 28.1 us
  local copies, waits for them, and re-layouts: 12.1 us -> 9.08 us
  matrix products: 9.63 us -> 11.7 us
    all_to_all x1 -> x2, waiting for transfers between devices: 26.2 us -> 14 us  [the longest x1 13.9 us: per_device(): fed = lax.all_to_all(fed, 'gx', 1, 1, tiled=True)]
    all_to_all x1 -> x2, starting transfers between devices: 13.8 us -> 23.6 us  [the longest x1 13.4 us: per_device(): calm = lax.all_to_all(calm, 'gx', 1, 1, tiled=True)]
    unnamed x12 -> x10, local copies, waits for them, and re-layouts: 3.39 us -> 0.49 us
    ppermute x3, waiting for transfers between devices: 2.49 us -> 0.01 us  [per_device(): lax.ppermute(packed, 'gz', [(i, (i + shift) % gz_count) for i in range(gz...]
    slice x2 -> x1, local copies, waits for them, and re-layouts: 2.88 us -> 0.81 us  [drop_source(): total = summed[:, :, 0]]
    dot_general x1 -> x2, matrix products: 1.02 us -> 3.04 us  [the longest x1 1.95 us: per_device(): calm = jnp.einsum('ay,fyx->fax', dual_full, field[:2, 0], precision=HI)]
  transfers between devices with their start and end apart: 4 -> 5, of which waited for: 3 -> 2; matrix products, arithmetic and copies ran while one was open for 3% -> 10% of each run, Pallas kernels for 0% -> 10%
where the time goes in v7:
time: 115 us; the launch traced here: 114 us
  blocking collectives  34.6 us (30%)
  starting transfers between devices  28.1 us (24%)
  waiting for transfers between devices  14 us (12%)
  matrix products  11.7 us (10%)
  Pallas kernels  11 us (10%)
  local copies, waits for them, and re-layouts  9.08 us (8%)
  other arithmetic  4.88 us (4%)
    all_to_all x1, blocking collectives, per_device(): gathered = lax.all_to_all(filtered, 'gx', 1, 1, tiled=True)  34.6 us
    all_to_all x1, waiting for transfers between devices, per_device(): fed = lax.all_to_all(fed, 'gx', 1, 1, tiled=True)  13.9 us
    all_to_all x1, starting transfers between devices, per_device(): calm = lax.all_to_all(calm, 'gx', 1, 1, tiled=True)  13.4 us
    pallas_call x1, Pallas kernels, drop_source(): pl.pallas_call(source_kernel, grid=(drops // chunk,), in_specs=[pl.BlockS...  11 us
    all_to_all x1, starting transfers between devices, per_device(): fed = lax.all_to_all(fed, 'gx', 1, 1, tiled=True)  10.3 us
    ppermute x3, starting transfers between devices, per_device(): lax.ppermute(packed, 'gz', [(i, (i + shift) % gz_count) for i in range(gz...  4.51 us
  transfers between devices with their start and end apart: 5, of which 2 were waited for; matrix products, arithmetic and copies ran while one was open for 10% of the time, Pallas kernels for 10%

profile of v7, /device:TPU:1, one launch (start us, length us, event | category | flops | bytes accessed | tf_op | source)
XLA Modules:
  0.0 114.4 jit_solution(13931594290177314424)
XLA Ops:
  0.0 0.7 add_convert_fusion
  0.7 0.8 pad_maximum_fusion.13
  1.5 3.4 %collective-permute-start.2 = (f32[3,4096]{1,0:T(4,128)S(1)}, f32[3,4096]{1,0:T(4,128)S(1)}, u32[]{:S(2)}, u32[]{:S(2)}) collective-permute-start(f32[3,4096]{1,0:T(4,128)S(1)} %pad_maximum_fusion.13), channel_id=1, source_target_pairs={{0,3},{1,0},{2,1},{3,2},{4,7},{5,4},{6,5},{7,6},{8,11},{9,8},{10,9... | collective-permute-start | bytes 147464 | tf_op jit(solution)/shard_map/ppermute | solution.py:107
  4.9 0.5 collective-permute-start.1
  5.4 0.6 collective-permute-start
  6.0 2.0 %convolution_bitcast_fusion.3 = f32[2,512,128]{2,1,0:T(8,128)S(1)} fusion(f32[512,512]{1,0:T(8,128)} %param.16, f32[4,1,512,128]{3,2,0,1:T(8,128)} %bitcast.75), kind=kOutput, calls=%fused_computation.18 | convolution fusion | flops 403439616 | bytes 2097152 | tf_op jit(solution)/shard_map/ay,fyx->fax/dot_general | solution.py:118
  8.0 1.2 %copy.51 = f32[2,512,128]{2,0,1:T(2,128)} copy(f32[2,512,128]{2,1,0:T(8,128)S(1)} %convolution_bitcast_fusion.3) | data formatting | bytes 1048576 | tf_op jit(solution)/shard_map/ay,fyx->fax/transpose | solution.py:118
  9.2 13.4 %all-to-all-start = ((f32[2,512,128]{2,0,1:T(2,128)}), f32[2,512,128]{2,0,1:T(2,128)}, u32[]{:S(2)}, u32[]{:S(2)}) async-start(f32[2,512,128]{2,0,1:T(2,128)} %copy.51), calls=%async_computation | async-start | bytes 1048576 | tf_op jit(solution)/shard_map/all_to_all | solution.py:119
  22.6 0.5 compare_reduce_fusion
  24.3 0.3 and_select_fusion.2.row_ref
  24.6 11.0 %shard_map.91 = f32[512,512]{1,0:T(8,128)S(1)} custom-call(s32[1,16384]{1,0:T(1,128)S(1)} %and_select_fusion.2.row_ref, s32[1,16384]{1,0:T(1,128)S(1)} %get-tuple-element.9.col_ref, f32[4,16384]{1,0:T(4,128)S(1)} %reshape.135.piece_ref), custom_call_target="tpu_custom_call" | custom-call | flops 8589934592 | bytes 1048576 | tf_op jit(solution)/shard_map/pallas_call | solution.py:62
  35.6 0.7 reshape.136
  36.3 0.8 fusion.109
  37.2 0.5 copy-done.2
  37.6 1.1 convolution_bitcast_fusion.2
  38.7 1.0 copy.56
  39.8 10.3 %all-to-all-start.1 = ((f32[2,512,128]{2,0,1:T(2,128)}), f32[2,512,128]{2,0,1:T(2,128)S(1)}, u32[]{:S(2)}, u32[]{:S(2)}) async-start(f32[2,512,128]{2,0,1:T(2,128)} %copy.56), calls=%async_computation.1 | async-start | bytes 1048576 | tf_op jit(solution)/shard_map/all_to_all | solution.py:121
  50.7 0.8 dynamic_slice.3
  52.4 1.1 copy.57
  53.5 13.9 %all-to-all-done.1 = f32[2,512,128]{2,0,1:T(2,128)S(1)} async-done(((f32[2,512,128]{2,0,1:T(2,128)}), f32[2,512,128]{2,0,1:T(2,128)S(1)}, u32[]{:S(2)}, u32[]{:S(2)}) %all-to-all-start.1) | async-done | bytes 524320 | tf_op jit(solution)/shard_map/all_to_all | solution.py:121
  67.5 0.7 convolution_bitcast_fusion.1
  68.2 1.0 multiply_add_fusion.2
  69.4 2.0 %fusion.2 = f32[4,64,8,256]{3,2,1,0:T(8,128)S(1)} fusion(f32[4,64,8,256]{3,1,2,0:T(8,128)S(1)} %pad_maximum_fusion, f32[128,128]{1,0:T(8,128)S(1)} %get-tuple-element.23, f32[128,128]{1,0:T(8,128)S(1)} %get-tuple-element.22, f32[128,128]{1,0:T(8,128)S(1)} %fusion.81), kind=kOutput, calls=%fused_computation.4 | convolution fusion | flops 805502976 | bytes 4390912 | tf_op jit(solution)/shard_map/fkaj,jm->fkam/dot_general | solution.py:141
  71.5 0.6 multiply_subtract_fusion.1
  72.2 1.5 %fusion = f32[4,64,8,256]{3,1,2,0:T(8,128)S(1)} fusion(f32[4,64,8,256]{3,2,1,0:T(8,128)S(1)} %pad_maximum_fusion.1, f32[128,128]{1,0:T(8,128)S(1)} %get-tuple-element.23, f32[128,128]{1,0:T(8,128)S(1)} %fusion.81, f32[128,128]{1,0:T(8,128)S(1)} %get-tuple-element.22), kind=kOutput, calls=%fused_computation.2 | convolution fusion | flops 805502976 | bytes 4390912 | tf_op jit(solution)/shard_map/fkam,mj->fkaj/dot_general | solution.py:169
  73.7 0.7 fusion.15
  74.4 0.8 fusion.5
  75.2 0.6 copy.100
  75.9 0.7 copy.65
  76.6 34.6 %all_to_all.15 = f32[4,512,128]{2,0,1:T(4,128)S(1)} all-to-all(f32[4,512,128]{2,0,1:T(4,128)S(1)} %copy.65), channel_id=1, replica_groups=mesh['gx'=64,'gz'=4] {'gx'}, dimensions={1} | all-to-all | bytes 2097152 | tf_op jit(solution)/shard_map/all_to_all | solution.py:180
  111.2 1.9 %convolution_bitcast_fusion = f32[4,1,512,128]{2,3,0,1:T(8,128)S(1)} fusion(f32[512,512]{1,0:T(8,128)S(1)} %copy-done.1, f32[4,512,128]{2,0,1:T(4,128)S(1)} %all_to_all.15), kind=kOutput, calls=%fused_computation.10 | convolution fusion | flops 806092800 | bytes 3145728 | tf_op jit(solution)/shard_map/ya,fax->fyx/dot_general | solution.py:181
  113.1 1.3 %copy.67 = f32[4,1,512,128]{3,2,1,0:T(8,128)} copy(f32[4,1,512,128]{2,3,0,1:T(8,128)S(1)} %convolution_bitcast_fusion) | data formatting | bytes 2097152 | tf_op jit(solution)/shard_map/broadcast_in_dim | solution.py:182
  (29 shorter events, 2.5 us)
Async XLA Ops:
  1.5 21.1 %collective-permute-start.2 = (f32[3,4096]{1,0:T(4,128)S(1)}, f32[3,4096]{1,0:T(4,128)S(1)}, u32[]{:S(2)}, u32[]{:S(2)}) collective-permute-start(f32[3,4096]{1,0:T(4,128)S(1)} %pad_maximum_fusion.13), channel_id=1, source_target_pairs={{0,3},{1,0},{2,1},{3,2},{4,7},{5,4},{6,5},{7,6},{8,11},{9,8},{10,9... | collective-permute-start | bytes 147464 | tf_op jit(solution)/shard_map/ppermute | solution.py:107
  4.9 17.7 %collective-permute-start.1 = (f32[3,4096]{1,0:T(4,128)S(1)}, f32[3,4096]{1,0:T(4,128)S(1)}, u32[]{:S(2)}, u32[]{:S(2)}) collective-permute-start(f32[3,4096]{1,0:T(4,128)S(1)} %pad_maximum_fusion.13), channel_id=1, source_target_pairs={{0,2},{1,3},{2,0},{3,1},{4,6},{5,7},{6,4},{7,5},{8,10},{9,11},{10,... | collective-permute-start | bytes 147464 | tf_op jit(solution)/shard_map/ppermute | solution.py:107
  5.4 17.2 %collective-permute-start = (f32[3,4096]{1,0:T(4,128)S(1)}, f32[3,4096]{1,0:T(4,128)S(1)}, u32[]{:S(2)}, u32[]{:S(2)}) collective-permute-start(f32[3,4096]{1,0:T(4,128)S(1)} %pad_maximum_fusion.13), channel_id=1, source_target_pairs={{0,1},{1,2},{2,3},{3,0},{4,5},{5,6},{6,7},{7,4},{8,9},{9,10},{10,1... | collective-permute-start | bytes 147464 | tf_op jit(solution)/shard_map/ppermute | solution.py:107
  6.0 16.6 %copy-start.3 = (f32[2,4096]{1,0:T(2,128)S(1)}, f32[2,4096]{1,0:T(2,128)}, u32[]{:S(2)}) copy-start(f32[2,4096]{1,0:T(2,128)} %param.12) | copy-start | bytes 98308
  9.2 30.6 %all-to-all-start = ((f32[2,512,128]{2,0,1:T(2,128)}), f32[2,512,128]{2,0,1:T(2,128)}, u32[]{:S(2)}, u32[]{:S(2)}) async-start(f32[2,512,128]{2,0,1:T(2,128)} %copy.51), calls=%async_computation | async-start | bytes 1048576 | tf_op jit(solution)/shard_map/all_to_all | solution.py:119
  35.6 1.5 %copy-start = (f32[512,512]{1,0:T(8,128)S(1)}, f32[512,512]{1,0:T(8,128)}, u32[]{:S(2)}) copy-start(f32[512,512]{1,0:T(8,128)} %param.16) | copy-start | bytes 3145732
  36.3 1.3 %copy-start.2 = (f32[4,1,512,128]{3,2,1,0:T(8,128)S(1)}, f32[4,1,512,128]{3,2,1,0:T(8,128)}, u32[]{:S(2)}) copy-start(f32[4,1,512,128]{3,2,1,0:T(8,128)} %param.9) | copy-start | bytes 3145732
  39.8 27.6 %all-to-all-start.1 = ((f32[2,512,128]{2,0,1:T(2,128)}), f32[2,512,128]{2,0,1:T(2,128)S(1)}, u32[]{:S(2)}, u32[]{:S(2)}) async-start(f32[2,512,128]{2,0,1:T(2,128)} %copy.56), calls=%async_computation.1 | async-start | bytes 1048576 | tf_op jit(solution)/shard_map/all_to_all | solution.py:121
  69.4 2.1 %copy-start.4 = (f32[4]{0:T(128)S(1)}, f32[4]{0:T(128)}, u32[]{:S(2)}) copy-start(f32[4]{0:T(128)} %param.13) | copy-start | bytes 52
  75.9 35.3 %copy-start.1 = (f32[512,512]{1,0:T(8,128)S(1)}, f32[512,512]{1,0:T(8,128)}, u32[]{:S(2)}) copy-start(f32[512,512]{1,0:T(8,128)} %param.15) | copy-start | bytes 3145732

commit v8 on v2

v8 whole, which is shorter than its diff:
```python
import math

import jax
import jax.numpy as jnp
from jax import lax
from jax.experimental import pallas as pl
from jax.experimental.pallas import tpu as pltpu
from jax.sharding import PartitionSpec as P

HI = lax.Precision.HIGH


def phase(numer, length):
    angle = 2.0 * math.pi / length * (numer % length).astype(jnp.float32)
    return jnp.cos(angle), jnp.sin(angle)


PIECES = 2
CHUNK = 2048


def source_kernel(row_ref, col_ref, piece_ref, out_ref):
    step = pl.program_id(0)
    row_count = out_ref.shape[0]
    slab_width = out_ref.shape[1] // piece_ref.shape[0]
    chunk = row_ref.shape[1]
    rows = row_ref[...]
    cols = col_ref[...]
    row_hit = lax.broadcasted_iota(jnp.int32, (row_count, chunk), 0) == rows
    lhs = jnp.where(row_hit, 1.0, 0.0).astype(jnp.bfloat16)
    col_hit = lax.broadcasted_iota(jnp.int32, (slab_width, chunk), 0) == cols
    pieces = piece_ref[...]
    rhs = jnp.concatenate(
        [jnp.where(col_hit, pieces[p : p + 1, :], 0.0) for p in range(pieces.shape[0])], axis=0
    ).astype(jnp.bfloat16)
    part = lax.dot_general(
        lhs, rhs, (((1,), (1,)), ((), ())), preferred_element_type=jnp.float32
    )

    @pl.when(step == 0)
    def _():
        out_ref[...] = part

    @pl.when(step > 0)
    def _():
        out_ref[...] += part


def drop_source(cells, rates, row_count, slab_width):
    drops = cells.shape[0]
    pieces = []
    rest = rates
    for _ in range(PIECES):
        piece = lax.reduce_precision(rest, exponent_bits=8, mantissa_bits=7)
        pieces.append(piece)
        rest = rest - piece
    pieces = jnp.stack(pieces, axis=1).reshape(2 * PIECES, drops)
    rows = (cells // slab_width).reshape(1, drops)
    cols = (cells % slab_width).reshape(1, drops)
    width = 2 * PIECES * slab_width
    chunk = min(CHUNK, drops)
    summed = pl.pallas_call(
        source_kernel,
        grid=(drops // chunk,),
        in_specs=[
            pl.BlockSpec((1, chunk), lambda i: (0, i)),
            pl.BlockSpec((1, chunk), lambda i: (0, i)),
            pl.BlockSpec((2 * PIECES, chunk), lambda i: (0, i)),
        ],
        out_specs=pl.BlockSpec((row_count, width), lambda i: (0, 0)),
        out_shape=jax.ShapeDtypeStruct((row_count, width), jnp.float32),
        compiler_params=pltpu.CompilerParams(vmem_limit_bytes=48 * 1024 * 1024),
        cost_estimate=pl.CostEstimate(
            flops=2 * row_count * width * drops, transcendentals=0, bytes_accessed=4 * row_count * width
        ),
    )(rows, cols, pieces)
    summed = summed.reshape(row_count, 2, PIECES, slab_width)
    total = summed[:, :, 0]
    for p in range(1, PIECES):
        total = total + summed[:, :, p]
    return jnp.transpose(total, (1, 0, 2))


def dft_tables(gx_count, slab_width):
    total_cells = gx_count * slab_width
    d_index = jnp.arange(gx_count, dtype=jnp.int32)
    j_index = jnp.arange(slab_width, dtype=jnp.int32)
    c64, s64 = phase(d_index[:, None] * d_index[None, :], gx_count)
    ct, st = phase(d_index[:, None] * j_index[None, :], total_cells)
    c128, s128 = phase(j_index[:, None] * j_index[None, :], slab_width)
    return d_index, j_index, c64, s64, ct, st, c128, s128


def fft_filter(spread, diffusivity, eigen_here, bulk_shift, tables):
    d_index, j_index, c64, s64, ct, st, c128, s128 = tables
    field_count, row_count, slab_width = spread.shape
    gx_count = c64.shape[0]
    rows_here = row_count // gx_count
    total_cells = gx_count * slab_width
    spread = spread.reshape(field_count, gx_count, rows_here, slab_width)

    a_real = jnp.einsum("kd,fdaj->fkaj", c64, spread, precision=HI)
    a_imag = -jnp.einsum("kd,fdaj->fkaj", s64, spread, precision=HI)
    ct4 = ct[None, :, None, :]
    st4 = st[None, :, None, :]
    b_real = a_real * ct4 + a_imag * st4
    b_imag = a_imag * ct4 - a_real * st4
    joined = jnp.concatenate([b_real, b_imag], axis=-1)
    forward_table = jnp.concatenate(
        [jnp.concatenate([c128, -s128], axis=1), jnp.concatenate([s128, c128], axis=1)], axis=0
    )
    spec = jnp.einsum("fkaj,jm->fkam", joined, forward_table, precision=HI)
    spec_real = spec[..., :slab_width]
    spec_imag = spec[..., slab_width:]

    mode_index = d_index[:, None] + gx_count * j_index[None, :]
    folded = jnp.minimum(mode_index, total_cells - mode_index).astype(jnp.float32)
    wavenumber = 2.0 * math.pi / total_cells * folded
    growth = diffusivity[:, None, None, None] * (
        eigen_here[None, None, :, None] + (wavenumber**2)[None, :, None, :]
    )
    damping = (1.0 - growth) / (1.0 + growth)
    signed = jnp.where(2 * mode_index >= total_cells, mode_index - total_cells, mode_index).astype(
        jnp.float32
    )
    travel = 2.0 * math.pi / total_cells * signed * bulk_shift[0]
    cos_travel = jnp.cos(travel)[None, :, None, :]
    sin_travel = jnp.sin(travel)[None, :, None, :]
    factor_real = damping * cos_travel
    factor_imag = -damping * sin_travel
    turned_real = spec_real * factor_real - spec_imag * factor_imag
    turned_imag = spec_real * factor_imag + spec_imag * factor_real

    joined = jnp.concatenate([turned_real, turned_imag], axis=-1)
    inverse_table = jnp.concatenate(
        [jnp.concatenate([c128, s128], axis=1), jnp.concatenate([-s128, c128], axis=1)], axis=0
    )
    back = jnp.einsum("fkam,mj->fkaj", joined, inverse_table, precision=HI)
    back_real = back[..., :slab_width]
    back_imag = back[..., slab_width:]
    e_real = back_real * ct4 - back_imag * st4
    e_imag = back_real * st4 + back_imag * ct4
    filtered = (
        jnp.einsum("dk,fkaj->fdaj", c64, e_real, precision=HI)
        - jnp.einsum("dk,fkaj->fdaj", s64, e_imag, precision=HI)
    ) / total_cells

    return filtered.reshape(field_count, row_count, slab_width)


def per_device(
    field,
    drop_cell,
    drop_plane,
    drop_rate,
    diffusivity,
    wall_eigen,
    basis_part,
    dual_part,
    bulk_shift,
):
    field_count, plane_count, row_count, slab_width = field.shape
    gx_count = lax.axis_size("gx")
    gz_count = lax.axis_size("gz")
    total_cells = slab_width * gx_count
    plane_cells = row_count * slab_width
    rows_here = row_count // gx_count

    plane_here = lax.axis_index("gz")
    packed = jnp.concatenate(
        [(drop_plane * plane_cells + drop_cell).astype(jnp.float32)[None, :], drop_rate], axis=0
    )
    shares = [packed] + [
        lax.ppermute(packed, "gz", [(i, (i + shift) % gz_count) for i in range(gz_count)])
        for shift in range(1, gz_count)
    ]
    packed = jnp.concatenate(shares, axis=1)
    keys = packed[0].astype(jnp.int32)
    cells = keys % plane_cells
    planes = keys // plane_cells
    rates = jnp.where((planes == plane_here)[None, :], packed[1:], 0.0)
    source = drop_source(cells, rates, row_count, slab_width)
    identity = jnp.eye(row_count, dtype=jnp.float32)
    dual_full = identity + dual_part
    calm = jnp.einsum("ay,fyx->fax", dual_full, field[:2, 0], precision=HI)
    calm = lax.all_to_all(calm, "gx", 1, 1, tiled=True)
    fed = jnp.einsum("ay,fyx->fax", dual_full, field[2:, 0] + source, precision=HI)
    fed = lax.all_to_all(fed, "gx", 1, 1, tiled=True)
    tables = dft_tables(gx_count, slab_width)
    position = lax.axis_index("gx")
    eigen_here = lax.dynamic_slice_in_dim(wall_eigen, position * rows_here, rows_here)
    calm = fft_filter(calm, diffusivity[:2], eigen_here, bulk_shift, tables)
    calm, fed = lax.optimization_barrier((calm, fed))
    fed = fft_filter(fed, diffusivity[2:], eigen_here, bulk_shift, tables)
    filtered = jnp.concatenate([calm, fed], axis=0)
    filtered = filtered.reshape(field_count, row_count, slab_width)
    gathered = lax.all_to_all(filtered, "gx", 1, 1, tiled=True)
    result = jnp.einsum("ya,fax->fyx", identity + basis_part, gathered, precision=HI)
    return result[:, None]


def solution(mesh):
    in_specs = (
        P(None, "gz", None, "gx"),
        P(("gx", "gz")),
        P(("gx", "gz")),
        P(None, ("gx", "gz")),
        P(),
        P(),
        P(),
        P(),
        P(),
    )
    out_specs = P(None, "gz", None, "gx")
    return jax.shard_map(
        per_device, mesh=mesh, in_specs=in_specs, out_specs=out_specs, check_vma=False
    )
```

time: 156 us -> 113 us (0.72)
  blocking collectives: 63.5 us -> 34.8 us
  waiting for transfers between devices: 26 us -> 12.4 us
  starting transfers between devices: 21.1 us -> 28 us
  Pallas kernels: 16.1 us -> 11 us
  matrix products: 16.2 us -> 13 us
  other arithmetic: 2.41 us -> 4.17 us
    all_gather x3 -> x0, blocking collectives: 28.9 us -> none  [the longest x1 10.4 us: per_device(): cells = lax.all_gather(drop_cell, 'gz', tiled=True)]
    all_to_all x1 -> x2, waiting for transfers between devices: 26 us -> 12.4 us  [the longest x1 12.4 us: per_device(): fed = lax.all_to_all(fed, 'gx', 1, 1, tiled=True)]
    pallas_call x1, Pallas kernels: 16.1 us -> 11 us  [drop_source(): pl.pallas_call(source_kernel, grid=(drops // chunk,), in_specs=[pl.BlockS...]
    ppermute x0 -> x3, starting transfers between devices: none -> 4.51 us  [per_device(): lax.ppermute(packed, 'gz', [(i, (i + shift) % gz_count) for i in range(gz...]
    all_to_all x1 -> x2, starting transfers between devices: 21.1 us -> 23.5 us  [the longest x1 13.2 us: per_device(): calm = lax.all_to_all(calm, 'gx', 1, 1, tiled=True)]
    dot_general x1, matrix products: 3.48 us -> 1.86 us  [per_device(): jnp.einsum('ya,fax->fyx', identity + basis_part, gathered, precision=HI)]
    unnamed x10, local copies, waits for them, and re-layouts: 2.36 us -> 0.77 us
    dot_general x7 -> x14, matrix products: 12.7 us -> 11.2 us  [the longest x2 2.15 us: fft_filter(): spec = jnp.einsum('fkaj,jm->fkam', joined, forward_table, precision=HI)]
  transfers between devices with their start and end apart: 1 -> 5, of which waited for: 1 -> 1; matrix products, arithmetic and copies ran while one was open for 1% -> 14% of each run, Pallas kernels for 0% -> 10%
where the time goes in v8:
time: 113 us
  blocking collectives  34.8 us (31%)
  starting transfers between devices  28 us (25%)
  matrix products  13 us (12%)
  waiting for transfers between devices  12.4 us (11%)
  Pallas kernels  11 us (10%)
  local copies, waits for them, and re-layouts  8.39 us (7%)
  other arithmetic  4.17 us (4%)
    all_to_all x1, blocking collectives, per_device(): gathered = lax.all_to_all(filtered, 'gx', 1, 1, tiled=True)  34.8 us
    all_to_all x1, starting transfers between devices, per_device(): calm = lax.all_to_all(calm, 'gx', 1, 1, tiled=True)  13.2 us
    all_to_all x1, waiting for transfers between devices, per_device(): fed = lax.all_to_all(fed, 'gx', 1, 1, tiled=True)  12.4 us
    pallas_call x1, Pallas kernels, drop_source(): pl.pallas_call(source_kernel, grid=(drops // chunk,), in_specs=[pl.BlockS...  11 us
    all_to_all x1, starting transfers between devices, per_device(): fed = lax.all_to_all(fed, 'gx', 1, 1, tiled=True)  10.3 us
    ppermute x3, starting transfers between devices, per_device(): lax.ppermute(packed, 'gz', [(i, (i + shift) % gz_count) for i in range(gz...  4.51 us
  transfers between devices with their start and end apart: 5, of which 1 were waited for; matrix products, arithmetic and copies ran while one was open for 14% of the time, Pallas kernels for 10%

profile of v8, /device:TPU:1, one launch (start us, length us, event | category | flops | bytes accessed | tf_op | source)
XLA Modules:
  0.0 112.8 jit_solution(17983185208836958788)
XLA Ops:
  0.0 0.7 add_convert_fusion
  0.8 3.4 %collective-permute-start.2 = (f32[3,4096]{1,0:T(4,128)S(1)}, f32[3,4096]{1,0:T(4,128)S(1)}, u32[]{:S(2)}, u32[]{:S(2)}) collective-permute-start(f32[3,4096]{1,0:T(4,128)S(1)} %pad_maximum_fusion.14), channel_id=1, source_target_pairs={{0,3},{1,0},{2,1},{3,2},{4,7},{5,4},{6,5},{7,6},{8,11},{9,8},{10,9... | collective-permute-start | bytes 147464 | tf_op jit(solution)/shard_map/ppermute | solution.py:174
  4.2 0.5 collective-permute-start.1
  4.7 0.6 collective-permute-start
  5.3 1.9 %convolution_bitcast_fusion.4 = f32[2,512,128]{2,1,0:T(8,128)S(1)} fusion(f32[512,512]{1,0:T(8,128)} %param.16, f32[4,1,512,128]{3,2,0,1:T(8,128)} %bitcast.105), kind=kOutput, calls=%fused_computation.10 | convolution fusion | flops 403439616 | bytes 2097152 | tf_op jit(solution)/shard_map/ay,fyx->fax/dot_general | solution.py:185
  7.3 1.2 %copy.69 = f32[2,512,128]{2,0,1:T(2,128)} copy(f32[2,512,128]{2,1,0:T(8,128)S(1)} %convolution_bitcast_fusion.4) | data formatting | bytes 1048576 | tf_op jit(solution)/shard_map/ay,fyx->fax/transpose | solution.py:185
  8.5 13.2 %all-to-all-start = ((f32[2,512,128]{2,0,1:T(2,128)}), f32[2,512,128]{2,0,1:T(2,128)S(1)}, u32[]{:S(2)}, u32[]{:S(2)}) async-start(f32[2,512,128]{2,0,1:T(2,128)} %copy.69), calls=%async_computation | async-start | bytes 1048576 | tf_op jit(solution)/shard_map/all_to_all | solution.py:186
  23.0 0.8 dynamic_slice.3
  24.2 0.5 compare_reduce_fusion
  26.2 11.0 %shard_map.91 = f32[512,512]{1,0:T(8,128)S(1)} custom-call(s32[1,16384]{1,0:T(1,128)S(1)} %and_select_fusion.2.row_ref, s32[1,16384]{1,0:T(1,128)S(1)} %get-tuple-element.13.col_ref, f32[4,16384]{1,0:T(4,128)S(1)} %reshape.144.piece_ref), custom_call_target="tpu_custom_call" | custom-call | flops 8589934592 | bytes 1048576 | tf_op jit(solution)/shard_map/pallas_call | solution.py:62
  37.2 0.7 reshape.145
  37.9 0.8 fusion.158
  39.4 1.1 convolution_bitcast_fusion.2
  40.5 1.0 copy.81
  41.5 10.3 %all-to-all-start.1 = ((f32[2,512,128]{2,0,1:T(2,128)}), f32[2,512,128]{2,0,1:T(2,128)S(1)}, u32[]{:S(2)}, u32[]{:S(2)}) async-start(f32[2,512,128]{2,0,1:T(2,128)} %copy.81), calls=%async_computation.1 | async-start | bytes 1048576 | tf_op jit(solution)/shard_map/all_to_all | solution.py:188
  51.9 0.5 convolution_bitcast_fusion.3
  52.4 0.6 multiply_add_fusion.5
  53.1 1.1 fusion.16
  54.6 0.8 fusion.11
  55.4 0.5 fusion.38
  55.9 0.5 fusion.5
  56.8 12.4 %all-to-all-done.1 = f32[2,512,128]{2,0,1:T(2,128)S(1)} async-done(((f32[2,512,128]{2,0,1:T(2,128)}), f32[2,512,128]{2,0,1:T(2,128)S(1)}, u32[]{:S(2)}, u32[]{:S(2)}) %all-to-all-start.1) | async-done | bytes 524320 | tf_op jit(solution)/shard_map/all_to_all | solution.py:188
  69.2 0.5 convolution_bitcast_fusion.1
  69.7 0.6 multiply_add_fusion.3
  70.4 1.1 fusion.14
  71.9 0.8 fusion.9
  72.7 0.5 fusion.30
  73.3 0.5 fusion.3
  74.2 0.7 copy.89
  74.9 34.8 %all_to_all.15 = f32[4,512,128]{2,0,1:T(4,128)S(1)} all-to-all(f32[4,512,128]{2,0,1:T(4,128)S(1)} %copy.89), channel_id=1, replica_groups=mesh['gx'=64,'gz'=4] {'gx'}, dimensions={1} | all-to-all | bytes 2097152 | tf_op jit(solution)/shard_map/all_to_all | solution.py:197
  109.7 1.9 %convolution_bitcast_fusion = f32[4,1,512,128]{2,3,0,1:T(8,128)S(1)} fusion(f32[512,512]{1,0:T(8,128)S(1)} %copy-done.1, f32[4,512,128]{2,0,1:T(4,128)S(1)} %all_to_all.15), kind=kOutput, calls=%fused_computation.2 | convolution fusion | flops 806092800 | bytes 3145728 | tf_op jit(solution)/shard_map/ya,fax->fyx/dot_general | solution.py:198
  111.5 1.3 %copy.91 = f32[4,1,512,128]{3,2,1,0:T(8,128)} copy(f32[4,1,512,128]{2,3,0,1:T(8,128)S(1)} %convolution_bitcast_fusion) | data formatting | bytes 2097152 | tf_op jit(solution)/shard_map/broadcast_in_dim | solution.py:199
  (40 shorter events, 4.8 us)
Async XLA Ops:
  0.0 0.8 copy-start.3
  0.8 23.3 %collective-permute-start.2 = (f32[3,4096]{1,0:T(4,128)S(1)}, f32[3,4096]{1,0:T(4,128)S(1)}, u32[]{:S(2)}, u32[]{:S(2)}) collective-permute-start(f32[3,4096]{1,0:T(4,128)S(1)} %pad_maximum_fusion.14), channel_id=1, source_target_pairs={{0,3},{1,0},{2,1},{3,2},{4,7},{5,4},{6,5},{7,6},{8,11},{9,8},{10,9... | collective-permute-start | bytes 147464 | tf_op jit(solution)/shard_map/ppermute | solution.py:174
  4.2 19.9 %collective-permute-start.1 = (f32[3,4096]{1,0:T(4,128)S(1)}, f32[3,4096]{1,0:T(4,128)S(1)}, u32[]{:S(2)}, u32[]{:S(2)}) collective-permute-start(f32[3,4096]{1,0:T(4,128)S(1)} %pad_maximum_fusion.14), channel_id=1, source_target_pairs={{0,2},{1,3},{2,0},{3,1},{4,6},{5,7},{6,4},{7,5},{8,10},{9,11},{10,... | collective-permute-start | bytes 147464 | tf_op jit(solution)/shard_map/ppermute | solution.py:174
  4.7 19.4 %collective-permute-start = (f32[3,4096]{1,0:T(4,128)S(1)}, f32[3,4096]{1,0:T(4,128)S(1)}, u32[]{:S(2)}, u32[]{:S(2)}) collective-permute-start(f32[3,4096]{1,0:T(4,128)S(1)} %pad_maximum_fusion.14), channel_id=1, source_target_pairs={{0,1},{1,2},{2,3},{3,0},{4,5},{5,6},{6,7},{7,4},{8,9},{9,10},{10,1... | collective-permute-start | bytes 147464 | tf_op jit(solution)/shard_map/ppermute | solution.py:174
  8.5 33.0 %all-to-all-start = ((f32[2,512,128]{2,0,1:T(2,128)}), f32[2,512,128]{2,0,1:T(2,128)S(1)}, u32[]{:S(2)}, u32[]{:S(2)}) async-start(f32[2,512,128]{2,0,1:T(2,128)} %copy.69), calls=%async_computation | async-start | bytes 1048576 | tf_op jit(solution)/shard_map/all_to_all | solution.py:186
  22.2 0.7 copy-start.4
  37.9 1.2 %copy-start = (f32[512,512]{1,0:T(8,128)S(1)}, f32[512,512]{1,0:T(8,128)}, u32[]{:S(2)}) copy-start(f32[512,512]{1,0:T(8,128)} %param.16) | copy-start | bytes 3145732
  37.9 1.5 %copy-start.2 = (f32[4,1,512,128]{3,2,1,0:T(8,128)S(1)}, f32[4,1,512,128]{3,2,1,0:T(8,128)}, u32[]{:S(2)}) copy-start(f32[4,1,512,128]{3,2,1,0:T(8,128)} %param.9) | copy-start | bytes 3145732
  41.5 27.6 %all-to-all-start.1 = ((f32[2,512,128]{2,0,1:T(2,128)}), f32[2,512,128]{2,0,1:T(2,128)S(1)}, u32[]{:S(2)}, u32[]{:S(2)}) async-start(f32[2,512,128]{2,0,1:T(2,128)} %copy.81), calls=%async_computation.1 | async-start | bytes 1048576 | tf_op jit(solution)/shard_map/all_to_all | solution.py:188
  74.9 34.8 %copy-start.1 = (f32[512,512]{1,0:T(8,128)S(1)}, f32[512,512]{1,0:T(8,128)}, u32[]{:S(2)}) copy-start(f32[512,512]{1,0:T(8,128)} %param.15) | copy-start | bytes 3145732

commit v9 on v8

--- a/solution.py
+++ b/solution.py
@@ -8,6 +8,7 @@
 from jax.sharding import PartitionSpec as P
 
 HI = lax.Precision.HIGH
+EXACT = lax.Precision.HIGHEST
 
 
 def phase(numer, length):
@@ -99,8 +100,8 @@
     total_cells = gx_count * slab_width
     spread = spread.reshape(field_count, gx_count, rows_here, slab_width)
 
-    a_real = jnp.einsum("kd,fdaj->fkaj", c64, spread, precision=HI)
-    a_imag = -jnp.einsum("kd,fdaj->fkaj", s64, spread, precision=HI)
+    a_real = jnp.einsum("kd,fdaj->fkaj", c64, spread, precision=EXACT)
+    a_imag = -jnp.einsum("kd,fdaj->fkaj", s64, spread, precision=EXACT)
     ct4 = ct[None, :, None, :]
     st4 = st[None, :, None, :]
     b_real = a_real * ct4 + a_imag * st4
@@ -109,7 +110,7 @@
     forward_table = jnp.concatenate(
         [jnp.concatenate([c128, -s128], axis=1), jnp.concatenate([s128, c128], axis=1)], axis=0
     )
-    spec = jnp.einsum("fkaj,jm->fkam", joined, forward_table, precision=HI)
+    spec = jnp.einsum("fkaj,jm->fkam", joined, forward_table, precision=EXACT)
     spec_real = spec[..., :slab_width]
     spec_imag = spec[..., slab_width:]
 
@@ -135,14 +136,14 @@
     inverse_table = jnp.concatenate(
         [jnp.concatenate([c128, s128], axis=1), jnp.concatenate([-s128, c128], axis=1)], axis=0
     )
-    back = jnp.einsum("fkam,mj->fkaj", joined, inverse_table, precision=HI)
+    back = jnp.einsum("fkam,mj->fkaj", joined, inverse_table, precision=EXACT)
     back_real = back[..., :slab_width]
     back_imag = back[..., slab_width:]
     e_real = back_real * ct4 - back_imag * st4
     e_imag = back_real * st4 + back_imag * ct4
     filtered = (
-        jnp.einsum("dk,fkaj->fdaj", c64, e_real, precision=HI)
-        - jnp.einsum("dk,fkaj->fdaj", s64, e_imag, precision=HI)
+        jnp.einsum("dk,fkaj->fdaj", c64, e_real, precision=EXACT)
+        - jnp.einsum("dk,fkaj->fdaj", s64, e_imag, precision=EXACT)
     ) / total_cells
 
     return filtered.reshape(field_count, row_count, slab_width)

time: 113 us -> 115 us (1.018)
  matrix products: 13 us -> 16.7 us
  waiting for transfers between devices: 12.4 us -> 10.5 us
    dot_general x12, matrix products: 8.11 us -> 11.8 us  [the longest x2 2.96 us: fft_filter(): spec = jnp.einsum('fkaj,jm->fkam', joined, forward_table, precision=EXACT)]
    all_to_all x1, waiting for transfers between devices: 12.4 us -> 10.5 us  [per_device(): fed = lax.all_to_all(fed, 'gx', 1, 1, tiled=True)]
  transfers between devices with their start and end apart: 5 -> 5, of which waited for: 1 -> 1; matrix products, arithmetic and copies ran while one was open for 14% -> 15% of each run, Pallas kernels for 10% -> 10%
where the time goes in v9:
time: 115 us
  blocking collectives  34.8 us (30%)
  starting transfers between devices  28.2 us (25%)
  matrix products  16.7 us (15%)
  Pallas kernels  11 us (10%)
  waiting for transfers between devices  10.5 us (9%)
  local copies, waits for them, and re-layouts  8.39 us (7%)
  other arithmetic  4.17 us (4%)
    all_to_all x1, blocking collectives, per_device(): gathered = lax.all_to_all(filtered, 'gx', 1, 1, tiled=True)  34.8 us
    all_to_all x1, starting transfers between devices, per_device(): calm = lax.all_to_all(calm, 'gx', 1, 1, tiled=True)  13.2 us
    pallas_call x1, Pallas kernels, drop_source(): pl.pallas_call(source_kernel, grid=(drops // chunk,), in_specs=[pl.BlockS...  11 us
    all_to_all x1, starting transfers between devices, per_device(): fed = lax.all_to_all(fed, 'gx', 1, 1, tiled=True)  10.5 us
    all_to_all x1, waiting for transfers between devices, per_device(): fed = lax.all_to_all(fed, 'gx', 1, 1, tiled=True)  10.5 us
    ppermute x3, starting transfers between devices, per_device(): lax.ppermute(packed, 'gz', [(i, (i + shift) % gz_count) for i in range(gz...  4.51 us
    dot_general x2, matrix products, fft_filter(): spec = jnp.einsum('fkaj,jm->fkam', joined, forward_table, precision=EXACT)  2.96 us
    dot_general x2, matrix products, fft_filter(): back = jnp.einsum('fkam,mj->fkaj', joined, inverse_table, precision=EXACT)  2.31 us
  transfers between devices with their start and end apart: 5, of which 1 were waited for; matrix products, arithmetic and copies ran while one was open for 15% of the time, Pallas kernels for 10%

profile of v9, /device:TPU:1, one launch (start us, length us, event | category | flops | bytes accessed | tf_op | source)
XLA Modules:
  0.0 114.8 jit_solution(15795159192603975570)
XLA Ops:
  0.0 0.7 add_convert_fusion
  0.8 3.4 %collective-permute-start.2 = (f32[3,4096]{1,0:T(4,128)S(1)}, f32[3,4096]{1,0:T(4,128)S(1)}, u32[]{:S(2)}, u32[]{:S(2)}) collective-permute-start(f32[3,4096]{1,0:T(4,128)S(1)} %pad_maximum_fusion.14), channel_id=1, source_target_pairs={{0,3},{1,0},{2,1},{3,2},{4,7},{5,4},{6,5},{7,6},{8,11},{9,8},{10,9... | collective-permute-start | bytes 147464 | tf_op jit(solution)/shard_map/ppermute | solution.py:175
  4.2 0.5 collective-permute-start.1
  4.7 0.6 collective-permute-start
  5.3 1.9 %convolution_bitcast_fusion.4 = f32[2,512,128]{2,1,0:T(8,128)S(1)} fusion(f32[512,512]{1,0:T(8,128)} %param.16, f32[4,1,512,128]{3,2,0,1:T(8,128)} %bitcast.105), kind=kOutput, calls=%fused_computation.10 | convolution fusion | flops 403439616 | bytes 2097152 | tf_op jit(solution)/shard_map/ay,fyx->fax/dot_general | solution.py:186
  7.3 1.2 %copy.69 = f32[2,512,128]{2,0,1:T(2,128)} copy(f32[2,512,128]{2,1,0:T(8,128)S(1)} %convolution_bitcast_fusion.4) | data formatting | bytes 1048576 | tf_op jit(solution)/shard_map/ay,fyx->fax/transpose | solution.py:186
  8.5 13.2 %all-to-all-start = ((f32[2,512,128]{2,0,1:T(2,128)}), f32[2,512,128]{2,0,1:T(2,128)S(1)}, u32[]{:S(2)}, u32[]{:S(2)}) async-start(f32[2,512,128]{2,0,1:T(2,128)} %copy.69), calls=%async_computation | async-start | bytes 1048576 | tf_op jit(solution)/shard_map/all_to_all | solution.py:187
  23.0 0.8 dynamic_slice.3
  24.2 0.5 compare_reduce_fusion
  26.2 11.0 %shard_map.91 = f32[512,512]{1,0:T(8,128)S(1)} custom-call(s32[1,16384]{1,0:T(1,128)S(1)} %and_select_fusion.2.row_ref, s32[1,16384]{1,0:T(1,128)S(1)} %get-tuple-element.13.col_ref, f32[4,16384]{1,0:T(4,128)S(1)} %reshape.144.piece_ref), custom_call_target="tpu_custom_call" | custom-call | flops 8589934592 | bytes 1048576 | tf_op jit(solution)/shard_map/pallas_call | solution.py:63
  37.2 0.7 reshape.145
  37.9 0.8 fusion.158
  39.4 1.1 convolution_bitcast_fusion.2
  40.5 1.0 copy.81
  41.5 10.5 %all-to-all-start.1 = ((f32[2,512,128]{2,0,1:T(2,128)}), f32[2,512,128]{2,0,1:T(2,128)S(1)}, u32[]{:S(2)}, u32[]{:S(2)}) async-start(f32[2,512,128]{2,0,1:T(2,128)} %copy.81), calls=%async_computation.1 | async-start | bytes 1048576 | tf_op jit(solution)/shard_map/all_to_all | solution.py:189
  52.1 0.7 convolution_bitcast_fusion.3
  52.8 0.9 multiply_add_fusion.5
  53.8 1.5 %fusion.16 = f32[2,64,8,256]{3,2,1,0:T(8,128)S(1)} fusion(f32[2,64,8,256]{3,1,2,0:T(8,128)S(1)} %pad_maximum_fusion, f32[128,128]{1,0:T(8,128)S(1)} %get-tuple-element.33, f32[128,128]{1,0:T(8,128)S(1)} %get-tuple-element.32, f32[128,128]{1,0:T(8,128)S(1)} %fusion.108), kind=kOutput, calls=%fused_computation.31 | convolution fusion | flops 805502976 | bytes 2293760 | tf_op jit(solution)/shard_map/fkaj,jm->fkam/dot_general | solution.py:113
  55.7 1.2 %fusion.11 = f32[2,64,8,256]{3,1,2,0:T(8,128)S(1)} fusion(f32[2,64,8,256]{3,2,1,0:T(8,128)S(1)} %pad_maximum_fusion.1, f32[128,128]{1,0:T(8,128)S(1)} %get-tuple-element.33, f32[128,128]{1,0:T(8,128)S(1)} %fusion.108, f32[128,128]{1,0:T(8,128)S(1)} %get-tuple-element.32), kind=kOutput, calls=%fused_computation.26 | convolution fusion | flops 805502976 | bytes 2293760 | tf_op jit(solution)/shard_map/fkam,mj->fkaj/dot_general | solution.py:139
  56.8 0.8 fusion.38
  57.6 0.8 fusion.5
  58.7 10.5 %all-to-all-done.1 = f32[2,512,128]{2,0,1:T(2,128)S(1)} async-done(((f32[2,512,128]{2,0,1:T(2,128)}), f32[2,512,128]{2,0,1:T(2,128)S(1)}, u32[]{:S(2)}, u32[]{:S(2)}) %all-to-all-start.1) | async-done | bytes 524320 | tf_op jit(solution)/shard_map/all_to_all | solution.py:189
  69.2 0.7 convolution_bitcast_fusion.1
  70.0 0.9 multiply_add_fusion.3
  70.9 1.5 %fusion.14 = f32[2,64,8,256]{3,2,1,0:T(8,128)S(1)} fusion(f32[2,64,8,256]{3,1,2,0:T(8,128)S(1)} %pad_maximum_fusion.2, f32[128,128]{1,0:T(8,128)S(1)} %get-tuple-element.33, f32[128,128]{1,0:T(8,128)S(1)} %get-tuple-element.32, f32[128,128]{1,0:T(8,128)S(1)} %fusion.108), kind=kOutput, calls=%fused_computation.29 | convolution fusion | flops 805502976 | bytes 2293760 | tf_op jit(solution)/shard_map/fkaj,jm->fkam/dot_general | solution.py:113
  72.8 1.2 %fusion.9 = f32[2,64,8,256]{3,1,2,0:T(8,128)S(1)} fusion(f32[2,64,8,256]{3,2,1,0:T(8,128)S(1)} %pad_maximum_fusion.3, f32[128,128]{1,0:T(8,128)S(1)} %get-tuple-element.33, f32[128,128]{1,0:T(8,128)S(1)} %fusion.108, f32[128,128]{1,0:T(8,128)S(1)} %get-tuple-element.32), kind=kOutput, calls=%fused_computation.24 | convolution fusion | flops 805502976 | bytes 2293760 | tf_op jit(solution)/shard_map/fkam,mj->fkaj/dot_general | solution.py:139
  74.0 1.0 fusion.30
  75.0 0.8 fusion.3
  76.2 0.7 copy.89
  76.9 34.8 %all_to_all.15 = f32[4,512,128]{2,0,1:T(4,128)S(1)} all-to-all(f32[4,512,128]{2,0,1:T(4,128)S(1)} %copy.89), channel_id=1, replica_groups=mesh['gx'=64,'gz'=4] {'gx'}, dimensions={1} | all-to-all | bytes 2097152 | tf_op jit(solution)/shard_map/all_to_all | solution.py:198
  111.6 1.9 %convolution_bitcast_fusion = f32[4,1,512,128]{2,3,0,1:T(8,128)S(1)} fusion(f32[512,512]{1,0:T(8,128)S(1)} %copy-done.1, f32[4,512,128]{2,0,1:T(4,128)S(1)} %all_to_all.15), kind=kOutput, calls=%fused_computation.2 | convolution fusion | flops 806092800 | bytes 3145728 | tf_op jit(solution)/shard_map/ya,fax->fyx/dot_general | solution.py:199
  113.5 1.3 %copy.91 = f32[4,1,512,128]{3,2,1,0:T(8,128)} copy(f32[4,1,512,128]{2,3,0,1:T(8,128)S(1)} %convolution_bitcast_fusion) | data formatting | bytes 2097152 | tf_op jit(solution)/shard_map/broadcast_in_dim | solution.py:200
  (40 shorter events, 4.8 us)
Async XLA Ops:
  0.0 0.8 copy-start.3
  0.8 23.3 %collective-permute-start.2 = (f32[3,4096]{1,0:T(4,128)S(1)}, f32[3,4096]{1,0:T(4,128)S(1)}, u32[]{:S(2)}, u32[]{:S(2)}) collective-permute-start(f32[3,4096]{1,0:T(4,128)S(1)} %pad_maximum_fusion.14), channel_id=1, source_target_pairs={{0,3},{1,0},{2,1},{3,2},{4,7},{5,4},{6,5},{7,6},{8,11},{9,8},{10,9... | collective-permute-start | bytes 147464 | tf_op jit(solution)/shard_map/ppermute | solution.py:175
  4.2 19.9 %collective-permute-start.1 = (f32[3,4096]{1,0:T(4,128)S(1)}, f32[3,4096]{1,0:T(4,128)S(1)}, u32[]{:S(2)}, u32[]{:S(2)}) collective-permute-start(f32[3,4096]{1,0:T(4,128)S(1)} %pad_maximum_fusion.14), channel_id=1, source_target_pairs={{0,2},{1,3},{2,0},{3,1},{4,6},{5,7},{6,4},{7,5},{8,10},{9,11},{10,... | collective-permute-start | bytes 147464 | tf_op jit(solution)/shard_map/ppermute | solution.py:175
  4.7 19.4 %collective-permute-start = (f32[3,4096]{1,0:T(4,128)S(1)}, f32[3,4096]{1,0:T(4,128)S(1)}, u32[]{:S(2)}, u32[]{:S(2)}) collective-permute-start(f32[3,4096]{1,0:T(4,128)S(1)} %pad_maximum_fusion.14), channel_id=1, source_target_pairs={{0,1},{1,2},{2,3},{3,0},{4,5},{5,6},{6,7},{7,4},{8,9},{9,10},{10,1... | collective-permute-start | bytes 147464 | tf_op jit(solution)/shard_map/ppermute | solution.py:175
  8.5 33.0 %all-to-all-start = ((f32[2,512,128]{2,0,1:T(2,128)}), f32[2,512,128]{2,0,1:T(2,128)S(1)}, u32[]{:S(2)}, u32[]{:S(2)}) async-start(f32[2,512,128]{2,0,1:T(2,128)} %copy.69), calls=%async_computation | async-start | bytes 1048576 | tf_op jit(solution)/shard_map/all_to_all | solution.py:187
  22.2 0.7 copy-start.4
  37.9 1.2 %copy-start = (f32[512,512]{1,0:T(8,128)S(1)}, f32[512,512]{1,0:T(8,128)}, u32[]{:S(2)}) copy-start(f32[512,512]{1,0:T(8,128)} %param.16) | copy-start | bytes 3145732
  37.9 1.5 %copy-start.2 = (f32[4,1,512,128]{3,2,1,0:T(8,128)S(1)}, f32[4,1,512,128]{3,2,1,0:T(8,128)}, u32[]{:S(2)}) copy-start(f32[4,1,512,128]{3,2,1,0:T(8,128)} %param.9) | copy-start | bytes 3145732
  41.5 27.6 %all-to-all-start.1 = ((f32[2,512,128]{2,0,1:T(2,128)}), f32[2,512,128]{2,0,1:T(2,128)S(1)}, u32[]{:S(2)}, u32[]{:S(2)}) async-start(f32[2,512,128]{2,0,1:T(2,128)} %copy.81), calls=%async_computation.1 | async-start | bytes 1048576 | tf_op jit(solution)/shard_map/all_to_all | solution.py:189
  76.8 34.8 %copy-start.1 = (f32[512,512]{1,0:T(8,128)S(1)}, f32[512,512]{1,0:T(8,128)}, u32[]{:S(2)}) copy-start(f32[512,512]{1,0:T(8,128)} %param.15) | copy-start | bytes 3145732

commit v10 on v9

--- a/solution.py
+++ b/solution.py
@@ -192,11 +192,17 @@
     eigen_here = lax.dynamic_slice_in_dim(wall_eigen, position * rows_here, rows_here)
     calm = fft_filter(calm, diffusivity[:2], eigen_here, bulk_shift, tables)
     calm, fed = lax.optimization_barrier((calm, fed))
+    calm = lax.all_to_all(calm, "gx", 1, 1, tiled=True)
     fed = fft_filter(fed, diffusivity[2:], eigen_here, bulk_shift, tables)
-    filtered = jnp.concatenate([calm, fed], axis=0)
-    filtered = filtered.reshape(field_count, row_count, slab_width)
-    gathered = lax.all_to_all(filtered, "gx", 1, 1, tiled=True)
-    result = jnp.einsum("ya,fax->fyx", identity + basis_part, gathered, precision=HI)
+    fed = lax.all_to_all(fed, "gx", 1, 1, tiled=True)
+    basis_full = identity + basis_part
+    result = jnp.concatenate(
+        [
+            jnp.einsum("ya,fax->fyx", basis_full, calm, precision=HI),
+            jnp.einsum("ya,fax->fyx", basis_full, fed, precision=HI),
+        ],
+        axis=0,
+    )
     return result[:, None]
 
 

time: 115 us -> 121 us (1.052)
  blocking collectives: 34.8 us -> 0 us
  waiting for transfers between devices: 10.5 us -> 36.3 us
  starting transfers between devices: 28.2 us -> 40.6 us
  local copies, waits for them, and re-layouts: 8.39 us -> 10.1 us
    all_to_all x1 -> x0, blocking collectives: 34.8 us -> none  [per_device(): gathered = lax.all_to_all(filtered, 'gx', 1, 1, tiled=True)]
    all_to_all x1 -> x2, waiting for transfers between devices: 10.5 us -> 26.9 us  [per_device(): fed = lax.all_to_all(fed, 'gx', 1, 1, tiled=True)]
    all_to_all x1 -> x2, waiting for transfers between devices: 0.01 us -> 9.42 us  [per_device(): calm = lax.all_to_all(calm, 'gx', 1, 1, tiled=True)]
    all_to_all x1 -> x2, starting transfers between devices: 13.2 us -> 19.5 us  [per_device(): calm = lax.all_to_all(calm, 'gx', 1, 1, tiled=True)]
    all_to_all x1 -> x2, starting transfers between devices: 10.5 us -> 16.6 us  [per_device(): fed = lax.all_to_all(fed, 'gx', 1, 1, tiled=True)]
  transfers between devices with their start and end apart: 5 -> 7, of which waited for: 1 -> 3; matrix products, arithmetic and copies ran while one was open for 15% -> 22% of each run, Pallas kernels for 10% -> 9%
where the time goes in v10:
time: 121 us; the launch traced here: 120 us
  starting transfers between devices  40.6 us (34%)
  waiting for transfers between devices  36.3 us (30%)
  matrix products  16.7 us (14%)
  Pallas kernels  11 us (9%)
  local copies, waits for them, and re-layouts  10.1 us (8%)
  other arithmetic  4.18 us (3%)
    all_to_all x2, waiting for transfers between devices, per_device(): fed = lax.all_to_all(fed, 'gx', 1, 1, tiled=True)  26.9 us
    all_to_all x2, starting transfers between devices, per_device(): calm = lax.all_to_all(calm, 'gx', 1, 1, tiled=True)  19.5 us
    all_to_all x2, starting transfers between devices, per_device(): fed = lax.all_to_all(fed, 'gx', 1, 1, tiled=True)  16.6 us
    pallas_call x1, Pallas kernels, drop_source(): pl.pallas_call(source_kernel, grid=(drops // chunk,), in_specs=[pl.BlockS...  11 us
    all_to_all x2, waiting for transfers between devices, per_device(): calm = lax.all_to_all(calm, 'gx', 1, 1, tiled=True)  9.42 us
    ppermute x3, starting transfers between devices, per_device(): lax.ppermute(packed, 'gz', [(i, (i + shift) % gz_count) for i in range(gz...  4.51 us
    dot_general x2, matrix products, fft_filter(): spec = jnp.einsum('fkaj,jm->fkam', joined, forward_table, precision=EXACT)  2.96 us
  transfers between devices with their start and end apart: 7, of which 3 were waited for; matrix products, arithmetic and copies ran while one was open for 22% of the time, Pallas kernels for 9%

profile of v10, /device:TPU:1, one launch (start us, length us, event | category | flops | bytes accessed | tf_op | source)
XLA Modules:
  0.0 120.1 jit_solution(15338897361962199088)
XLA Ops:
  0.8 3.4 %collective-permute-start.2 = (f32[3,4096]{1,0:T(4,128)S(1)}, f32[3,4096]{1,0:T(4,128)S(1)}, u32[]{:S(2)}, u32[]{:S(2)}) collective-permute-start(f32[3,4096]{1,0:T(4,128)S(1)} %pad_maximum_fusion.13), channel_id=1, source_target_pairs={{0,3},{1,0},{2,1},{3,2},{4,7},{5,4},{6,5},{7,6},{8,11},{9,8},{10,9... | collective-permute-start | bytes 147464 | tf_op jit(solution)/shard_map/ppermute | solution.py:175
  5.3 1.9 %convolution_bitcast_fusion.5 = f32[2,512,128]{2,1,0:T(8,128)S(1)} fusion(f32[512,512]{1,0:T(8,128)} %param.16, f32[4,1,512,128]{3,2,0,1:T(8,128)} %bitcast.108), kind=kOutput, calls=%fused_computation.11 | convolution fusion | flops 403439616 | bytes 2097152 | tf_op jit(solution)/shard_map/ay,fyx->fax/dot_general | solution.py:186
  7.3 1.2 %copy.71 = f32[2,512,128]{2,0,1:T(2,128)} copy(f32[2,512,128]{2,1,0:T(8,128)S(1)} %convolution_bitcast_fusion.5) | data formatting | bytes 1048576 | tf_op jit(solution)/shard_map/ay,fyx->fax/transpose | solution.py:186
  8.5 13.2 %all-to-all-start = ((f32[2,512,128]{2,0,1:T(2,128)}), f32[2,512,128]{2,0,1:T(2,128)S(1)}, u32[]{:S(2)}, u32[]{:S(2)}) async-start(f32[2,512,128]{2,0,1:T(2,128)} %copy.71), calls=%async_computation | async-start | bytes 1048576 | tf_op jit(solution)/shard_map/all_to_all | solution.py:187
  23.0 0.8 dynamic_slice.3
  26.2 11.0 %shard_map.91 = f32[512,512]{1,0:T(8,128)S(1)} custom-call(s32[1,16384]{1,0:T(1,128)S(1)} %and_select_fusion.2.row_ref, s32[1,16384]{1,0:T(1,128)S(1)} %get-tuple-element.13.col_ref, f32[4,16384]{1,0:T(4,128)S(1)} %reshape.144.piece_ref), custom_call_target="tpu_custom_call" | custom-call | flops 8589934592 | bytes 1048576 | tf_op jit(solution)/shard_map/pallas_call | solution.py:63
  37.9 0.8 fusion.160
  39.4 1.1 convolution_bitcast_fusion.3
  40.5 1.0 copy.83
  41.5 10.4 %all-to-all-start.1 = ((f32[2,512,128]{2,0,1:T(2,128)}), f32[2,512,128]{2,0,1:T(2,128)S(1)}, u32[]{:S(2)}, u32[]{:S(2)}) async-start(f32[2,512,128]{2,0,1:T(2,128)} %copy.83), calls=%async_computation.1 | async-start | bytes 1048576 | tf_op jit(solution)/shard_map/all_to_all | solution.py:189
  51.9 0.8 convolution_bitcast_fusion.4
  52.7 0.9 multiply_add_fusion.5
  53.6 1.5 %fusion.14 = f32[2,64,8,256]{3,2,1,0:T(8,128)S(1)} fusion(f32[2,64,8,256]{3,1,2,0:T(8,128)S(1)} %pad_maximum_fusion, f32[128,128]{1,0:T(8,128)S(1)} %get-tuple-element.33, f32[128,128]{1,0:T(8,128)S(1)} %get-tuple-element.32, f32[128,128]{1,0:T(8,128)S(1)} %fusion.110), kind=kOutput, calls=%fused_computation.31 | convolution fusion | flops 805502976 | bytes 2293760 | tf_op jit(solution)/shard_map/fkaj,jm->fkam/dot_general | solution.py:113
  55.5 1.2 fusion.10
  56.7 0.8 fusion.40
  57.5 0.8 fusion.5
  58.6 10.6 %all-to-all-done.1 = f32[2,512,128]{2,0,1:T(2,128)S(1)} async-done(((f32[2,512,128]{2,0,1:T(2,128)}), f32[2,512,128]{2,0,1:T(2,128)S(1)}, u32[]{:S(2)}, u32[]{:S(2)}) %all-to-all-start.1) | async-done | bytes 524320 | tf_op jit(solution)/shard_map/all_to_all | solution.py:189
  69.2 1.2 %copy.84 = f32[2,512,128]{2,0,1:T(2,128)} copy(f32[2,512,128]{2,1,0:T(8,128)S(1)} %bitcast.106) | data formatting | bytes 1048576 | tf_op jit(solution)/shard_map/optimization_barrier | solution.py:194
  70.4 6.3 %all-to-all-start.2 = ((f32[2,512,128]{2,0,1:T(2,128)}), f32[2,512,128]{2,0,1:T(2,128)S(1)}, u32[]{:S(2)}, u32[]{:S(2)}) async-start(f32[2,512,128]{2,0,1:T(2,128)} %copy.84), calls=%async_computation.2 | async-start | bytes 1048576 | tf_op jit(solution)/shard_map/all_to_all | solution.py:195
  76.7 0.8 convolution_bitcast_fusion.1
  77.5 0.9 multiply_add_fusion.3
  78.5 1.5 %fusion.12 = f32[2,64,8,256]{3,2,1,0:T(8,128)S(1)} fusion(f32[2,64,8,256]{3,1,2,0:T(8,128)S(1)} %pad_maximum_fusion.2, f32[128,128]{1,0:T(8,128)S(1)} %get-tuple-element.33, f32[128,128]{1,0:T(8,128)S(1)} %get-tuple-element.32, f32[128,128]{1,0:T(8,128)S(1)} %fusion.110), kind=kOutput, calls=%fused_computation.29 | convolution fusion | flops 805502976 | bytes 2293760 | tf_op jit(solution)/shard_map/fkaj,jm->fkam/dot_general | solution.py:113
  80.3 1.2 fusion.8
  81.5 0.8 fusion.32
  82.3 0.8 fusion.3
  83.4 1.2 copy.93
  84.6 9.4 %all-to-all-done.2 = f32[2,512,128]{2,0,1:T(2,128)S(1)} async-done(((f32[2,512,128]{2,0,1:T(2,128)}), f32[2,512,128]{2,0,1:T(2,128)S(1)}, u32[]{:S(2)}, u32[]{:S(2)}) %all-to-all-start.2) | async-done | bytes 524320 | tf_op jit(solution)/shard_map/all_to_all | solution.py:195
  94.0 6.3 %all-to-all-start.3 = ((f32[2,512,128]{2,0,1:T(2,128)}), f32[2,512,128]{2,0,1:T(2,128)S(1)}, u32[]{:S(2)}, u32[]{:S(2)}) async-start(f32[2,512,128]{2,0,1:T(2,128)} %copy.93), calls=%async_computation.3 | async-start | bytes 1048576 | tf_op jit(solution)/shard_map/all_to_all | solution.py:197
  100.3 1.0 convolution_bitcast_fusion.2
  101.4 16.3 %all-to-all-done.3 = f32[2,512,128]{2,0,1:T(2,128)S(1)} async-done(((f32[2,512,128]{2,0,1:T(2,128)}), f32[2,512,128]{2,0,1:T(2,128)S(1)}, u32[]{:S(2)}, u32[]{:S(2)}) %all-to-all-start.3) | async-done | bytes 524320 | tf_op jit(solution)/shard_map/all_to_all | solution.py:197
  117.6 1.0 convolution_bitcast_fusion
  118.8 1.3 %copy.95 = f32[4,1,512,128]{3,2,1,0:T(8,128)} copy(f32[4,1,512,128]{2,3,0,1:T(8,128)S(1)} %maximum_bitcast_fusion) | data formatting | bytes 2097152 | tf_op jit(solution)/shard_map/broadcast_in_dim | solution.py:206
  (45 shorter events, 7.9 us)
Async XLA Ops:
  0.0 0.8 copy-start.3
  0.8 23.3 %collective-permute-start.2 = (f32[3,4096]{1,0:T(4,128)S(1)}, f32[3,4096]{1,0:T(4,128)S(1)}, u32[]{:S(2)}, u32[]{:S(2)}) collective-permute-start(f32[3,4096]{1,0:T(4,128)S(1)} %pad_maximum_fusion.13), channel_id=1, source_target_pairs={{0,3},{1,0},{2,1},{3,2},{4,7},{5,4},{6,5},{7,6},{8,11},{9,8},{10,9... | collective-permute-start | bytes 147464 | tf_op jit(solution)/shard_map/ppermute | solution.py:175
  4.2 19.9 %collective-permute-start.1 = (f32[3,4096]{1,0:T(4,128)S(1)}, f32[3,4096]{1,0:T(4,128)S(1)}, u32[]{:S(2)}, u32[]{:S(2)}) collective-permute-start(f32[3,4096]{1,0:T(4,128)S(1)} %pad_maximum_fusion.13), channel_id=1, source_target_pairs={{0,2},{1,3},{2,0},{3,1},{4,6},{5,7},{6,4},{7,5},{8,10},{9,11},{10,... | collective-permute-start | bytes 147464 | tf_op jit(solution)/shard_map/ppermute | solution.py:175
  4.7 19.4 %collective-permute-start = (f32[3,4096]{1,0:T(4,128)S(1)}, f32[3,4096]{1,0:T(4,128)S(1)}, u32[]{:S(2)}, u32[]{:S(2)}) collective-permute-start(f32[3,4096]{1,0:T(4,128)S(1)} %pad_maximum_fusion.13), channel_id=1, source_target_pairs={{0,1},{1,2},{2,3},{3,0},{4,5},{5,6},{6,7},{7,4},{8,9},{9,10},{10,1... | collective-permute-start | bytes 147464 | tf_op jit(solution)/shard_map/ppermute | solution.py:175
  8.5 33.0 %all-to-all-start = ((f32[2,512,128]{2,0,1:T(2,128)}), f32[2,512,128]{2,0,1:T(2,128)S(1)}, u32[]{:S(2)}, u32[]{:S(2)}) async-start(f32[2,512,128]{2,0,1:T(2,128)} %copy.71), calls=%async_computation | async-start | bytes 1048576 | tf_op jit(solution)/shard_map/all_to_all | solution.py:187
  22.2 0.7 copy-start.4
  37.9 1.2 %copy-start = (f32[512,512]{1,0:T(8,128)S(1)}, f32[512,512]{1,0:T(8,128)}, u32[]{:S(2)}) copy-start(f32[512,512]{1,0:T(8,128)} %param.16) | copy-start | bytes 3145732
  37.9 1.5 %copy-start.2 = (f32[4,1,512,128]{3,2,1,0:T(8,128)S(1)}, f32[4,1,512,128]{3,2,1,0:T(8,128)}, u32[]{:S(2)}) copy-start(f32[4,1,512,128]{3,2,1,0:T(8,128)} %param.9) | copy-start | bytes 3145732
  41.5 27.7 %all-to-all-start.1 = ((f32[2,512,128]{2,0,1:T(2,128)}), f32[2,512,128]{2,0,1:T(2,128)S(1)}, u32[]{:S(2)}, u32[]{:S(2)}) async-start(f32[2,512,128]{2,0,1:T(2,128)} %copy.83), calls=%async_computation.1 | async-start | bytes 1048576 | tf_op jit(solution)/shard_map/all_to_all | solution.py:189
  70.4 23.6 %all-to-all-start.2 = ((f32[2,512,128]{2,0,1:T(2,128)}), f32[2,512,128]{2,0,1:T(2,128)S(1)}, u32[]{:S(2)}, u32[]{:S(2)}) async-start(f32[2,512,128]{2,0,1:T(2,128)} %copy.84), calls=%async_computation.2 | async-start | bytes 1048576 | tf_op jit(solution)/shard_map/all_to_all | solution.py:195
  83.4 16.9 %copy-start.1 = (f32[512,512]{1,0:T(8,128)S(1)}, f32[512,512]{1,0:T(8,128)}, u32[]{:S(2)}) copy-start(f32[512,512]{1,0:T(8,128)} %param.15) | copy-start | bytes 3145732
  94.0 23.6 %all-to-all-start.3 = ((f32[2,512,128]{2,0,1:T(2,128)}), f32[2,512,128]{2,0,1:T(2,128)S(1)}, u32[]{:S(2)}, u32[]{:S(2)}) async-start(f32[2,512,128]{2,0,1:T(2,128)} %copy.93), calls=%async_computation.3 | async-start | bytes 1048576 | tf_op jit(solution)/shard_map/all_to_all | solution.py:197

commit v11 on v9

--- a/solution.py
+++ b/solution.py
@@ -20,10 +20,10 @@
 CHUNK = 2048
 
 
-def source_kernel(row_ref, col_ref, piece_ref, out_ref):
+def source_kernel(row_ref, col_ref, piece_ref, field_ref, out_ref, acc_ref):
     step = pl.program_id(0)
-    row_count = out_ref.shape[0]
-    slab_width = out_ref.shape[1] // piece_ref.shape[0]
+    row_count = acc_ref.shape[0]
+    slab_width = out_ref.shape[2]
     chunk = row_ref.shape[1]
     rows = row_ref[...]
     cols = col_ref[...]
@@ -40,15 +40,25 @@
 
     @pl.when(step == 0)
     def _():
-        out_ref[...] = part
+        acc_ref[...] = part
 
     @pl.when(step > 0)
     def _():
-        out_ref[...] += part
-
-
-def drop_source(cells, rates, row_count, slab_width):
+        acc_ref[...] += part
+
+    @pl.when(step == pl.num_programs(0) - 1)
+    def _():
+        for c in range(out_ref.shape[0]):
+            total = field_ref[c, 0]
+            for p in range(PIECES):
+                start = (c * PIECES + p) * slab_width
+                total = total + acc_ref[:, start : start + slab_width]
+            out_ref[c] = total
+
+
+def drop_source(cells, rates, field):
     drops = cells.shape[0]
+    field_count, _, row_count, slab_width = field.shape
     pieces = []
     rest = rates
     for _ in range(PIECES):
@@ -60,26 +70,23 @@
     cols = (cells % slab_width).reshape(1, drops)
     width = 2 * PIECES * slab_width
     chunk = min(CHUNK, drops)
-    summed = pl.pallas_call(
+    return pl.pallas_call(
         source_kernel,
         grid=(drops // chunk,),
         in_specs=[
             pl.BlockSpec((1, chunk), lambda i: (0, i)),
             pl.BlockSpec((1, chunk), lambda i: (0, i)),
             pl.BlockSpec((2 * PIECES, chunk), lambda i: (0, i)),
+            pl.BlockSpec((2, 1, row_count, slab_width), lambda i: (1, 0, 0, 0)),
         ],
-        out_specs=pl.BlockSpec((row_count, width), lambda i: (0, 0)),
-        out_shape=jax.ShapeDtypeStruct((row_count, width), jnp.float32),
+        out_specs=pl.BlockSpec((2, row_count, slab_width), lambda i: (0, 0, 0)),
+        out_shape=jax.ShapeDtypeStruct((2, row_count, slab_width), jnp.float32),
+        scratch_shapes=[pltpu.VMEM((row_count, width), jnp.float32)],
         compiler_params=pltpu.CompilerParams(vmem_limit_bytes=48 * 1024 * 1024),
         cost_estimate=pl.CostEstimate(
             flops=2 * row_count * width * drops, transcendentals=0, bytes_accessed=4 * row_count * width
         ),
-    )(rows, cols, pieces)
-    summed = summed.reshape(row_count, 2, PIECES, slab_width)
-    total = summed[:, :, 0]
-    for p in range(1, PIECES):
-        total = total + summed[:, :, p]
-    return jnp.transpose(total, (1, 0, 2))
+    )(rows, cols, pieces, field)
 
 
 def dft_tables(gx_count, slab_width):
@@ -180,12 +187,12 @@
     cells = keys % plane_cells
     planes = keys // plane_cells
     rates = jnp.where((planes == plane_here)[None, :], packed[1:], 0.0)
-    source = drop_source(cells, rates, row_count, slab_width)
+    fed_side = drop_source(cells, rates, field)
     identity = jnp.eye(row_count, dtype=jnp.float32)
     dual_full = identity + dual_part
     calm = jnp.einsum("ay,fyx->fax", dual_full, field[:2, 0], precision=HI)
     calm = lax.all_to_all(calm, "gx", 1, 1, tiled=True)
-    fed = jnp.einsum("ay,fyx->fax", dual_full, field[2:, 0] + source, precision=HI)
+    fed = jnp.einsum("ay,fyx->fax", dual_full, fed_side, precision=HI)
     fed = lax.all_to_all(fed, "gx", 1, 1, tiled=True)
     tables = dft_tables(gx_count, slab_width)
     position = lax.axis_index("gx")

time: 115 us -> 114 us (level)
  local copies, waits for them, and re-layouts: 8.39 us -> 6.21 us
  starting transfers between devices: 28.2 us -> 29.4 us
    ppermute x3, starting transfers between devices: 4.51 us -> 5.72 us  [per_device(): lax.ppermute(packed, 'gz', [(i, (i + shift) % gz_count) for i in range(gz...]
  transfers between devices with their start and end apart: 5 -> 5, of which waited for: 1 -> 1; matrix products, arithmetic and copies ran while one was open for 15% -> 14% of each run, Pallas kernels for 10% -> 10%
where the time goes in v11:
time: 114 us
  blocking collectives  34.8 us (31%)
  starting transfers between devices  29.4 us (26%)
  matrix products  16.7 us (15%)
  Pallas kernels  11.2 us (10%)
  waiting for transfers between devices  10.5 us (9%)
  local copies, waits for them, and re-layouts  6.21 us (5%)
  other arithmetic  4.18 us (4%)
    all_to_all x1, blocking collectives, per_device(): gathered = lax.all_to_all(filtered, 'gx', 1, 1, tiled=True)  34.8 us
    all_to_all x1, starting transfers between devices, per_device(): calm = lax.all_to_all(calm, 'gx', 1, 1, tiled=True)  13.2 us
    pallas_call x1, Pallas kernels, drop_source(): pl.pallas_call(source_kernel, grid=(drops // chunk,), in_specs=[pl.BlockS...  11.2 us
    all_to_all x1, starting transfers between devices, per_device(): fed = lax.all_to_all(fed, 'gx', 1, 1, tiled=True)  10.5 us
    all_to_all x1, waiting for transfers between devices, per_device(): fed = lax.all_to_all(fed, 'gx', 1, 1, tiled=True)  10.5 us
    ppermute x3, starting transfers between devices, per_device(): lax.ppermute(packed, 'gz', [(i, (i + shift) % gz_count) for i in range(gz...  5.72 us
    dot_general x2, matrix products, fft_filter(): spec = jnp.einsum('fkaj,jm->fkam', joined, forward_table, precision=EXACT)  2.96 us
    dot_general x2, matrix products, fft_filter(): back = jnp.einsum('fkam,mj->fkaj', joined, inverse_table, precision=EXACT)  2.31 us
  transfers between devices with their start and end apart: 5, of which 1 were waited for; matrix products, arithmetic and copies ran while one was open for 14% of the time, Pallas kernels for 10%

profile of v11, /device:TPU:1, one launch (start us, length us, event | category | flops | bytes accessed | tf_op | source)
XLA Modules:
  0.0 113.9 jit_solution(9280109007290746170)
XLA Ops:
  0.0 0.7 add_convert_fusion
  0.8 2.1 %collective-permute-start = (f32[3,4096]{1,0:T(4,128)S(1)}, f32[3,4096]{1,0:T(4,128)S(1)}, u32[]{:S(2)}, u32[]{:S(2)}) collective-permute-start(f32[3,4096]{1,0:T(4,128)S(1)} %pad_maximum_fusion.14), channel_id=1, source_target_pairs={{0,1},{1,2},{2,3},{3,0},{4,5},{5,6},{6,7},{7,4},{8,9},{9,10},{10,1... | collective-permute-start | bytes 147464 | tf_op jit(solution)/shard_map/ppermute | solution.py:182
  2.9 2.5 %collective-permute-start.1 = (f32[3,4096]{1,0:T(4,128)S(1)}, f32[3,4096]{1,0:T(4,128)S(1)}, u32[]{:S(2)}, u32[]{:S(2)}) collective-permute-start(f32[3,4096]{1,0:T(4,128)S(1)} %pad_maximum_fusion.14), channel_id=1, source_target_pairs={{0,2},{1,3},{2,0},{3,1},{4,6},{5,7},{6,4},{7,5},{8,10},{9,11},{10,... | collective-permute-start | bytes 147464 | tf_op jit(solution)/shard_map/ppermute | solution.py:182
  5.4 1.2 %collective-permute-start.2 = (f32[3,4096]{1,0:T(4,128)S(1)}, f32[3,4096]{1,0:T(4,128)S(1)}, u32[]{:S(2)}, u32[]{:S(2)}) collective-permute-start(f32[3,4096]{1,0:T(4,128)S(1)} %pad_maximum_fusion.14), channel_id=1, source_target_pairs={{0,3},{1,0},{2,1},{3,2},{4,7},{5,4},{6,5},{7,6},{8,11},{9,8},{10,9... | collective-permute-start | bytes 147464 | tf_op jit(solution)/shard_map/ppermute | solution.py:182
  6.5 1.9 %convolution_bitcast_fusion.4 = f32[2,512,128]{2,1,0:T(8,128)S(1)} fusion(f32[512,512]{1,0:T(8,128)} %param.16, f32[4,1,512,128]{3,2,0,1:T(8,128)} %bitcast.88), kind=kOutput, calls=%fused_computation.10 | convolution fusion | flops 403439616 | bytes 2097152 | tf_op jit(solution)/shard_map/ay,fyx->fax/dot_general | solution.py:193
  8.5 1.2 %copy.63 = f32[2,512,128]{2,0,1:T(2,128)} copy(f32[2,512,128]{2,1,0:T(8,128)S(1)} %convolution_bitcast_fusion.4) | data formatting | bytes 1048576 | tf_op jit(solution)/shard_map/ay,fyx->fax/transpose | solution.py:193
  9.7 13.2 %all-to-all-start = ((f32[2,512,128]{2,0,1:T(2,128)}), f32[2,512,128]{2,0,1:T(2,128)S(1)}, u32[]{:S(2)}, u32[]{:S(2)}) async-start(f32[2,512,128]{2,0,1:T(2,128)} %copy.63), calls=%async_computation | async-start | bytes 1048576 | tf_op jit(solution)/shard_map/all_to_all | solution.py:194
  24.1 0.8 dynamic_slice.3
  25.4 0.5 compare_reduce_fusion
  27.0 0.3 and_select_fusion.2.row_ref
  27.4 11.2 %shard_map.91 = f32[2,512,128]{2,1,0:T(8,128)S(1)} custom-call(s32[1,16384]{1,0:T(1,128)S(1)} %and_select_fusion.2.row_ref, s32[1,16384]{1,0:T(1,128)S(1)} %get-tuple-element.13.col_ref, f32[4,16384]{1,0:T(4,128)S(1)} %reshape.140.piece_ref, f32[4,1,512,128]{3,2,1,0:T(8,128)S(1)} %copy-done), custom_call_target="tpu_custom_call" | custom-call | flops 8589934592 | bytes 1048576 | tf_op jit(solution)/shard_map/pallas_call | solution.py:73
  38.6 1.0 convolution_bitcast_fusion.2
  39.6 1.0 copy.73
  40.6 10.5 %all-to-all-start.1 = ((f32[2,512,128]{2,0,1:T(2,128)}), f32[2,512,128]{2,0,1:T(2,128)S(1)}, u32[]{:S(2)}, u32[]{:S(2)}) async-start(f32[2,512,128]{2,0,1:T(2,128)} %copy.73), calls=%async_computation.1 | async-start | bytes 1048576 | tf_op jit(solution)/shard_map/all_to_all | solution.py:196
  51.2 0.7 convolution_bitcast_fusion.3
  51.9 0.9 multiply_add_fusion.5
  52.9 1.5 %fusion.16 = f32[2,64,8,256]{3,2,1,0:T(8,128)S(1)} fusion(f32[2,64,8,256]{3,1,2,0:T(8,128)S(1)} %pad_maximum_fusion, f32[128,128]{1,0:T(8,128)S(1)} %get-tuple-element.31, f32[128,128]{1,0:T(8,128)S(1)} %get-tuple-element.30, f32[128,128]{1,0:T(8,128)S(1)} %fusion.102), kind=kOutput, calls=%fused_computation.31 | convolution fusion | flops 805502976 | bytes 2293760 | tf_op jit(solution)/shard_map/fkaj,jm->fkam/dot_general | solution.py:120
  54.4 0.3 multiply_subtract_fusion.4
  54.8 1.2 %fusion.11 = f32[2,64,8,256]{3,1,2,0:T(8,128)S(1)} fusion(f32[2,64,8,256]{3,2,1,0:T(8,128)S(1)} %pad_maximum_fusion.1, f32[128,128]{1,0:T(8,128)S(1)} %get-tuple-element.31, f32[128,128]{1,0:T(8,128)S(1)} %fusion.102, f32[128,128]{1,0:T(8,128)S(1)} %get-tuple-element.30), kind=kOutput, calls=%fused_computation.26 | convolution fusion | flops 805502976 | bytes 2293760 | tf_op jit(solution)/shard_map/fkam,mj->fkaj/dot_general | solution.py:146
  55.9 0.8 fusion.32
  56.7 0.8 fusion.5
  57.8 10.5 %all-to-all-done.1 = f32[2,512,128]{2,0,1:T(2,128)S(1)} async-done(((f32[2,512,128]{2,0,1:T(2,128)}), f32[2,512,128]{2,0,1:T(2,128)S(1)}, u32[]{:S(2)}, u32[]{:S(2)}) %all-to-all-start.1) | async-done | bytes 524320 | tf_op jit(solution)/shard_map/all_to_all | solution.py:196
  68.3 0.7 convolution_bitcast_fusion.1
  69.1 0.9 multiply_add_fusion.3
  70.0 1.5 %fusion.14 = f32[2,64,8,256]{3,2,1,0:T(8,128)S(1)} fusion(f32[2,64,8,256]{3,1,2,0:T(8,128)S(1)} %pad_maximum_fusion.2, f32[128,128]{1,0:T(8,128)S(1)} %get-tuple-element.31, f32[128,128]{1,0:T(8,128)S(1)} %get-tuple-element.30, f32[128,128]{1,0:T(8,128)S(1)} %fusion.102), kind=kOutput, calls=%fused_computation.29 | convolution fusion | flops 805502976 | bytes 2293760 | tf_op jit(solution)/shard_map/fkaj,jm->fkam/dot_general | solution.py:120
  71.9 1.2 %fusion.9 = f32[2,64,8,256]{3,1,2,0:T(8,128)S(1)} fusion(f32[2,64,8,256]{3,2,1,0:T(8,128)S(1)} %pad_maximum_fusion.3, f32[128,128]{1,0:T(8,128)S(1)} %get-tuple-element.31, f32[128,128]{1,0:T(8,128)S(1)} %fusion.102, f32[128,128]{1,0:T(8,128)S(1)} %get-tuple-element.30), kind=kOutput, calls=%fused_computation.24 | convolution fusion | flops 805502976 | bytes 2293760 | tf_op jit(solution)/shard_map/fkam,mj->fkaj/dot_general | solution.py:146
  73.1 1.0 fusion.25
  74.1 0.8 fusion.3
  75.3 0.7 copy.81
  76.0 34.8 %all_to_all.15 = f32[4,512,128]{2,0,1:T(4,128)S(1)} all-to-all(f32[4,512,128]{2,0,1:T(4,128)S(1)} %copy.81), channel_id=1, replica_groups=mesh['gx'=64,'gz'=4] {'gx'}, dimensions={1} | all-to-all | bytes 2097152 | tf_op jit(solution)/shard_map/all_to_all | solution.py:205
  110.8 1.9 %convolution_bitcast_fusion = f32[4,1,512,128]{2,3,0,1:T(8,128)S(1)} fusion(f32[512,512]{1,0:T(8,128)S(1)} %copy-done.2, f32[4,512,128]{2,0,1:T(4,128)S(1)} %all_to_all.15), kind=kOutput, calls=%fused_computation.2 | convolution fusion | flops 806092800 | bytes 3145728 | tf_op jit(solution)/shard_map/ya,fax->fyx/dot_general | solution.py:206
  112.6 1.3 %copy.83 = f32[4,1,512,128]{3,2,1,0:T(8,128)} copy(f32[4,1,512,128]{2,3,0,1:T(8,128)S(1)} %convolution_bitcast_fusion) | data formatting | bytes 2097152 | tf_op jit(solution)/shard_map/broadcast_in_dim | solution.py:207
  (38 shorter events, 3.5 us)
Async XLA Ops:
  0.0 0.8 copy-start.3
  0.8 24.5 %collective-permute-start = (f32[3,4096]{1,0:T(4,128)S(1)}, f32[3,4096]{1,0:T(4,128)S(1)}, u32[]{:S(2)}, u32[]{:S(2)}) collective-permute-start(f32[3,4096]{1,0:T(4,128)S(1)} %pad_maximum_fusion.14), channel_id=1, source_target_pairs={{0,1},{1,2},{2,3},{3,0},{4,5},{5,6},{6,7},{7,4},{8,9},{9,10},{10,1... | collective-permute-start | bytes 147464 | tf_op jit(solution)/shard_map/ppermute | solution.py:182
  2.9 22.4 %collective-permute-start.1 = (f32[3,4096]{1,0:T(4,128)S(1)}, f32[3,4096]{1,0:T(4,128)S(1)}, u32[]{:S(2)}, u32[]{:S(2)}) collective-permute-start(f32[3,4096]{1,0:T(4,128)S(1)} %pad_maximum_fusion.14), channel_id=1, source_target_pairs={{0,2},{1,3},{2,0},{3,1},{4,6},{5,7},{6,4},{7,5},{8,10},{9,11},{10,... | collective-permute-start | bytes 147464 | tf_op jit(solution)/shard_map/ppermute | solution.py:182
  5.4 20.0 %collective-permute-start.2 = (f32[3,4096]{1,0:T(4,128)S(1)}, f32[3,4096]{1,0:T(4,128)S(1)}, u32[]{:S(2)}, u32[]{:S(2)}) collective-permute-start(f32[3,4096]{1,0:T(4,128)S(1)} %pad_maximum_fusion.14), channel_id=1, source_target_pairs={{0,3},{1,0},{2,1},{3,2},{4,7},{5,4},{6,5},{7,6},{8,11},{9,8},{10,9... | collective-permute-start | bytes 147464 | tf_op jit(solution)/shard_map/ppermute | solution.py:182
  9.7 30.9 %all-to-all-start = ((f32[2,512,128]{2,0,1:T(2,128)}), f32[2,512,128]{2,0,1:T(2,128)S(1)}, u32[]{:S(2)}, u32[]{:S(2)}) async-start(f32[2,512,128]{2,0,1:T(2,128)} %copy.63), calls=%async_computation | async-start | bytes 1048576 | tf_op jit(solution)/shard_map/all_to_all | solution.py:194
  23.3 0.7 copy-start.4
  26.2 1.2 %copy-start = (f32[4,1,512,128]{3,2,1,0:T(8,128)S(1)}, f32[4,1,512,128]{3,2,1,0:T(8,128)}, u32[]{:S(2)}) copy-start(f32[4,1,512,128]{3,2,1,0:T(8,128)} %field_ref.1) | copy-start | bytes 3145732
  27.4 11.2 %copy-start.1 = (f32[512,512]{1,0:T(8,128)S(1)}, f32[512,512]{1,0:T(8,128)}, u32[]{:S(2)}) copy-start(f32[512,512]{1,0:T(8,128)} %param.16) | copy-start | bytes 3145732
  40.6 27.6 %all-to-all-start.1 = ((f32[2,512,128]{2,0,1:T(2,128)}), f32[2,512,128]{2,0,1:T(2,128)S(1)}, u32[]{:S(2)}, u32[]{:S(2)}) async-start(f32[2,512,128]{2,0,1:T(2,128)} %copy.73), calls=%async_computation.1 | async-start | bytes 1048576 | tf_op jit(solution)/shard_map/all_to_all | solution.py:196
  76.0 34.8 %copy-start.2 = (f32[512,512]{1,0:T(8,128)S(1)}, f32[512,512]{1,0:T(8,128)}, u32[]{:S(2)}) copy-start(f32[512,512]{1,0:T(8,128)} %param.15) | copy-start | bytes 3145732

commit v12 on v11

--- a/solution.py
+++ b/solution.py
@@ -17,7 +17,7 @@
 
 
 PIECES = 2
-CHUNK = 2048
+CHUNK = 16384
 
 
 def source_kernel(row_ref, col_ref, piece_ref, field_ref, out_ref, acc_ref):

time: 114 us -> 112 us (0.982)
  Pallas kernels: 11.2 us -> 8.83 us
  starting transfers between devices: 29.4 us -> 27.5 us
  waiting for transfers between devices: 10.5 us -> 12.3 us
    pallas_call x1, Pallas kernels: 11.2 us -> 8.83 us  [drop_source(): pl.pallas_call(source_kernel, grid=(drops // chunk,), in_specs=[pl.BlockS...]
    all_to_all x1, waiting for transfers between devices: 0.01 us -> 1.89 us  [per_device(): calm = lax.all_to_all(calm, 'gx', 1, 1, tiled=True)]
    all_to_all x1, starting transfers between devices: 10.5 us -> 8.64 us  [per_device(): fed = lax.all_to_all(fed, 'gx', 1, 1, tiled=True)]
  transfers between devices with their start and end apart: 5 -> 5, of which waited for: 1 -> 2; matrix products, arithmetic and copies ran while one was open for 14% -> 14% of each run, Pallas kernels for 10% -> 8%
where the time goes in v12:
time: 112 us
  blocking collectives  34.8 us (31%)
  starting transfers between devices  27.5 us (25%)
  matrix products  16.7 us (15%)
  waiting for transfers between devices  12.3 us (11%)
  Pallas kernels  8.83 us (8%)
  local copies, waits for them, and re-layouts  6.21 us (6%)
  other arithmetic  4.18 us (4%)
    all_to_all x1, blocking collectives, per_device(): gathered = lax.all_to_all(filtered, 'gx', 1, 1, tiled=True)  34.8 us
    all_to_all x1, starting transfers between devices, per_device(): calm = lax.all_to_all(calm, 'gx', 1, 1, tiled=True)  13.2 us
    all_to_all x1, waiting for transfers between devices, per_device(): fed = lax.all_to_all(fed, 'gx', 1, 1, tiled=True)  10.4 us
    pallas_call x1, Pallas kernels, drop_source(): pl.pallas_call(source_kernel, grid=(drops // chunk,), in_specs=[pl.BlockS...  8.83 us
    all_to_all x1, starting transfers between devices, per_device(): fed = lax.all_to_all(fed, 'gx', 1, 1, tiled=True)  8.64 us
    ppermute x3, starting transfers between devices, per_device(): lax.ppermute(packed, 'gz', [(i, (i + shift) % gz_count) for i in range(gz...  5.72 us
    dot_general x2, matrix products, fft_filter(): spec = jnp.einsum('fkaj,jm->fkam', joined, forward_table, precision=EXACT)  2.96 us
    dot_general x2, matrix products, fft_filter(): back = jnp.einsum('fkam,mj->fkaj', joined, inverse_table, precision=EXACT)  2.31 us
  transfers between devices with their start and end apart: 5, of which 2 were waited for; matrix products, arithmetic and copies ran while one was open for 14% of the time, Pallas kernels for 8%

profile of v12, /device:TPU:1, one launch (start us, length us, event | category | flops | bytes accessed | tf_op | source)
XLA Modules:
  0.0 111.6 jit_solution(11811653265361444552)
XLA Ops:
  0.0 0.7 add_convert_fusion
  0.8 2.1 %collective-permute-start = (f32[3,4096]{1,0:T(4,128)S(1)}, f32[3,4096]{1,0:T(4,128)S(1)}, u32[]{:S(2)}, u32[]{:S(2)}) collective-permute-start(f32[3,4096]{1,0:T(4,128)S(1)} %pad_maximum_fusion.14), channel_id=1, source_target_pairs={{0,1},{1,2},{2,3},{3,0},{4,5},{5,6},{6,7},{7,4},{8,9},{9,10},{10,1... | collective-permute-start | bytes 147464 | tf_op jit(solution)/shard_map/ppermute | solution.py:182
  2.9 2.5 %collective-permute-start.1 = (f32[3,4096]{1,0:T(4,128)S(1)}, f32[3,4096]{1,0:T(4,128)S(1)}, u32[]{:S(2)}, u32[]{:S(2)}) collective-permute-start(f32[3,4096]{1,0:T(4,128)S(1)} %pad_maximum_fusion.14), channel_id=1, source_target_pairs={{0,2},{1,3},{2,0},{3,1},{4,6},{5,7},{6,4},{7,5},{8,10},{9,11},{10,... | collective-permute-start | bytes 147464 | tf_op jit(solution)/shard_map/ppermute | solution.py:182
  5.4 1.2 %collective-permute-start.2 = (f32[3,4096]{1,0:T(4,128)S(1)}, f32[3,4096]{1,0:T(4,128)S(1)}, u32[]{:S(2)}, u32[]{:S(2)}) collective-permute-start(f32[3,4096]{1,0:T(4,128)S(1)} %pad_maximum_fusion.14), channel_id=1, source_target_pairs={{0,3},{1,0},{2,1},{3,2},{4,7},{5,4},{6,5},{7,6},{8,11},{9,8},{10,9... | collective-permute-start | bytes 147464 | tf_op jit(solution)/shard_map/ppermute | solution.py:182
  6.5 1.9 %convolution_bitcast_fusion.4 = f32[2,512,128]{2,1,0:T(8,128)S(1)} fusion(f32[512,512]{1,0:T(8,128)} %param.16, f32[4,1,512,128]{3,2,0,1:T(8,128)} %bitcast.88), kind=kOutput, calls=%fused_computation.10 | convolution fusion | flops 403439616 | bytes 2097152 | tf_op jit(solution)/shard_map/ay,fyx->fax/dot_general | solution.py:193
  8.5 1.2 %copy.63 = f32[2,512,128]{2,0,1:T(2,128)} copy(f32[2,512,128]{2,1,0:T(8,128)S(1)} %convolution_bitcast_fusion.4) | data formatting | bytes 1048576 | tf_op jit(solution)/shard_map/ay,fyx->fax/transpose | solution.py:193
  9.7 13.2 %all-to-all-start = ((f32[2,512,128]{2,0,1:T(2,128)}), f32[2,512,128]{2,0,1:T(2,128)S(1)}, u32[]{:S(2)}, u32[]{:S(2)}) async-start(f32[2,512,128]{2,0,1:T(2,128)} %copy.63), calls=%async_computation | async-start | bytes 1048576 | tf_op jit(solution)/shard_map/all_to_all | solution.py:194
  24.1 0.8 dynamic_slice.3
  25.4 0.5 compare_reduce_fusion
  27.0 0.3 and_select_fusion.2.row_ref
  27.4 8.8 %shard_map.91 = f32[2,512,128]{2,1,0:T(8,128)S(1)} custom-call(s32[1,16384]{1,0:T(1,128)S(1)} %and_select_fusion.2.row_ref, s32[1,16384]{1,0:T(1,128)S(1)} %get-tuple-element.13.col_ref, f32[4,16384]{1,0:T(4,128)S(1)} %reshape.140.piece_ref, f32[4,1,512,128]{3,2,1,0:T(8,128)S(1)} %copy-done), custom_call_target="tpu_custom_call" | custom-call | flops 8589934592 | bytes 1048576 | tf_op jit(solution)/shard_map/pallas_call | solution.py:73
  36.3 1.1 convolution_bitcast_fusion.2
  37.3 1.0 copy.73
  38.3 1.9 %all-to-all-done = f32[2,512,128]{2,0,1:T(2,128)S(1)} async-done(((f32[2,512,128]{2,0,1:T(2,128)}), f32[2,512,128]{2,0,1:T(2,128)S(1)}, u32[]{:S(2)}, u32[]{:S(2)}) %all-to-all-start) | async-done | bytes 524320 | tf_op jit(solution)/shard_map/all_to_all | solution.py:194
  40.2 8.6 %all-to-all-start.1 = ((f32[2,512,128]{2,0,1:T(2,128)}), f32[2,512,128]{2,0,1:T(2,128)S(1)}, u32[]{:S(2)}, u32[]{:S(2)}) async-start(f32[2,512,128]{2,0,1:T(2,128)} %copy.73), calls=%async_computation.1 | async-start | bytes 1048576 | tf_op jit(solution)/shard_map/all_to_all | solution.py:196
  48.9 0.8 convolution_bitcast_fusion.3
  49.7 0.9 multiply_add_fusion.5
  50.6 1.5 %fusion.16 = f32[2,64,8,256]{3,2,1,0:T(8,128)S(1)} fusion(f32[2,64,8,256]{3,1,2,0:T(8,128)S(1)} %pad_maximum_fusion, f32[128,128]{1,0:T(8,128)S(1)} %get-tuple-element.31, f32[128,128]{1,0:T(8,128)S(1)} %get-tuple-element.30, f32[128,128]{1,0:T(8,128)S(1)} %fusion.102), kind=kOutput, calls=%fused_computation.31 | convolution fusion | flops 805502976 | bytes 2293760 | tf_op jit(solution)/shard_map/fkaj,jm->fkam/dot_general | solution.py:120
  52.5 1.2 %fusion.11 = f32[2,64,8,256]{3,1,2,0:T(8,128)S(1)} fusion(f32[2,64,8,256]{3,2,1,0:T(8,128)S(1)} %pad_maximum_fusion.1, f32[128,128]{1,0:T(8,128)S(1)} %get-tuple-element.31, f32[128,128]{1,0:T(8,128)S(1)} %fusion.102, f32[128,128]{1,0:T(8,128)S(1)} %get-tuple-element.30), kind=kOutput, calls=%fused_computation.26 | convolution fusion | flops 805502976 | bytes 2293760 | tf_op jit(solution)/shard_map/fkam,mj->fkaj/dot_general | solution.py:146
  53.6 0.8 fusion.32
  54.4 0.8 fusion.5
  55.5 10.4 %all-to-all-done.1 = f32[2,512,128]{2,0,1:T(2,128)S(1)} async-done(((f32[2,512,128]{2,0,1:T(2,128)}), f32[2,512,128]{2,0,1:T(2,128)S(1)}, u32[]{:S(2)}, u32[]{:S(2)}) %all-to-all-start.1) | async-done | bytes 524320 | tf_op jit(solution)/shard_map/all_to_all | solution.py:196
  66.0 0.7 convolution_bitcast_fusion.1
  66.7 0.9 multiply_add_fusion.3
  67.7 1.5 %fusion.14 = f32[2,64,8,256]{3,2,1,0:T(8,128)S(1)} fusion(f32[2,64,8,256]{3,1,2,0:T(8,128)S(1)} %pad_maximum_fusion.2, f32[128,128]{1,0:T(8,128)S(1)} %get-tuple-element.31, f32[128,128]{1,0:T(8,128)S(1)} %get-tuple-element.30, f32[128,128]{1,0:T(8,128)S(1)} %fusion.102), kind=kOutput, calls=%fused_computation.29 | convolution fusion | flops 805502976 | bytes 2293760 | tf_op jit(solution)/shard_map/fkaj,jm->fkam/dot_general | solution.py:120
  69.6 1.2 %fusion.9 = f32[2,64,8,256]{3,1,2,0:T(8,128)S(1)} fusion(f32[2,64,8,256]{3,2,1,0:T(8,128)S(1)} %pad_maximum_fusion.3, f32[128,128]{1,0:T(8,128)S(1)} %get-tuple-element.31, f32[128,128]{1,0:T(8,128)S(1)} %fusion.102, f32[128,128]{1,0:T(8,128)S(1)} %get-tuple-element.30), kind=kOutput, calls=%fused_computation.24 | convolution fusion | flops 805502976 | bytes 2293760 | tf_op jit(solution)/shard_map/fkam,mj->fkaj/dot_general | solution.py:146
  70.7 1.0 fusion.25
  71.8 0.8 fusion.3
  73.0 0.7 copy.81
  73.7 34.8 %all_to_all.15 = f32[4,512,128]{2,0,1:T(4,128)S(1)} all-to-all(f32[4,512,128]{2,0,1:T(4,128)S(1)} %copy.81), channel_id=1, replica_groups=mesh['gx'=64,'gz'=4] {'gx'}, dimensions={1} | all-to-all | bytes 2097152 | tf_op jit(solution)/shard_map/all_to_all | solution.py:205
  108.5 1.9 %convolution_bitcast_fusion = f32[4,1,512,128]{2,3,0,1:T(8,128)S(1)} fusion(f32[512,512]{1,0:T(8,128)S(1)} %copy-done.2, f32[4,512,128]{2,0,1:T(4,128)S(1)} %all_to_all.15), kind=kOutput, calls=%fused_computation.2 | convolution fusion | flops 806092800 | bytes 3145728 | tf_op jit(solution)/shard_map/ya,fax->fyx/dot_general | solution.py:206
  110.3 1.3 %copy.83 = f32[4,1,512,128]{3,2,1,0:T(8,128)} copy(f32[4,1,512,128]{2,3,0,1:T(8,128)S(1)} %convolution_bitcast_fusion) | data formatting | bytes 2097152 | tf_op jit(solution)/shard_map/broadcast_in_dim | solution.py:207
  (38 shorter events, 3.8 us)
Async XLA Ops:
  0.0 0.8 copy-start.3
  0.8 24.5 %collective-permute-start = (f32[3,4096]{1,0:T(4,128)S(1)}, f32[3,4096]{1,0:T(4,128)S(1)}, u32[]{:S(2)}, u32[]{:S(2)}) collective-permute-start(f32[3,4096]{1,0:T(4,128)S(1)} %pad_maximum_fusion.14), channel_id=1, source_target_pairs={{0,1},{1,2},{2,3},{3,0},{4,5},{5,6},{6,7},{7,4},{8,9},{9,10},{10,1... | collective-permute-start | bytes 147464 | tf_op jit(solution)/shard_map/ppermute | solution.py:182
  2.9 22.4 %collective-permute-start.1 = (f32[3,4096]{1,0:T(4,128)S(1)}, f32[3,4096]{1,0:T(4,128)S(1)}, u32[]{:S(2)}, u32[]{:S(2)}) collective-permute-start(f32[3,4096]{1,0:T(4,128)S(1)} %pad_maximum_fusion.14), channel_id=1, source_target_pairs={{0,2},{1,3},{2,0},{3,1},{4,6},{5,7},{6,4},{7,5},{8,10},{9,11},{10,... | collective-permute-start | bytes 147464 | tf_op jit(solution)/shard_map/ppermute | solution.py:182
  5.4 20.0 %collective-permute-start.2 = (f32[3,4096]{1,0:T(4,128)S(1)}, f32[3,4096]{1,0:T(4,128)S(1)}, u32[]{:S(2)}, u32[]{:S(2)}) collective-permute-start(f32[3,4096]{1,0:T(4,128)S(1)} %pad_maximum_fusion.14), channel_id=1, source_target_pairs={{0,3},{1,0},{2,1},{3,2},{4,7},{5,4},{6,5},{7,6},{8,11},{9,8},{10,9... | collective-permute-start | bytes 147464 | tf_op jit(solution)/shard_map/ppermute | solution.py:182
  9.7 30.5 %all-to-all-start = ((f32[2,512,128]{2,0,1:T(2,128)}), f32[2,512,128]{2,0,1:T(2,128)S(1)}, u32[]{:S(2)}, u32[]{:S(2)}) async-start(f32[2,512,128]{2,0,1:T(2,128)} %copy.63), calls=%async_computation | async-start | bytes 1048576 | tf_op jit(solution)/shard_map/all_to_all | solution.py:194
  23.3 0.7 copy-start.4
  26.2 1.2 %copy-start = (f32[4,1,512,128]{3,2,1,0:T(8,128)S(1)}, f32[4,1,512,128]{3,2,1,0:T(8,128)}, u32[]{:S(2)}) copy-start(f32[4,1,512,128]{3,2,1,0:T(8,128)} %field_ref.1) | copy-start | bytes 3145732
  27.4 8.8 %copy-start.1 = (f32[512,512]{1,0:T(8,128)S(1)}, f32[512,512]{1,0:T(8,128)}, u32[]{:S(2)}) copy-start(f32[512,512]{1,0:T(8,128)} %param.16) | copy-start | bytes 3145732
  40.2 25.8 %all-to-all-start.1 = ((f32[2,512,128]{2,0,1:T(2,128)}), f32[2,512,128]{2,0,1:T(2,128)S(1)}, u32[]{:S(2)}, u32[]{:S(2)}) async-start(f32[2,512,128]{2,0,1:T(2,128)} %copy.73), calls=%async_computation.1 | async-start | bytes 1048576 | tf_op jit(solution)/shard_map/all_to_all | solution.py:196
  73.7 34.8 %copy-start.2 = (f32[512,512]{1,0:T(8,128)S(1)}, f32[512,512]{1,0:T(8,128)}, u32[]{:S(2)}) copy-start(f32[512,512]{1,0:T(8,128)} %param.15) | copy-start | bytes 3145732

commit v13 on v12

--- a/solution.py
+++ b/solution.py
@@ -203,7 +203,7 @@
     filtered = jnp.concatenate([calm, fed], axis=0)
     filtered = filtered.reshape(field_count, row_count, slab_width)
     gathered = lax.all_to_all(filtered, "gx", 1, 1, tiled=True)
-    result = jnp.einsum("ya,fax->fyx", identity + basis_part, gathered, precision=HI)
+    result = jnp.einsum("fax,ya->fyx", gathered, identity + basis_part, precision=HI)
     return result[:, None]
 
 

time: 112 us -> 111 us (level)
  local copies, waits for them, and re-layouts: 6.21 us -> 4.91 us
    broadcast_in_dim x1 -> x0, local copies, waits for them, and re-layouts: 1.31 us -> none  [per_device(): return result[:, None]]
where the time goes in v13:
time: 111 us; the launch traced here: 110 us
  blocking collectives  34.8 us (31%)
  starting transfers between devices  27.5 us (25%)
  matrix products  16.9 us (15%)
  waiting for transfers between devices  12.3 us (11%)
  Pallas kernels  8.83 us (8%)
  local copies, waits for them, and re-layouts  4.91 us (4%)
  other arithmetic  4.18 us (4%)
    all_to_all x1, blocking collectives, per_device(): gathered = lax.all_to_all(filtered, 'gx', 1, 1, tiled=True)  34.8 us
    all_to_all x1, starting transfers between devices, per_device(): calm = lax.all_to_all(calm, 'gx', 1, 1, tiled=True)  13.2 us
    all_to_all x1, waiting for transfers between devices, per_device(): fed = lax.all_to_all(fed, 'gx', 1, 1, tiled=True)  10.4 us
    pallas_call x1, Pallas kernels, drop_source(): pl.pallas_call(source_kernel, grid=(drops // chunk,), in_specs=[pl.BlockS...  8.83 us
    all_to_all x1, starting transfers between devices, per_device(): fed = lax.all_to_all(fed, 'gx', 1, 1, tiled=True)  8.64 us
    ppermute x3, starting transfers between devices, per_device(): lax.ppermute(packed, 'gz', [(i, (i + shift) % gz_count) for i in range(gz...  5.72 us
    dot_general x2, matrix products, fft_filter(): spec = jnp.einsum('fkaj,jm->fkam', joined, forward_table, precision=EXACT)  2.96 us
    dot_general x2, matrix products, fft_filter(): back = jnp.einsum('fkam,mj->fkaj', joined, inverse_table, precision=EXACT)  2.31 us
  transfers between devices with their start and end apart: 5, of which 2 were waited for; matrix products, arithmetic and copies ran while one was open for 14% of the time, Pallas kernels for 8%

profile of v13, /device:TPU:1, one launch (start us, length us, event | category | flops | bytes accessed | tf_op | source)
XLA Modules:
  0.0 110.5 jit_solution(5797186572744695615)
XLA Ops:
  0.0 0.7 add_convert_fusion
  0.8 2.1 %collective-permute-start = (f32[3,4096]{1,0:T(4,128)S(1)}, f32[3,4096]{1,0:T(4,128)S(1)}, u32[]{:S(2)}, u32[]{:S(2)}) collective-permute-start(f32[3,4096]{1,0:T(4,128)S(1)} %pad_maximum_fusion.14), channel_id=1, source_target_pairs={{0,1},{1,2},{2,3},{3,0},{4,5},{5,6},{6,7},{7,4},{8,9},{9,10},{10,1... | collective-permute-start | bytes 147464 | tf_op jit(solution)/shard_map/ppermute | solution.py:182
  2.9 2.5 %collective-permute-start.1 = (f32[3,4096]{1,0:T(4,128)S(1)}, f32[3,4096]{1,0:T(4,128)S(1)}, u32[]{:S(2)}, u32[]{:S(2)}) collective-permute-start(f32[3,4096]{1,0:T(4,128)S(1)} %pad_maximum_fusion.14), channel_id=1, source_target_pairs={{0,2},{1,3},{2,0},{3,1},{4,6},{5,7},{6,4},{7,5},{8,10},{9,11},{10,... | collective-permute-start | bytes 147464 | tf_op jit(solution)/shard_map/ppermute | solution.py:182
  5.4 1.2 %collective-permute-start.2 = (f32[3,4096]{1,0:T(4,128)S(1)}, f32[3,4096]{1,0:T(4,128)S(1)}, u32[]{:S(2)}, u32[]{:S(2)}) collective-permute-start(f32[3,4096]{1,0:T(4,128)S(1)} %pad_maximum_fusion.14), channel_id=1, source_target_pairs={{0,3},{1,0},{2,1},{3,2},{4,7},{5,4},{6,5},{7,6},{8,11},{9,8},{10,9... | collective-permute-start | bytes 147464 | tf_op jit(solution)/shard_map/ppermute | solution.py:182
  6.5 1.9 %convolution_bitcast_fusion.4 = f32[2,512,128]{2,1,0:T(8,128)S(1)} fusion(f32[512,512]{1,0:T(8,128)} %param.16, f32[4,1,512,128]{3,2,0,1:T(8,128)} %bitcast.90), kind=kOutput, calls=%fused_computation.10 | convolution fusion | flops 403439616 | bytes 2097152 | tf_op jit(solution)/shard_map/ay,fyx->fax/dot_general | solution.py:193
  8.5 1.2 %copy.61 = f32[2,512,128]{2,0,1:T(2,128)} copy(f32[2,512,128]{2,1,0:T(8,128)S(1)} %convolution_bitcast_fusion.4) | data formatting | bytes 1048576 | tf_op jit(solution)/shard_map/ay,fyx->fax/transpose | solution.py:193
  9.7 13.2 %all-to-all-start = ((f32[2,512,128]{2,0,1:T(2,128)}), f32[2,512,128]{2,0,1:T(2,128)S(1)}, u32[]{:S(2)}, u32[]{:S(2)}) async-start(f32[2,512,128]{2,0,1:T(2,128)} %copy.61), calls=%async_computation | async-start | bytes 1048576 | tf_op jit(solution)/shard_map/all_to_all | solution.py:194
  24.1 0.8 dynamic_slice.3
  25.4 0.5 compare_reduce_fusion
  27.0 0.3 and_select_fusion.2.row_ref
  27.4 8.8 %shard_map.91 = f32[2,512,128]{2,1,0:T(8,128)S(1)} custom-call(s32[1,16384]{1,0:T(1,128)S(1)} %and_select_fusion.2.row_ref, s32[1,16384]{1,0:T(1,128)S(1)} %get-tuple-element.13.col_ref, f32[4,16384]{1,0:T(4,128)S(1)} %reshape.140.piece_ref, f32[4,1,512,128]{3,2,1,0:T(8,128)S(1)} %copy-done), custom_call_target="tpu_custom_call" | custom-call | flops 8589934592 | bytes 1048576 | tf_op jit(solution)/shard_map/pallas_call | solution.py:73
  36.3 1.1 convolution_bitcast_fusion.2
  37.3 1.0 copy.71
  38.3 1.9 %all-to-all-done = f32[2,512,128]{2,0,1:T(2,128)S(1)} async-done(((f32[2,512,128]{2,0,1:T(2,128)}), f32[2,512,128]{2,0,1:T(2,128)S(1)}, u32[]{:S(2)}, u32[]{:S(2)}) %all-to-all-start) | async-done | bytes 524320 | tf_op jit(solution)/shard_map/all_to_all | solution.py:194
  40.2 8.6 %all-to-all-start.1 = ((f32[2,512,128]{2,0,1:T(2,128)}), f32[2,512,128]{2,0,1:T(2,128)S(1)}, u32[]{:S(2)}, u32[]{:S(2)}) async-start(f32[2,512,128]{2,0,1:T(2,128)} %copy.71), calls=%async_computation.1 | async-start | bytes 1048576 | tf_op jit(solution)/shard_map/all_to_all | solution.py:196
  48.9 0.8 convolution_bitcast_fusion.3
  49.7 0.9 multiply_add_fusion.5
  50.6 1.5 %fusion.16 = f32[2,64,8,256]{3,2,1,0:T(8,128)S(1)} fusion(f32[2,64,8,256]{3,1,2,0:T(8,128)S(1)} %pad_maximum_fusion, f32[128,128]{1,0:T(8,128)S(1)} %get-tuple-element.31, f32[128,128]{1,0:T(8,128)S(1)} %get-tuple-element.30, f32[128,128]{1,0:T(8,128)S(1)} %fusion.102), kind=kOutput, calls=%fused_computation.31 | convolution fusion | flops 805502976 | bytes 2293760 | tf_op jit(solution)/shard_map/fkaj,jm->fkam/dot_general | solution.py:120
  52.1 0.3 multiply_subtract_fusion.4
  52.5 1.2 %fusion.11 = f32[2,64,8,256]{3,1,2,0:T(8,128)S(1)} fusion(f32[2,64,8,256]{3,2,1,0:T(8,128)S(1)} %pad_maximum_fusion.1, f32[128,128]{1,0:T(8,128)S(1)} %get-tuple-element.31, f32[128,128]{1,0:T(8,128)S(1)} %fusion.102, f32[128,128]{1,0:T(8,128)S(1)} %get-tuple-element.30), kind=kOutput, calls=%fused_computation.26 | convolution fusion | flops 805502976 | bytes 2293760 | tf_op jit(solution)/shard_map/fkam,mj->fkaj/dot_general | solution.py:146
  53.6 0.8 fusion.32
  54.4 0.8 fusion.5
  55.5 10.4 %all-to-all-done.1 = f32[2,512,128]{2,0,1:T(2,128)S(1)} async-done(((f32[2,512,128]{2,0,1:T(2,128)}), f32[2,512,128]{2,0,1:T(2,128)S(1)}, u32[]{:S(2)}, u32[]{:S(2)}) %all-to-all-start.1) | async-done | bytes 524320 | tf_op jit(solution)/shard_map/all_to_all | solution.py:196
  66.0 0.7 convolution_bitcast_fusion.1
  66.7 0.9 multiply_add_fusion.3
  67.7 1.5 %fusion.14 = f32[2,64,8,256]{3,2,1,0:T(8,128)S(1)} fusion(f32[2,64,8,256]{3,1,2,0:T(8,128)S(1)} %pad_maximum_fusion.2, f32[128,128]{1,0:T(8,128)S(1)} %get-tuple-element.31, f32[128,128]{1,0:T(8,128)S(1)} %get-tuple-element.30, f32[128,128]{1,0:T(8,128)S(1)} %fusion.102), kind=kOutput, calls=%fused_computation.29 | convolution fusion | flops 805502976 | bytes 2293760 | tf_op jit(solution)/shard_map/fkaj,jm->fkam/dot_general | solution.py:120
  69.6 1.2 %fusion.9 = f32[2,64,8,256]{3,1,2,0:T(8,128)S(1)} fusion(f32[2,64,8,256]{3,2,1,0:T(8,128)S(1)} %pad_maximum_fusion.3, f32[128,128]{1,0:T(8,128)S(1)} %get-tuple-element.31, f32[128,128]{1,0:T(8,128)S(1)} %fusion.102, f32[128,128]{1,0:T(8,128)S(1)} %get-tuple-element.30), kind=kOutput, calls=%fused_computation.24 | convolution fusion | flops 805502976 | bytes 2293760 | tf_op jit(solution)/shard_map/fkam,mj->fkaj/dot_general | solution.py:146
  70.7 1.0 fusion.25
  71.8 0.8 fusion.3
  73.0 0.7 copy.79
  73.7 34.8 %all_to_all.15 = f32[4,512,128]{2,0,1:T(4,128)S(1)} all-to-all(f32[4,512,128]{2,0,1:T(4,128)S(1)} %copy.79), channel_id=1, replica_groups=mesh['gx'=64,'gz'=4] {'gx'}, dimensions={1} | all-to-all | bytes 2097152 | tf_op jit(solution)/shard_map/all_to_all | solution.py:205
  108.5 2.0 %convolution_bitcast_fusion = f32[4,1,512,128]{3,2,1,0:T(8,128)} fusion(f32[512,512]{1,0:T(8,128)S(1)} %copy-done.2, f32[4,512,128]{2,0,1:T(4,128)S(1)} %all_to_all.15), kind=kOutput, calls=%fused_computation.2 | convolution fusion | flops 806092800 | bytes 3145728 | tf_op jit(solution)/shard_map/fax,ya->fyx/dot_general | solution.py:206
  (37 shorter events, 3.5 us)
Async XLA Ops:
  0.0 0.8 copy-start.3
  0.8 24.5 %collective-permute-start = (f32[3,4096]{1,0:T(4,128)S(1)}, f32[3,4096]{1,0:T(4,128)S(1)}, u32[]{:S(2)}, u32[]{:S(2)}) collective-permute-start(f32[3,4096]{1,0:T(4,128)S(1)} %pad_maximum_fusion.14), channel_id=1, source_target_pairs={{0,1},{1,2},{2,3},{3,0},{4,5},{5,6},{6,7},{7,4},{8,9},{9,10},{10,1... | collective-permute-start | bytes 147464 | tf_op jit(solution)/shard_map/ppermute | solution.py:182
  2.9 22.4 %collective-permute-start.1 = (f32[3,4096]{1,0:T(4,128)S(1)}, f32[3,4096]{1,0:T(4,128)S(1)}, u32[]{:S(2)}, u32[]{:S(2)}) collective-permute-start(f32[3,4096]{1,0:T(4,128)S(1)} %pad_maximum_fusion.14), channel_id=1, source_target_pairs={{0,2},{1,3},{2,0},{3,1},{4,6},{5,7},{6,4},{7,5},{8,10},{9,11},{10,... | collective-permute-start | bytes 147464 | tf_op jit(solution)/shard_map/ppermute | solution.py:182
  5.4 20.0 %collective-permute-start.2 = (f32[3,4096]{1,0:T(4,128)S(1)}, f32[3,4096]{1,0:T(4,128)S(1)}, u32[]{:S(2)}, u32[]{:S(2)}) collective-permute-start(f32[3,4096]{1,0:T(4,128)S(1)} %pad_maximum_fusion.14), channel_id=1, source_target_pairs={{0,3},{1,0},{2,1},{3,2},{4,7},{5,4},{6,5},{7,6},{8,11},{9,8},{10,9... | collective-permute-start | bytes 147464 | tf_op jit(solution)/shard_map/ppermute | solution.py:182
  9.7 30.5 %all-to-all-start = ((f32[2,512,128]{2,0,1:T(2,128)}), f32[2,512,128]{2,0,1:T(2,128)S(1)}, u32[]{:S(2)}, u32[]{:S(2)}) async-start(f32[2,512,128]{2,0,1:T(2,128)} %copy.61), calls=%async_computation | async-start | bytes 1048576 | tf_op jit(solution)/shard_map/all_to_all | solution.py:194
  23.3 0.7 copy-start.4
  26.2 1.2 %copy-start = (f32[4,1,512,128]{3,2,1,0:T(8,128)S(1)}, f32[4,1,512,128]{3,2,1,0:T(8,128)}, u32[]{:S(2)}) copy-start(f32[4,1,512,128]{3,2,1,0:T(8,128)} %field_ref.1) | copy-start | bytes 3145732
  27.4 8.8 %copy-start.1 = (f32[512,512]{1,0:T(8,128)S(1)}, f32[512,512]{1,0:T(8,128)}, u32[]{:S(2)}) copy-start(f32[512,512]{1,0:T(8,128)} %param.16) | copy-start | bytes 3145732
  40.2 25.8 %all-to-all-start.1 = ((f32[2,512,128]{2,0,1:T(2,128)}), f32[2,512,128]{2,0,1:T(2,128)S(1)}, u32[]{:S(2)}, u32[]{:S(2)}) async-start(f32[2,512,128]{2,0,1:T(2,128)} %copy.71), calls=%async_computation.1 | async-start | bytes 1048576 | tf_op jit(solution)/shard_map/all_to_all | solution.py:196
  73.7 34.8 %copy-start.2 = (f32[512,512]{1,0:T(8,128)S(1)}, f32[512,512]{1,0:T(8,128)}, u32[]{:S(2)}) copy-start(f32[512,512]{1,0:T(8,128)} %param.15) | copy-start | bytes 3145732

commit v14 on v13

--- a/solution.py
+++ b/solution.py
@@ -101,39 +101,37 @@
 
 def fft_filter(spread, diffusivity, eigen_here, bulk_shift, tables):
     d_index, j_index, c64, s64, ct, st, c128, s128 = tables
-    field_count, row_count, slab_width = spread.shape
-    gx_count = c64.shape[0]
-    rows_here = row_count // gx_count
+    gx_count, rows_here, field_count, slab_width = spread.shape
     total_cells = gx_count * slab_width
-    spread = spread.reshape(field_count, gx_count, rows_here, slab_width)
-
-    a_real = jnp.einsum("kd,fdaj->fkaj", c64, spread, precision=EXACT)
-    a_imag = -jnp.einsum("kd,fdaj->fkaj", s64, spread, precision=EXACT)
-    ct4 = ct[None, :, None, :]
-    st4 = st[None, :, None, :]
+    stacked = jnp.concatenate([c64, -s64], axis=0)
+    a_both = jnp.einsum("kd,dafj->kafj", stacked, spread, precision=EXACT)
+    a_real = a_both[:gx_count]
+    a_imag = a_both[gx_count:]
+    ct4 = ct[:, None, None, :]
+    st4 = st[:, None, None, :]
     b_real = a_real * ct4 + a_imag * st4
     b_imag = a_imag * ct4 - a_real * st4
     joined = jnp.concatenate([b_real, b_imag], axis=-1)
     forward_table = jnp.concatenate(
         [jnp.concatenate([c128, -s128], axis=1), jnp.concatenate([s128, c128], axis=1)], axis=0
     )
-    spec = jnp.einsum("fkaj,jm->fkam", joined, forward_table, precision=EXACT)
+    spec = jnp.einsum("kafj,jm->kafm", joined, forward_table, precision=EXACT)
     spec_real = spec[..., :slab_width]
     spec_imag = spec[..., slab_width:]
 
     mode_index = d_index[:, None] + gx_count * j_index[None, :]
     folded = jnp.minimum(mode_index, total_cells - mode_index).astype(jnp.float32)
     wavenumber = 2.0 * math.pi / total_cells * folded
-    growth = diffusivity[:, None, None, None] * (
-        eigen_here[None, None, :, None] + (wavenumber**2)[None, :, None, :]
+    growth = diffusivity[None, None, :, None] * (
+        eigen_here[None, :, None, None] + (wavenumber**2)[:, None, None, :]
     )
     damping = (1.0 - growth) / (1.0 + growth)
     signed = jnp.where(2 * mode_index >= total_cells, mode_index - total_cells, mode_index).astype(
         jnp.float32
     )
     travel = 2.0 * math.pi / total_cells * signed * bulk_shift[0]
-    cos_travel = jnp.cos(travel)[None, :, None, :]
-    sin_travel = jnp.sin(travel)[None, :, None, :]
+    cos_travel = jnp.cos(travel)[:, None, None, :]
+    sin_travel = jnp.sin(travel)[:, None, None, :]
     factor_real = damping * cos_travel
     factor_imag = -damping * sin_travel
     turned_real = spec_real * factor_real - spec_imag * factor_imag
@@ -143,17 +141,14 @@
     inverse_table = jnp.concatenate(
         [jnp.concatenate([c128, s128], axis=1), jnp.concatenate([-s128, c128], axis=1)], axis=0
     )
-    back = jnp.einsum("fkam,mj->fkaj", joined, inverse_table, precision=EXACT)
+    back = jnp.einsum("kafm,mj->kafj", joined, inverse_table, precision=EXACT)
     back_real = back[..., :slab_width]
     back_imag = back[..., slab_width:]
     e_real = back_real * ct4 - back_imag * st4
     e_imag = back_real * st4 + back_imag * ct4
-    filtered = (
-        jnp.einsum("dk,fkaj->fdaj", c64, e_real, precision=EXACT)
-        - jnp.einsum("dk,fkaj->fdaj", s64, e_imag, precision=EXACT)
-    ) / total_cells
-
-    return filtered.reshape(field_count, row_count, slab_width)
+    e_both = jnp.concatenate([e_real, e_imag], axis=0)
+    unstack = jnp.concatenate([c64, -s64], axis=1)
+    return jnp.einsum("dk,kafj->dafj", unstack, e_both, precision=EXACT) / total_cells
 
 
 def per_device(
@@ -190,20 +185,21 @@
     fed_side = drop_source(cells, rates, field)
     identity = jnp.eye(row_count, dtype=jnp.float32)
     dual_full = identity + dual_part
-    calm = jnp.einsum("ay,fyx->fax", dual_full, field[:2, 0], precision=HI)
-    calm = lax.all_to_all(calm, "gx", 1, 1, tiled=True)
-    fed = jnp.einsum("ay,fyx->fax", dual_full, fed_side, precision=HI)
-    fed = lax.all_to_all(fed, "gx", 1, 1, tiled=True)
+    calm = jnp.einsum("ay,fyx->afx", dual_full, field[:2, 0], precision=HI)
+    calm = lax.all_to_all(calm.reshape(row_count, -1), "gx", 0, 0, tiled=True)
+    fed = jnp.einsum("ay,fyx->afx", dual_full, fed_side, precision=HI)
+    fed = lax.all_to_all(fed.reshape(row_count, -1), "gx", 0, 0, tiled=True)
     tables = dft_tables(gx_count, slab_width)
     position = lax.axis_index("gx")
     eigen_here = lax.dynamic_slice_in_dim(wall_eigen, position * rows_here, rows_here)
-    calm = fft_filter(calm, diffusivity[:2], eigen_here, bulk_shift, tables)
+    group_shape = (gx_count, rows_here, 2, slab_width)
+    calm = fft_filter(calm.reshape(group_shape), diffusivity[:2], eigen_here, bulk_shift, tables)
     calm, fed = lax.optimization_barrier((calm, fed))
-    fed = fft_filter(fed, diffusivity[2:], eigen_here, bulk_shift, tables)
-    filtered = jnp.concatenate([calm, fed], axis=0)
-    filtered = filtered.reshape(field_count, row_count, slab_width)
-    gathered = lax.all_to_all(filtered, "gx", 1, 1, tiled=True)
-    result = jnp.einsum("fax,ya->fyx", gathered, identity + basis_part, precision=HI)
+    fed = fft_filter(fed.reshape(group_shape), diffusivity[2:], eigen_here, bulk_shift, tables)
+    filtered = jnp.concatenate([calm, fed], axis=2).reshape(row_count, field_count * slab_width)
+    gathered = lax.all_to_all(filtered, "gx", 0, 0, tiled=True)
+    gathered = gathered.reshape(row_count, field_count, slab_width)
+    result = jnp.einsum("afx,ya->fyx", gathered, identity + basis_part, precision=HI)
     return result[:, None]
 
 

time: 111 us -> 113 us (1.018)
  matrix products: 16.9 us -> 13.5 us
  local copies, waits for them, and re-layouts: 4.91 us -> 7.7 us
  starting transfers between devices: 27.5 us -> 29.2 us
  other arithmetic: 4.18 us -> 5.57 us
    dot_general x15 -> x11, matrix products: 16.9 us -> 13.5 us  [the longest x2 2.96 us: fft_filter(): spec = jnp.einsum('kafj,jm->kafm', joined, forward_table, precision=EXACT)]
    transpose x2 -> x0, local copies, waits for them, and re-layouts: 2.19 us -> none  [the longest x1 1.2 us: per_device(): calm = jnp.einsum('ay,fyx->fax', dual_full, field[:2, 0], precision=HI)]
    all_to_all x2, starting transfers between devices: 21.8 us -> 23.5 us  [the longest x1 13.2 us: per_device(): calm = lax.all_to_all(calm.reshape(row_count, -1), 'gx', 0, 0, tiled=True)]
    dot_general x0 -> x3, local copies, waits for them, and re-layouts: none -> 1.68 us  [the longest x2 1.27 us: per_device(): calm = jnp.einsum('ay,fyx->afx', dual_full, field[:2, 0], precision=HI)]
    all_to_all x1, local copies, waits for them, and re-layouts: 0.04 us -> 1.21 us  [per_device(): fed = lax.all_to_all(fed.reshape(row_count, -1), 'gx', 0, 0, tiled=True)]
  transfers between devices with their start and end apart: 5 -> 5, of which waited for: 2 -> 1; matrix products, arithmetic and copies ran while one was open for 14% -> 14% of each run, Pallas kernels for 8% -> 8%
where the time goes in v14:
time: 113 us; the launch traced here: 112 us
  blocking collectives  34.6 us (31%)
  starting transfers between devices  29.2 us (26%)
  matrix products  13.5 us (12%)
  waiting for transfers between devices  11.7 us (10%)
  Pallas kernels  8.83 us (8%)
  local copies, waits for them, and re-layouts  7.7 us (7%)
  other arithmetic  5.57 us (5%)
    all_to_all x1, blocking collectives, per_device(): gathered = lax.all_to_all(filtered, 'gx', 0, 0, tiled=True)  34.6 us
    all_to_all x1, starting transfers between devices, per_device(): calm = lax.all_to_all(calm.reshape(row_count, -1), 'gx', 0, 0, tiled=True)  13.2 us
    all_to_all x1, waiting for transfers between devices, per_device(): fed = lax.all_to_all(fed.reshape(row_count, -1), 'gx', 0, 0, tiled=True)  11.7 us
    all_to_all x1, starting transfers between devices, per_device(): fed = lax.all_to_all(fed.reshape(row_count, -1), 'gx', 0, 0, tiled=True)  10.3 us
    pallas_call x1, Pallas kernels, drop_source(): pl.pallas_call(source_kernel, grid=(drops // chunk,), in_specs=[pl.BlockS...  8.83 us
    ppermute x3, starting transfers between devices, per_device(): lax.ppermute(packed, 'gz', [(i, (i + shift) % gz_count) for i in range(gz...  5.72 us
    dot_general x2, matrix products, fft_filter(): spec = jnp.einsum('kafj,jm->kafm', joined, forward_table, precision=EXACT)  2.96 us
    dot_general x2, matrix products, fft_filter(): back = jnp.einsum('kafm,mj->kafj', joined, inverse_table, precision=EXACT)  2.95 us
  transfers between devices with their start and end apart: 5, of which 1 were waited for; matrix products, arithmetic and copies ran while one was open for 14% of the time, Pallas kernels for 8%

profile of v14, /device:TPU:1, one launch (start us, length us, event | category | flops | bytes accessed | tf_op | source)
XLA Modules:
  0.0 112.3 jit_solution(4073320785340716861)
XLA Ops:
  0.0 0.7 add_convert_fusion
  0.8 2.1 %collective-permute-start = (f32[3,4096]{1,0:T(4,128)S(1)}, f32[3,4096]{1,0:T(4,128)S(1)}, u32[]{:S(2)}, u32[]{:S(2)}) collective-permute-start(f32[3,4096]{1,0:T(4,128)S(1)} %pad_maximum_fusion.14), channel_id=1, source_target_pairs={{0,1},{1,2},{2,3},{3,0},{4,5},{5,6},{6,7},{7,4},{8,9},{9,10},{10,1... | collective-permute-start | bytes 147464 | tf_op jit(solution)/shard_map/ppermute | solution.py:177
  3.0 2.5 %collective-permute-start.1 = (f32[3,4096]{1,0:T(4,128)S(1)}, f32[3,4096]{1,0:T(4,128)S(1)}, u32[]{:S(2)}, u32[]{:S(2)}) collective-permute-start(f32[3,4096]{1,0:T(4,128)S(1)} %pad_maximum_fusion.14), channel_id=1, source_target_pairs={{0,2},{1,3},{2,0},{3,1},{4,6},{5,7},{6,4},{7,5},{8,10},{9,11},{10,... | collective-permute-start | bytes 147464 | tf_op jit(solution)/shard_map/ppermute | solution.py:177
  5.4 1.2 %collective-permute-start.2 = (f32[3,4096]{1,0:T(4,128)S(1)}, f32[3,4096]{1,0:T(4,128)S(1)}, u32[]{:S(2)}, u32[]{:S(2)}) collective-permute-start(f32[3,4096]{1,0:T(4,128)S(1)} %pad_maximum_fusion.14), channel_id=1, source_target_pairs={{0,3},{1,0},{2,1},{3,2},{4,7},{5,4},{6,5},{7,6},{8,11},{9,8},{10,9... | collective-permute-start | bytes 147464 | tf_op jit(solution)/shard_map/ppermute | solution.py:177
  6.6 1.1 slice_bitcast_fusion
  7.9 1.4 %fusion.10 = f32[64,8,256]{2,1,0:T(8,128)} fusion(f32[256,512,1]{1,0,2:T(8,128)S(1)} %bitcast.62, f32[512,512]{1,0:T(8,128)S(1)} %copy-done.1), kind=kOutput, calls=%fused_computation.19 | convolution fusion | flops 403439616 | bytes 2097152 | tf_op jit(solution)/shard_map/ay,fyx->afx/dot_general | solution.py:188
  9.3 13.2 %all-to-all-start = ((f32[64,8,256]{2,1,0:T(8,128)}), f32[64,8,256]{2,1,0:T(8,128)S(1)}, u32[]{:S(2)}, u32[]{:S(2)}) async-start(f32[64,8,256]{2,1,0:T(8,128)} %fusion.10), calls=%async_computation | async-start | bytes 1048576 | tf_op jit(solution)/shard_map/all_to_all | solution.py:189
  23.8 0.8 dynamic_slice.3
  24.6 0.8 fusion.52
  25.7 0.5 compare_reduce_fusion
  26.7 0.9 copy.28
  27.6 1.2 %reshape.140.piece_ref = f32[4,16384]{1,0:T(4,128)S(1)} reshape(f32[2,2,16384]{2,1,0:T(2,128)} %copy.28) | data formatting | bytes 524288 | tf_op jit(solution)/shard_map/reshape | solution.py:68
  29.0 0.3 and_select_fusion.2.row_ref
  29.4 8.8 %shard_map.91 = f32[2,512,128]{2,1,0:T(8,128)S(1)} custom-call(s32[1,16384]{1,0:T(1,128)S(1)} %and_select_fusion.2.row_ref, s32[1,16384]{1,0:T(1,128)S(1)} %get-tuple-element.13.col_ref, f32[4,16384]{1,0:T(4,128)S(1)} %reshape.140.piece_ref, f32[4,1,512,128]{3,2,1,0:T(8,128)S(1)} %copy-done), custom_call_target="tpu_custom_call" | custom-call | flops 8589934592 | bytes 1048576 | tf_op jit(solution)/shard_map/pallas_call | solution.py:73
  38.2 0.6 fusion.8
  38.8 0.4 copy.29
  39.2 1.2 %all_to_all.19 = f32[64,8,256]{2,1,0:T(8,128)} reshape(f32[512,2,128]{2,1,0:T(2,128)S(1)} %copy.29) | data formatting | bytes 1048576 | tf_op jit(solution)/shard_map/all_to_all | solution.py:191
  40.5 10.3 %all-to-all-start.1 = ((f32[64,8,256]{2,1,0:T(8,128)}), f32[64,8,256]{2,1,0:T(8,128)S(1)}, u32[]{:S(2)}, u32[]{:S(2)}) async-start(f32[64,8,256]{2,1,0:T(8,128)} %all_to_all.19), calls=%async_computation.1 | async-start | bytes 1048576 | tf_op jit(solution)/shard_map/all_to_all | solution.py:191
  50.8 1.1 fusion.25
  52.1 1.5 %fusion.19 = f32[64,8,2,256]{3,1,2,0:T(8,128)S(1)} fusion(f32[64,8,2,256]{3,0,2,1:T(8,128)S(1)} %pad_maximum_fusion, f32[128,128]{1,0:T(8,128)S(1)} %get-tuple-element.37, f32[128,128]{1,0:T(8,128)S(1)} %get-tuple-element.36, f32[128,128]{1,0:T(8,128)S(1)} %fusion.65), kind=kOutput, calls=%fused_computation.29 | convolution fusion | flops 805502976 | bytes 2293760 | tf_op jit(solution)/shard_map/kafj,jm->kafm/dot_general | solution.py:118
  54.1 1.5 %fusion.14 = f32[64,8,2,256]{3,0,2,1:T(8,128)S(1)} fusion(f32[64,8,2,256]{3,1,2,0:T(8,128)S(1)} %pad_maximum_fusion.1, f32[128,128]{1,0:T(8,128)S(1)} %get-tuple-element.37, f32[128,128]{1,0:T(8,128)S(1)} %fusion.65, f32[128,128]{1,0:T(8,128)S(1)} %get-tuple-element.36), kind=kOutput, calls=%fused_computation.23 | convolution fusion | flops 805502976 | bytes 2293760 | tf_op jit(solution)/shard_map/kafm,mj->kafj/dot_general | solution.py:144
  55.7 0.7 convolution_multiply_fusion.1
  56.4 11.7 %all-to-all-done.1 = f32[64,8,256]{2,1,0:T(8,128)S(1)} async-done(((f32[64,8,256]{2,1,0:T(8,128)}), f32[64,8,256]{2,1,0:T(8,128)S(1)}, u32[]{:S(2)}, u32[]{:S(2)}) %all-to-all-start.1) | async-done | bytes 524320 | tf_op jit(solution)/shard_map/all_to_all | solution.py:191
  68.1 1.1 fusion.23
  69.4 1.5 %fusion.17 = f32[64,8,2,256]{3,1,2,0:T(8,128)S(1)} fusion(f32[64,8,2,256]{3,0,2,1:T(8,128)S(1)} %pad_maximum_fusion.2, f32[128,128]{1,0:T(8,128)S(1)} %get-tuple-element.37, f32[128,128]{1,0:T(8,128)S(1)} %get-tuple-element.36, f32[128,128]{1,0:T(8,128)S(1)} %fusion.65), kind=kOutput, calls=%fused_computation.27 | convolution fusion | flops 805502976 | bytes 2293760 | tf_op jit(solution)/shard_map/kafj,jm->kafm/dot_general | solution.py:118
  71.3 1.5 %fusion.12 = f32[64,8,2,256]{3,0,2,1:T(8,128)S(1)} fusion(f32[64,8,2,256]{3,1,2,0:T(8,128)S(1)} %pad_maximum_fusion.3, f32[128,128]{1,0:T(8,128)S(1)} %get-tuple-element.37, f32[128,128]{1,0:T(8,128)S(1)} %fusion.65, f32[128,128]{1,0:T(8,128)S(1)} %get-tuple-element.36), kind=kOutput, calls=%fused_computation.21 | convolution fusion | flops 805502976 | bytes 2293760 | tf_op jit(solution)/shard_map/kafm,mj->kafj/dot_general | solution.py:144
  73.0 0.7 convolution_multiply_fusion
  73.8 0.6 copy.64
  74.4 34.6 %all_to_all.27 = f32[64,8,512]{2,1,0:T(8,128)S(1)} all-to-all(f32[64,8,512]{2,1,0:T(8,128)S(1)} %bitcast.59), channel_id=1, replica_groups=mesh['gx'=64,'gz'=4] {'gx'}, dimensions={0} | all-to-all | bytes 2097152 | tf_op jit(solution)/shard_map/all_to_all | solution.py:200
  109.0 0.4 reshape.142
  109.4 0.9 copy-done.2
  110.2 2.0 %convolution_bitcast_fusion = f32[4,1,512,128]{3,2,1,0:T(8,128)} fusion(f32[512,512]{1,0:T(8,128)S(1)} %copy-done.2, f32[512,4,128]{2,1,0:T(4,128)S(1)} %reshape.142), kind=kOutput, calls=%fused_computation.2 | convolution fusion | flops 806092800 | bytes 3145728 | tf_op jit(solution)/shard_map/afx,ya->fyx/dot_general | solution.py:202
  (41 shorter events, 3.5 us)
Async XLA Ops:
  0.0 0.8 copy-start.5
  0.8 7.0 %copy-start.1 = (f32[512,512]{1,0:T(8,128)S(1)}, f32[512,512]{1,0:T(8,128)}, u32[]{:S(2)}) copy-start(f32[512,512]{1,0:T(8,128)} %param.16) | copy-start | bytes 3145732
  0.8 24.9 %collective-permute-start = (f32[3,4096]{1,0:T(4,128)S(1)}, f32[3,4096]{1,0:T(4,128)S(1)}, u32[]{:S(2)}, u32[]{:S(2)}) collective-permute-start(f32[3,4096]{1,0:T(4,128)S(1)} %pad_maximum_fusion.14), channel_id=1, source_target_pairs={{0,1},{1,2},{2,3},{3,0},{4,5},{5,6},{6,7},{7,4},{8,9},{9,10},{10,1... | collective-permute-start | bytes 147464 | tf_op jit(solution)/shard_map/ppermute | solution.py:177
  3.0 22.8 %collective-permute-start.1 = (f32[3,4096]{1,0:T(4,128)S(1)}, f32[3,4096]{1,0:T(4,128)S(1)}, u32[]{:S(2)}, u32[]{:S(2)}) collective-permute-start(f32[3,4096]{1,0:T(4,128)S(1)} %pad_maximum_fusion.14), channel_id=1, source_target_pairs={{0,2},{1,3},{2,0},{3,1},{4,6},{5,7},{6,4},{7,5},{8,10},{9,11},{10,... | collective-permute-start | bytes 147464 | tf_op jit(solution)/shard_map/ppermute | solution.py:177
  5.4 20.3 %collective-permute-start.2 = (f32[3,4096]{1,0:T(4,128)S(1)}, f32[3,4096]{1,0:T(4,128)S(1)}, u32[]{:S(2)}, u32[]{:S(2)}) collective-permute-start(f32[3,4096]{1,0:T(4,128)S(1)} %pad_maximum_fusion.14), channel_id=1, source_target_pairs={{0,3},{1,0},{2,1},{3,2},{4,7},{5,4},{6,5},{7,6},{8,11},{9,8},{10,9... | collective-permute-start | bytes 147464 | tf_op jit(solution)/shard_map/ppermute | solution.py:177
  9.3 31.2 %all-to-all-start = ((f32[64,8,256]{2,1,0:T(8,128)}), f32[64,8,256]{2,1,0:T(8,128)S(1)}, u32[]{:S(2)}, u32[]{:S(2)}) async-start(f32[64,8,256]{2,1,0:T(8,128)} %fusion.10), calls=%async_computation | async-start | bytes 1048576 | tf_op jit(solution)/shard_map/all_to_all | solution.py:189
  23.1 0.7 copy-start.6
  26.5 2.8 %copy-start = (f32[4,1,512,128]{3,2,1,0:T(8,128)S(1)}, f32[4,1,512,128]{3,2,1,0:T(8,128)}, u32[]{:S(2)}) copy-start(f32[4,1,512,128]{3,2,1,0:T(8,128)} %field_ref.1) | copy-start | bytes 3145732
  40.5 27.6 %all-to-all-start.1 = ((f32[64,8,256]{2,1,0:T(8,128)}), f32[64,8,256]{2,1,0:T(8,128)S(1)}, u32[]{:S(2)}, u32[]{:S(2)}) async-start(f32[64,8,256]{2,1,0:T(8,128)} %all_to_all.19), calls=%async_computation.1 | async-start | bytes 1048576 | tf_op jit(solution)/shard_map/all_to_all | solution.py:191
  52.1 1.5 %copy-start.3 = (f32[64,128]{1,0:T(8,128)S(1)}, f32[64,128]{1,0:T(8,128)}, u32[]{:S(2)}) copy-start(f32[64,128]{1,0:T(8,128)} %get-tuple-element.30) | copy-start | bytes 98308
  52.1 1.5 %copy-start.4 = (f32[64,128]{1,0:T(8,128)S(1)}, f32[64,128]{1,0:T(8,128)}, u32[]{:S(2)}) copy-start(f32[64,128]{1,0:T(8,128)} %get-tuple-element.31) | copy-start | bytes 98308
  109.0 1.2 %copy-start.2 = (f32[512,512]{1,0:T(8,128)S(1)}, f32[512,512]{1,0:T(8,128)}, u32[]{:S(2)}) copy-start(f32[512,512]{1,0:T(8,128)} %param.15) | copy-start | bytes 3145732

commit v15 on v13

--- a/solution.py
+++ b/solution.py
@@ -20,20 +20,30 @@
 CHUNK = 16384
 
 
-def source_kernel(row_ref, col_ref, piece_ref, field_ref, out_ref, acc_ref):
+def source_kernel(plane_ref, packed_ref, field_ref, out_ref, acc_ref):
     step = pl.program_id(0)
     row_count = acc_ref.shape[0]
     slab_width = out_ref.shape[2]
-    chunk = row_ref.shape[1]
-    rows = row_ref[...]
-    cols = col_ref[...]
+    chunk = packed_ref.shape[1]
+    col_bits = slab_width.bit_length() - 1
+    cell_bits = (row_count * slab_width).bit_length() - 1
+    keys = packed_ref[0:1, :].astype(jnp.int32)
+    mine = lax.shift_right_logical(keys, cell_bits) == plane_ref[0]
+    rows = lax.shift_right_logical(keys & ((1 << cell_bits) - 1), col_bits)
+    cols = keys & (slab_width - 1)
     row_hit = lax.broadcasted_iota(jnp.int32, (row_count, chunk), 0) == rows
     lhs = jnp.where(row_hit, 1.0, 0.0).astype(jnp.bfloat16)
     col_hit = lax.broadcasted_iota(jnp.int32, (slab_width, chunk), 0) == cols
-    pieces = piece_ref[...]
-    rhs = jnp.concatenate(
-        [jnp.where(col_hit, pieces[p : p + 1, :], 0.0) for p in range(pieces.shape[0])], axis=0
-    ).astype(jnp.bfloat16)
+    pieces = []
+    for c in range(2):
+        rest = jnp.where(mine, packed_ref[c + 1 : c + 2, :], 0.0)
+        for _ in range(PIECES):
+            piece = rest.astype(jnp.bfloat16).astype(jnp.float32)
+            pieces.append(piece)
+            rest = rest - piece
+    rhs = jnp.concatenate([jnp.where(col_hit, p, 0.0) for p in pieces], axis=0).astype(
+        jnp.bfloat16
+    )
     part = lax.dot_general(
         lhs, rhs, (((1,), (1,)), ((), ())), preferred_element_type=jnp.float32
     )
@@ -56,27 +66,17 @@
             out_ref[c] = total
 
 
-def drop_source(cells, rates, field):
-    drops = cells.shape[0]
+def drop_source(packed, plane_here, field):
+    drops = packed.shape[1]
     field_count, _, row_count, slab_width = field.shape
-    pieces = []
-    rest = rates
-    for _ in range(PIECES):
-        piece = lax.reduce_precision(rest, exponent_bits=8, mantissa_bits=7)
-        pieces.append(piece)
-        rest = rest - piece
-    pieces = jnp.stack(pieces, axis=1).reshape(2 * PIECES, drops)
-    rows = (cells // slab_width).reshape(1, drops)
-    cols = (cells % slab_width).reshape(1, drops)
     width = 2 * PIECES * slab_width
     chunk = min(CHUNK, drops)
     return pl.pallas_call(
         source_kernel,
         grid=(drops // chunk,),
         in_specs=[
-            pl.BlockSpec((1, chunk), lambda i: (0, i)),
-            pl.BlockSpec((1, chunk), lambda i: (0, i)),
-            pl.BlockSpec((2 * PIECES, chunk), lambda i: (0, i)),
+            pl.BlockSpec(memory_space=pltpu.SMEM),
+            pl.BlockSpec((packed.shape[0], chunk), lambda i: (0, i)),
             pl.BlockSpec((2, 1, row_count, slab_width), lambda i: (1, 0, 0, 0)),
         ],
         out_specs=pl.BlockSpec((2, row_count, slab_width), lambda i: (0, 0, 0)),
@@ -86,7 +86,7 @@
         cost_estimate=pl.CostEstimate(
             flops=2 * row_count * width * drops, transcendentals=0, bytes_accessed=4 * row_count * width
         ),
-    )(rows, cols, pieces, field)
+    )(plane_here.reshape(1), packed, field)
 
 
 def dft_tables(gx_count, slab_width):
@@ -183,11 +183,7 @@
         for shift in range(1, gz_count)
     ]
     packed = jnp.concatenate(shares, axis=1)
-    keys = packed[0].astype(jnp.int32)
-    cells = keys % plane_cells
-    planes = keys // plane_cells
-    rates = jnp.where((planes == plane_here)[None, :], packed[1:], 0.0)
-    fed_side = drop_source(cells, rates, field)
+    fed_side = drop_source(packed, plane_here.astype(jnp.int32), field)
     identity = jnp.eye(row_count, dtype=jnp.float32)
     dual_full = identity + dual_part
     calm = jnp.einsum("ay,fyx->fax", dual_full, field[:2, 0], precision=HI)

time: 111 us -> 109 us (0.982)
  waiting for transfers between devices: 12.3 us -> 14.2 us
  starting transfers between devices: 27.5 us -> 25.8 us
  other arithmetic: 4.18 us -> 2.76 us
    all_to_all x1, waiting for transfers between devices: 1.89 us -> 3.78 us  [per_device(): calm = lax.all_to_all(calm, 'gx', 1, 1, tiled=True)]
    all_to_all x1, starting transfers between devices: 8.64 us -> 6.76 us  [per_device(): fed = lax.all_to_all(fed, 'gx', 1, 1, tiled=True)]
  transfers between devices with their start and end apart: 5 -> 5, of which waited for: 2 -> 2; matrix products, arithmetic and copies ran while one was open for 14% -> 13% of each run, Pallas kernels for 8% -> 8%
where the time goes in v15:
time: 109 us
  blocking collectives  34.8 us (32%)
  starting transfers between devices  25.8 us (24%)
  matrix products  16.9 us (16%)
  waiting for transfers between devices  14.2 us (13%)
  Pallas kernels  8.84 us (8%)
  local copies, waits for them, and re-layouts  4.46 us (4%)
  other arithmetic  2.76 us (3%)
    all_to_all x1, blocking collectives, per_device(): gathered = lax.all_to_all(filtered, 'gx', 1, 1, tiled=True)  34.8 us
    all_to_all x1, starting transfers between devices, per_device(): calm = lax.all_to_all(calm, 'gx', 1, 1, tiled=True)  13.3 us
    all_to_all x1, waiting for transfers between devices, per_device(): fed = lax.all_to_all(fed, 'gx', 1, 1, tiled=True)  10.4 us
    pallas_call x1, Pallas kernels, drop_source(): pl.pallas_call(source_kernel, grid=(drops // chunk,), in_specs=[pl.BlockS...  8.84 us
    all_to_all x1, starting transfers between devices, per_device(): fed = lax.all_to_all(fed, 'gx', 1, 1, tiled=True)  6.76 us
    ppermute x3, starting transfers between devices, per_device(): lax.ppermute(packed, 'gz', [(i, (i + shift) % gz_count) for i in range(gz...  5.72 us
    all_to_all x1, waiting for transfers between devices, per_device(): calm = lax.all_to_all(calm, 'gx', 1, 1, tiled=True)  3.78 us
    dot_general x2, matrix products, fft_filter(): spec = jnp.einsum('fkaj,jm->fkam', joined, forward_table, precision=EXACT)  2.96 us
  transfers between devices with their start and end apart: 5, of which 2 were waited for; matrix products, arithmetic and copies ran while one was open for 13% of the time, Pallas kernels for 8%

profile of v15, /device:TPU:1, one launch (start us, length us, event | category | flops | bytes accessed | tf_op | source)
XLA Modules:
  0.0 108.7 jit_solution(11575741097643758311)
XLA Ops:
  0.0 0.7 add_convert_fusion
  0.8 2.1 %collective-permute-start = (f32[3,4096]{1,0:T(4,128)S(1)}, f32[3,4096]{1,0:T(4,128)S(1)}, u32[]{:S(2)}, u32[]{:S(2)}) collective-permute-start(f32[3,4096]{1,0:T(4,128)S(1)} %pad_maximum_fusion.10), channel_id=1, source_target_pairs={{0,1},{1,2},{2,3},{3,0},{4,5},{5,6},{6,7},{7,4},{8,9},{9,10},{10,1... | collective-permute-start | bytes 147464 | tf_op jit(solution)/shard_map/ppermute | solution.py:182
  2.9 2.5 %collective-permute-start.1 = (f32[3,4096]{1,0:T(4,128)S(1)}, f32[3,4096]{1,0:T(4,128)S(1)}, u32[]{:S(2)}, u32[]{:S(2)}) collective-permute-start(f32[3,4096]{1,0:T(4,128)S(1)} %pad_maximum_fusion.10), channel_id=1, source_target_pairs={{0,2},{1,3},{2,0},{3,1},{4,6},{5,7},{6,4},{7,5},{8,10},{9,11},{10,... | collective-permute-start | bytes 147464 | tf_op jit(solution)/shard_map/ppermute | solution.py:182
  5.4 1.2 %collective-permute-start.2 = (f32[3,4096]{1,0:T(4,128)S(1)}, f32[3,4096]{1,0:T(4,128)S(1)}, u32[]{:S(2)}, u32[]{:S(2)}) collective-permute-start(f32[3,4096]{1,0:T(4,128)S(1)} %pad_maximum_fusion.10), channel_id=1, source_target_pairs={{0,3},{1,0},{2,1},{3,2},{4,7},{5,4},{6,5},{7,6},{8,11},{9,8},{10,9... | collective-permute-start | bytes 147464 | tf_op jit(solution)/shard_map/ppermute | solution.py:182
  6.5 1.9 %convolution_bitcast_fusion.4 = f32[2,512,128]{2,1,0:T(8,128)S(1)} fusion(f32[512,512]{1,0:T(8,128)} %param.16, f32[4,1,512,128]{3,2,0,1:T(8,128)} %bitcast.87), kind=kOutput, calls=%fused_computation.10 | convolution fusion | flops 403439616 | bytes 2097152 | tf_op jit(solution)/shard_map/ay,fyx->fax/dot_general | solution.py:189
  8.5 1.2 %copy.58 = f32[2,512,128]{2,0,1:T(2,128)} copy(f32[2,512,128]{2,1,0:T(8,128)S(1)} %convolution_bitcast_fusion.4) | data formatting | bytes 1048576 | tf_op jit(solution)/shard_map/ay,fyx->fax/transpose | solution.py:189
  9.7 13.3 %all-to-all-start = ((f32[2,512,128]{2,0,1:T(2,128)}), f32[2,512,128]{2,0,1:T(2,128)S(1)}, u32[]{:S(2)}, u32[]{:S(2)}) async-start(f32[2,512,128]{2,0,1:T(2,128)} %copy.58), calls=%async_computation | async-start | bytes 1048576 | tf_op jit(solution)/shard_map/all_to_all | solution.py:190
  24.2 0.8 dynamic_slice.3
  25.6 8.8 %shard_map.91 = f32[2,512,128]{2,1,0:T(8,128)S(1)} custom-call(s32[1]{0:T(128)} %bitcast.20.plane_ref, f32[3,16384]{1,0:T(4,128)S(1)} %pad_maximum_fusion.9.packed_ref, f32[4,1,512,128]{3,2,1,0:T(8,128)S(1)} %copy-done), custom_call_target="tpu_custom_call" | custom-call | flops 8589934592 | bytes 1048576 | tf_op jit(solution)/shard_map/pallas_call | solution.py:74
  34.5 1.1 convolution_bitcast_fusion.2
  35.6 1.0 copy.67
  36.6 3.8 %all-to-all-done = f32[2,512,128]{2,0,1:T(2,128)S(1)} async-done(((f32[2,512,128]{2,0,1:T(2,128)}), f32[2,512,128]{2,0,1:T(2,128)S(1)}, u32[]{:S(2)}, u32[]{:S(2)}) %all-to-all-start) | async-done | bytes 524320 | tf_op jit(solution)/shard_map/all_to_all | solution.py:190
  40.3 6.8 %all-to-all-start.1 = ((f32[2,512,128]{2,0,1:T(2,128)}), f32[2,512,128]{2,0,1:T(2,128)S(1)}, u32[]{:S(2)}, u32[]{:S(2)}) async-start(f32[2,512,128]{2,0,1:T(2,128)} %copy.67), calls=%async_computation.1 | async-start | bytes 1048576 | tf_op jit(solution)/shard_map/all_to_all | solution.py:192
  47.2 0.8 convolution_bitcast_fusion.3
  47.9 0.9 multiply_add_fusion.5
  48.9 1.5 %fusion.16 = f32[2,64,8,256]{3,2,1,0:T(8,128)S(1)} fusion(f32[2,64,8,256]{3,1,2,0:T(8,128)S(1)} %pad_maximum_fusion, f32[128,128]{1,0:T(8,128)S(1)} %get-tuple-element.25, f32[128,128]{1,0:T(8,128)S(1)} %get-tuple-element.24, f32[128,128]{1,0:T(8,128)S(1)} %fusion.99), kind=kOutput, calls=%fused_computation.31 | convolution fusion | flops 805502976 | bytes 2293760 | tf_op jit(solution)/shard_map/fkaj,jm->fkam/dot_general | solution.py:120
  50.4 0.3 multiply_subtract_fusion.4
  50.8 1.2 %fusion.11 = f32[2,64,8,256]{3,1,2,0:T(8,128)S(1)} fusion(f32[2,64,8,256]{3,2,1,0:T(8,128)S(1)} %pad_maximum_fusion.1, f32[128,128]{1,0:T(8,128)S(1)} %get-tuple-element.25, f32[128,128]{1,0:T(8,128)S(1)} %fusion.99, f32[128,128]{1,0:T(8,128)S(1)} %get-tuple-element.24), kind=kOutput, calls=%fused_computation.26 | convolution fusion | flops 805502976 | bytes 2293760 | tf_op jit(solution)/shard_map/fkam,mj->fkaj/dot_general | solution.py:146
  51.9 0.8 fusion.32
  52.7 0.8 fusion.5
  53.5 0.3 copy.115
  53.8 10.4 %all-to-all-done.1 = f32[2,512,128]{2,0,1:T(2,128)S(1)} async-done(((f32[2,512,128]{2,0,1:T(2,128)}), f32[2,512,128]{2,0,1:T(2,128)S(1)}, u32[]{:S(2)}, u32[]{:S(2)}) %all-to-all-start.1) | async-done | bytes 524320 | tf_op jit(solution)/shard_map/all_to_all | solution.py:192
  64.3 0.8 convolution_bitcast_fusion.1
  65.0 0.9 multiply_add_fusion.3
  66.0 1.5 %fusion.14 = f32[2,64,8,256]{3,2,1,0:T(8,128)S(1)} fusion(f32[2,64,8,256]{3,1,2,0:T(8,128)S(1)} %pad_maximum_fusion.2, f32[128,128]{1,0:T(8,128)S(1)} %get-tuple-element.25, f32[128,128]{1,0:T(8,128)S(1)} %get-tuple-element.24, f32[128,128]{1,0:T(8,128)S(1)} %fusion.99), kind=kOutput, calls=%fused_computation.29 | convolution fusion | flops 805502976 | bytes 2293760 | tf_op jit(solution)/shard_map/fkaj,jm->fkam/dot_general | solution.py:120
  67.5 0.3 multiply_subtract_fusion.2
  67.8 1.2 %fusion.9 = f32[2,64,8,256]{3,1,2,0:T(8,128)S(1)} fusion(f32[2,64,8,256]{3,2,1,0:T(8,128)S(1)} %pad_maximum_fusion.3, f32[128,128]{1,0:T(8,128)S(1)} %get-tuple-element.25, f32[128,128]{1,0:T(8,128)S(1)} %fusion.99, f32[128,128]{1,0:T(8,128)S(1)} %get-tuple-element.24), kind=kOutput, calls=%fused_computation.24 | convolution fusion | flops 805502976 | bytes 2293760 | tf_op jit(solution)/shard_map/fkam,mj->fkaj/dot_general | solution.py:146
  69.0 1.0 fusion.25
  70.1 0.8 fusion.3
  71.2 0.7 copy.75
  71.9 34.8 %all_to_all.15 = f32[4,512,128]{2,0,1:T(4,128)S(1)} all-to-all(f32[4,512,128]{2,0,1:T(4,128)S(1)} %copy.75), channel_id=1, replica_groups=mesh['gx'=64,'gz'=4] {'gx'}, dimensions={1} | all-to-all | bytes 2097152 | tf_op jit(solution)/shard_map/all_to_all | solution.py:201
  106.7 2.0 %convolution_bitcast_fusion = f32[4,1,512,128]{3,2,1,0:T(8,128)} fusion(f32[512,512]{1,0:T(8,128)S(1)} %copy-done.2, f32[4,512,128]{2,0,1:T(4,128)S(1)} %all_to_all.15), kind=kOutput, calls=%fused_computation.2 | convolution fusion | flops 806092800 | bytes 3145728 | tf_op jit(solution)/shard_map/fax,ya->fyx/dot_general | solution.py:202
  (30 shorter events, 1.9 us)
Async XLA Ops:
  0.0 0.8 copy-start.3
  0.8 24.7 %collective-permute-start = (f32[3,4096]{1,0:T(4,128)S(1)}, f32[3,4096]{1,0:T(4,128)S(1)}, u32[]{:S(2)}, u32[]{:S(2)}) collective-permute-start(f32[3,4096]{1,0:T(4,128)S(1)} %pad_maximum_fusion.10), channel_id=1, source_target_pairs={{0,1},{1,2},{2,3},{3,0},{4,5},{5,6},{6,7},{7,4},{8,9},{9,10},{10,1... | collective-permute-start | bytes 147464 | tf_op jit(solution)/shard_map/ppermute | solution.py:182
  2.9 22.6 %collective-permute-start.1 = (f32[3,4096]{1,0:T(4,128)S(1)}, f32[3,4096]{1,0:T(4,128)S(1)}, u32[]{:S(2)}, u32[]{:S(2)}) collective-permute-start(f32[3,4096]{1,0:T(4,128)S(1)} %pad_maximum_fusion.10), channel_id=1, source_target_pairs={{0,2},{1,3},{2,0},{3,1},{4,6},{5,7},{6,4},{7,5},{8,10},{9,11},{10,... | collective-permute-start | bytes 147464 | tf_op jit(solution)/shard_map/ppermute | solution.py:182
  5.4 20.1 %collective-permute-start.2 = (f32[3,4096]{1,0:T(4,128)S(1)}, f32[3,4096]{1,0:T(4,128)S(1)}, u32[]{:S(2)}, u32[]{:S(2)}) collective-permute-start(f32[3,4096]{1,0:T(4,128)S(1)} %pad_maximum_fusion.10), channel_id=1, source_target_pairs={{0,3},{1,0},{2,1},{3,2},{4,7},{5,4},{6,5},{7,6},{8,11},{9,8},{10,9... | collective-permute-start | bytes 147464 | tf_op jit(solution)/shard_map/ppermute | solution.py:182
  9.7 15.9 %copy-start = (f32[4,1,512,128]{3,2,1,0:T(8,128)S(1)}, f32[4,1,512,128]{3,2,1,0:T(8,128)}, u32[]{:S(2)}) copy-start(f32[4,1,512,128]{3,2,1,0:T(8,128)} %field_ref.1) | copy-start | bytes 3145732
  9.7 30.6 %all-to-all-start = ((f32[2,512,128]{2,0,1:T(2,128)}), f32[2,512,128]{2,0,1:T(2,128)S(1)}, u32[]{:S(2)}, u32[]{:S(2)}) async-start(f32[2,512,128]{2,0,1:T(2,128)} %copy.58), calls=%async_computation | async-start | bytes 1048576 | tf_op jit(solution)/shard_map/all_to_all | solution.py:190
  23.5 0.7 copy-start.4
  25.6 8.9 %copy-start.1 = (f32[512,512]{1,0:T(8,128)S(1)}, f32[512,512]{1,0:T(8,128)}, u32[]{:S(2)}) copy-start(f32[512,512]{1,0:T(8,128)} %param.16) | copy-start | bytes 3145732
  40.3 23.9 %all-to-all-start.1 = ((f32[2,512,128]{2,0,1:T(2,128)}), f32[2,512,128]{2,0,1:T(2,128)S(1)}, u32[]{:S(2)}, u32[]{:S(2)}) async-start(f32[2,512,128]{2,0,1:T(2,128)} %copy.67), calls=%async_computation.1 | async-start | bytes 1048576 | tf_op jit(solution)/shard_map/all_to_all | solution.py:192
  71.9 34.8 %copy-start.2 = (f32[512,512]{1,0:T(8,128)S(1)}, f32[512,512]{1,0:T(8,128)}, u32[]{:S(2)}) copy-start(f32[512,512]{1,0:T(8,128)} %param.15) | copy-start | bytes 3145732

commit v16 on v15

--- a/solution.py
+++ b/solution.py
@@ -178,11 +178,9 @@
     packed = jnp.concatenate(
         [(drop_plane * plane_cells + drop_cell).astype(jnp.float32)[None, :], drop_rate], axis=0
     )
-    shares = [packed] + [
-        lax.ppermute(packed, "gz", [(i, (i + shift) % gz_count) for i in range(gz_count)])
-        for shift in range(1, gz_count)
-    ]
-    packed = jnp.concatenate(shares, axis=1)
+    slots = jnp.arange(gz_count, dtype=jnp.int32)[:, None, None] == plane_here
+    packed = lax.psum(jnp.where(slots, packed[None], 0.0), "gz")
+    packed = jnp.transpose(packed, (1, 0, 2)).reshape(packed.shape[1], -1)
     fed_side = drop_source(packed, plane_here.astype(jnp.int32), field)
     identity = jnp.eye(row_count, dtype=jnp.float32)
     dual_full = identity + dual_part

time: 109 us -> 166 us (1.52)
  waiting for transfers between devices: 14.2 us -> 55.1 us
  between operations: 0.99 us -> 14.4 us
  local copies, waits for them, and re-layouts: 4.46 us -> 6.76 us
    psum x0 -> x1, waiting for transfers between devices: none -> 44.7 us  [per_device(): packed = lax.psum(jnp.where(slots, packed[None], 0.0), 'gz')]
    all_to_all x1, starting transfers between devices: 6.76 us -> 13 us  [per_device(): fed = lax.all_to_all(fed, 'gx', 1, 1, tiled=True)]
    ppermute x3 -> x0, starting transfers between devices: 5.72 us -> none  [per_device(): lax.ppermute(packed, 'gz', [(i, (i + shift) % gz_count) for i in range(gz...]
    all_to_all x1, waiting for transfers between devices: 3.78 us -> 0.01 us  [per_device(): calm = lax.all_to_all(calm, 'gx', 1, 1, tiled=True)]
    unnamed x10 -> x17, local copies, waits for them, and re-layouts: 0.07 us -> 2.38 us
  transfers between devices with their start and end apart: 5 -> 3, of which waited for: 2 -> 2; matrix products, arithmetic and copies ran while one was open for 13% -> 7% of each run, Pallas kernels for 8% -> 5%
where the time goes in v16:
time: 166 us; the launch traced here: 165 us
  waiting for transfers between devices  55.1 us (33%)
  blocking collectives  34.8 us (21%)
  starting transfers between devices  26.3 us (16%)
  matrix products  16.9 us (10%)
  between operations  14.4 us (9%)
  Pallas kernels  8.84 us (5%)
  local copies, waits for them, and re-layouts  6.76 us (4%)
  other arithmetic  2.06 us (1%)
    psum x1, waiting for transfers between devices, per_device(): packed = lax.psum(jnp.where(slots, packed[None], 0.0), 'gz')  44.7 us
    all_to_all x1, blocking collectives, per_device(): gathered = lax.all_to_all(filtered, 'gx', 1, 1, tiled=True)  34.8 us
    all_to_all x1, starting transfers between devices, per_device(): calm = lax.all_to_all(calm, 'gx', 1, 1, tiled=True)  13.3 us
    all_to_all x1, starting transfers between devices, per_device(): fed = lax.all_to_all(fed, 'gx', 1, 1, tiled=True)  13 us
    all_to_all x1, waiting for transfers between devices, per_device(): fed = lax.all_to_all(fed, 'gx', 1, 1, tiled=True)  10.5 us
    pallas_call x1, Pallas kernels, drop_source(): pl.pallas_call(source_kernel, grid=(drops // chunk,), in_specs=[pl.BlockS...  8.84 us
  transfers between devices with their start and end apart: 3, of which 2 were waited for; matrix products, arithmetic and copies ran while one was open for 7% of the time, Pallas kernels for 5%

profile of v16, /device:TPU:1, one launch (start us, length us, event | category | flops | bytes accessed | tf_op | source)
XLA Modules:
  0.0 165.2 jit_solution(9801598453865731324)
XLA Ops:
  6.5 1.9 %convolution_bitcast_fusion.4 = f32[2,512,128]{2,1,0:T(8,128)S(1)} fusion(f32[512,512]{1,0:T(8,128)} %param.16, f32[4,1,512,128]{3,2,0,1:T(8,128)} %bitcast.91), kind=kOutput, calls=%fused_computation.10 | convolution fusion | flops 403439616 | bytes 2097152 | tf_op jit(solution)/shard_map/ay,fyx->fax/dot_general | solution.py:187
  8.5 1.2 copy.58
  9.7 13.3 %all-to-all-start = ((f32[2,512,128]{2,0,1:T(2,128)}), f32[2,512,128]{2,0,1:T(2,128)S(1)}, u32[]{:S(2)}, u32[]{:S(2)}) async-start(f32[2,512,128]{2,0,1:T(2,128)} %copy.58), calls=%async_computation | async-start | bytes 1048576 | tf_op jit(solution)/shard_map/all_to_all | solution.py:188
  23.3 0.8 copy.87
  25.5 0.8 dynamic_slice.3
  26.5 0.6 copy-done.7
  27.1 44.7 %all-reduce.2.cloned.1.call-done.packed_ref = f32[3,16384]{1,0:T(4,128)} async-done(((f32[3,16384]{1,0:T(4,128)}), f32[3,16384]{1,0:T(4,128)}) %all-reduce.2.cloned.1.call-update) | async-done | bytes 196624 | tf_op jit(solution)/shard_map/psum | solution.py:182
  71.8 0.9 copy-done.1
  72.8 8.8 %shard_map.91 = f32[2,512,128]{2,1,0:T(8,128)S(1)} custom-call(s32[1]{0:T(128)} %bitcast.20.plane_ref, f32[3,16384]{1,0:T(4,128)S(1)} %copy-done.1, f32[4,1,512,128]{3,2,1,0:T(8,128)S(1)} %copy-done), custom_call_target="tpu_custom_call" | custom-call | flops 8589934592 | bytes 1048576 | tf_op jit(solution)/shard_map/pallas_call | solution.py:74
  81.6 1.1 convolution_bitcast_fusion.2
  82.7 1.0 copy.67
  83.7 13.0 %all-to-all-start.1 = ((f32[2,512,128]{2,0,1:T(2,128)}), f32[2,512,128]{2,0,1:T(2,128)S(1)}, u32[]{:S(2)}, u32[]{:S(2)}) async-start(f32[2,512,128]{2,0,1:T(2,128)} %copy.67), calls=%async_computation.1 | async-start | bytes 1048576 | tf_op jit(solution)/shard_map/all_to_all | solution.py:190
  96.7 0.8 convolution_bitcast_fusion.3
  97.5 0.9 multiply_add_fusion.5
  98.5 1.5 fusion.16
  99.9 0.3 multiply_subtract_fusion.4
  100.3 1.2 fusion.11
  101.5 0.8 fusion.32
  102.3 0.8 fusion.5
  103.1 0.3 copy.116
  103.4 10.5 %all-to-all-done.1 = f32[2,512,128]{2,0,1:T(2,128)S(1)} async-done(((f32[2,512,128]{2,0,1:T(2,128)}), f32[2,512,128]{2,0,1:T(2,128)S(1)}, u32[]{:S(2)}, u32[]{:S(2)}) %all-to-all-start.1) | async-done | bytes 524320 | tf_op jit(solution)/shard_map/all_to_all | solution.py:190
  113.9 0.8 convolution_bitcast_fusion.1
  114.6 0.9 multiply_add_fusion.3
  115.6 1.5 fusion.14
  117.1 0.3 multiply_subtract_fusion.2
  117.5 1.2 fusion.9
  118.7 1.0 fusion.25
  119.7 0.8 fusion.3
  120.5 0.3 copy.114
  120.9 0.7 copy.75
  121.6 34.8 %all_to_all.15 = f32[4,512,128]{2,0,1:T(4,128)S(1)} all-to-all(f32[4,512,128]{2,0,1:T(4,128)S(1)} %copy.75), channel_id=1, replica_groups=mesh['gx'=64,'gz'=4] {'gx'}, dimensions={1} | all-to-all | bytes 2097152 | tf_op jit(solution)/shard_map/all_to_all | solution.py:199
  156.3 2.0 %convolution_bitcast_fusion = f32[4,1,512,128]{3,2,1,0:T(8,128)} fusion(f32[512,512]{1,0:T(8,128)S(1)} %copy-done.3, f32[4,512,128]{2,0,1:T(4,128)S(1)} %all_to_all.15), kind=kOutput, calls=%fused_computation.2 | convolution fusion | flops 806092800 | bytes 3145728 | tf_op jit(solution)/shard_map/fax,ya->fyx/dot_general | solution.py:200
  (35 shorter events, 1.7 us)
Async XLA Ops:
  9.7 13.4 %copy-start.5 = (s32[4096]{0:T(1024)S(1)}, s32[4096]{0:T(1024)}, u32[]{:S(2)}) copy-start(s32[4096]{0:T(1024)} %param.10) | copy-start | bytes 49156
  9.7 13.4 %copy-start.6 = (s32[4096]{0:T(1024)S(1)}, s32[4096]{0:T(1024)}, u32[]{:S(2)}) copy-start(s32[4096]{0:T(1024)} %param.11) | copy-start | bytes 49156
  9.7 13.4 %copy-start.4 = (f32[2,4096]{1,0:T(2,128)S(1)}, f32[2,4096]{1,0:T(2,128)}, u32[]{:S(2)}) copy-start(f32[2,4096]{1,0:T(2,128)} %param.12) | copy-start | bytes 98308
  9.7 74.0 %all-to-all-start = ((f32[2,512,128]{2,0,1:T(2,128)}), f32[2,512,128]{2,0,1:T(2,128)S(1)}, u32[]{:S(2)}, u32[]{:S(2)}) async-start(f32[2,512,128]{2,0,1:T(2,128)} %copy.58), calls=%async_computation | async-start | bytes 1048576 | tf_op jit(solution)/shard_map/all_to_all | solution.py:188
  23.0 48.8 %copy-start = (f32[4,1,512,128]{3,2,1,0:T(8,128)S(1)}, f32[4,1,512,128]{3,2,1,0:T(8,128)}, u32[]{:S(2)}) copy-start(f32[4,1,512,128]{3,2,1,0:T(8,128)} %field_ref.1) | copy-start | bytes 3145732
  23.0 48.8 %all-reduce.2.cloned.1.call-start = ((), (), s32[]{:S(2)}) async-start(), calls=%async_computation.3 | async-start | bytes 524288 | tf_op jit(solution)/shard_map/psum | solution.py:182
  26.4 0.7 copy-start.7
  71.8 1.0 copy-start.1
  72.8 8.8 %copy-start.2 = (f32[512,512]{1,0:T(8,128)S(1)}, f32[512,512]{1,0:T(8,128)}, u32[]{:S(2)}) copy-start(f32[512,512]{1,0:T(8,128)} %param.16) | copy-start | bytes 3145732
  83.7 30.2 %all-to-all-start.1 = ((f32[2,512,128]{2,0,1:T(2,128)}), f32[2,512,128]{2,0,1:T(2,128)S(1)}, u32[]{:S(2)}, u32[]{:S(2)}) async-start(f32[2,512,128]{2,0,1:T(2,128)} %copy.67), calls=%async_computation.1 | async-start | bytes 1048576 | tf_op jit(solution)/shard_map/all_to_all | solution.py:190
  121.5 34.8 %copy-start.3 = (f32[512,512]{1,0:T(8,128)S(1)}, f32[512,512]{1,0:T(8,128)}, u32[]{:S(2)}) copy-start(f32[512,512]{1,0:T(8,128)} %param.15) | copy-start | bytes 3145732
Sparse Core Ops, SparseCore 0:
  26.2 45.5 all-reduce.1

commit v17 on v16

--- a/solution.py
+++ b/solution.py
@@ -178,9 +178,11 @@
     packed = jnp.concatenate(
         [(drop_plane * plane_cells + drop_cell).astype(jnp.float32)[None, :], drop_rate], axis=0
     )
-    slots = jnp.arange(gz_count, dtype=jnp.int32)[:, None, None] == plane_here
-    packed = lax.psum(jnp.where(slots, packed[None], 0.0), "gz")
-    packed = jnp.transpose(packed, (1, 0, 2)).reshape(packed.shape[1], -1)
+    span = 1
+    while span < gz_count:
+        partner = lax.ppermute(packed, "gz", [(i, i ^ span) for i in range(gz_count)])
+        packed = jnp.concatenate([packed, partner], axis=1)
+        span *= 2
     fed_side = drop_source(packed, plane_here.astype(jnp.int32), field)
     identity = jnp.eye(row_count, dtype=jnp.float32)
     dual_full = identity + dual_part

time: 166 us -> 111 us (0.67)
  waiting for transfers between devices: 55.1 us -> 13.1 us
  between operations: 14.4 us -> 0.99 us
  starting transfers between devices: 26.3 us -> 29.9 us
  local copies, waits for them, and re-layouts: 6.76 us -> 4.42 us
    psum x1 -> x0, waiting for transfers between devices: 44.7 us -> none  [per_device(): packed = lax.psum(jnp.where(slots, packed[None], 0.0), 'gz')]
    ppermute x0 -> x2, starting transfers between devices: none -> 4.31 us  [per_device(): lax.ppermute(packed, 'gz', [(i, i ^ span) for i in range(gz_count)])]
    ppermute x0 -> x2, waiting for transfers between devices: none -> 2.64 us  [per_device(): lax.ppermute(packed, 'gz', [(i, i ^ span) for i in range(gz_count)])]
    unnamed x17 -> x14, local copies, waits for them, and re-layouts: 2.38 us -> 0.03 us
  transfers between devices with their start and end apart: 3 -> 4, of which waited for: 2 -> 2; matrix products, arithmetic and copies ran while one was open for 7% -> 10% of each run, Pallas kernels for 5% -> 8%
where the time goes in v17:
time: 111 us
  blocking collectives  34.8 us (31%)
  starting transfers between devices  29.9 us (27%)
  matrix products  16.9 us (15%)
  waiting for transfers between devices  13.1 us (12%)
  Pallas kernels  8.84 us (8%)
  local copies, waits for them, and re-layouts  4.42 us (4%)
  other arithmetic  2.07 us (2%)
    all_to_all x1, blocking collectives, per_device(): gathered = lax.all_to_all(filtered, 'gx', 1, 1, tiled=True)  34.8 us
    all_to_all x1, starting transfers between devices, per_device(): calm = lax.all_to_all(calm, 'gx', 1, 1, tiled=True)  13.3 us
    all_to_all x1, starting transfers between devices, per_device(): fed = lax.all_to_all(fed, 'gx', 1, 1, tiled=True)  12.3 us
    all_to_all x1, waiting for transfers between devices, per_device(): fed = lax.all_to_all(fed, 'gx', 1, 1, tiled=True)  10.4 us
    pallas_call x1, Pallas kernels, drop_source(): pl.pallas_call(source_kernel, grid=(drops // chunk,), in_specs=[pl.BlockS...  8.84 us
    ppermute x2, starting transfers between devices, per_device(): lax.ppermute(packed, 'gz', [(i, i ^ span) for i in range(gz_count)])  4.31 us
    dot_general x2, matrix products, fft_filter(): spec = jnp.einsum('fkaj,jm->fkam', joined, forward_table, precision=EXACT)  2.96 us
    ppermute x2, waiting for transfers between devices, per_device(): lax.ppermute(packed, 'gz', [(i, i ^ span) for i in range(gz_count)])  2.64 us
  transfers between devices with their start and end apart: 4, of which 2 were waited for; matrix products, arithmetic and copies ran while one was open for 10% of the time, Pallas kernels for 8%

profile of v17, /device:TPU:1, one launch (start us, length us, event | category | flops | bytes accessed | tf_op | source)
XLA Modules:
  0.0 110.9 jit_solution(1923831938107869267)
XLA Ops:
  0.0 1.9 %convolution_bitcast_fusion.4 = f32[2,512,128]{2,1,0:T(8,128)S(1)} fusion(f32[512,512]{1,0:T(8,128)} %param.16, f32[4,1,512,128]{3,2,0,1:T(8,128)} %bitcast.87), kind=kOutput, calls=%fused_computation.10 | convolution fusion | flops 403439616 | bytes 2097152 | tf_op jit(solution)/shard_map/ay,fyx->fax/dot_general | solution.py:189
  2.0 1.2 %copy.58 = f32[2,512,128]{2,0,1:T(2,128)} copy(f32[2,512,128]{2,1,0:T(8,128)S(1)} %convolution_bitcast_fusion.4) | data formatting | bytes 1048576 | tf_op jit(solution)/shard_map/ay,fyx->fax/transpose | solution.py:189
  3.2 13.3 %all-to-all-start = ((f32[2,512,128]{2,0,1:T(2,128)}), f32[2,512,128]{2,0,1:T(2,128)S(1)}, u32[]{:S(2)}, u32[]{:S(2)}) async-start(f32[2,512,128]{2,0,1:T(2,128)} %copy.58), calls=%async_computation | async-start | bytes 1048576 | tf_op jit(solution)/shard_map/all_to_all | solution.py:190
  16.6 1.3 %collective-permute-start = (f32[3,4096]{1,0:T(4,128)S(1)}, f32[3,4096]{1,0:T(4,128)S(1)}, u32[]{:S(2)}, u32[]{:S(2)}) collective-permute-start(f32[3,4096]{1,0:T(4,128)S(1)} %pad_maximum_fusion.11), channel_id=1, source_target_pairs={{0,1},{1,0},{2,3},{3,2},{4,5},{5,4},{6,7},{7,6},{8,9},{9,8},{10,11... | collective-permute-start | bytes 147464 | tf_op jit(solution)/shard_map/ppermute | solution.py:183
  17.9 0.3 fusion.91
  18.9 0.8 dynamic_slice.3
  20.1 3.0 %collective-permute-start.1 = (f32[3,8192]{1,0:T(4,128)S(1)}, f32[3,8192]{1,0:T(4,128)S(1)}, u32[]{:S(2)}, u32[]{:S(2)}) collective-permute-start(f32[3,8192]{1,0:T(4,128)S(1)} %pad_maximum_fusion.10), channel_id=1, source_target_pairs={{0,2},{1,3},{2,0},{3,1},{4,6},{5,7},{6,4},{7,5},{8,10},{9,11},{10,... | collective-permute-start | bytes 294920 | tf_op jit(solution)/shard_map/ppermute | solution.py:183
  23.4 2.6 %collective-permute-done.1 = f32[3,8192]{1,0:T(4,128)S(1)} collective-permute-done((f32[3,8192]{1,0:T(4,128)S(1)}, f32[3,8192]{1,0:T(4,128)S(1)}, u32[]{:S(2)}, u32[]{:S(2)}) %collective-permute-start.1) | collective-permute-done | bytes 98336 | tf_op jit(solution)/shard_map/ppermute | solution.py:183
  26.1 8.8 %shard_map.91 = f32[2,512,128]{2,1,0:T(8,128)S(1)} custom-call(s32[1]{0:T(128)} %bitcast.20.plane_ref, f32[3,16384]{1,0:T(4,128)S(1)} %pad_maximum_fusion.9.packed_ref, f32[4,1,512,128]{3,2,1,0:T(8,128)S(1)} %copy-done), custom_call_target="tpu_custom_call" | custom-call | flops 8589934592 | bytes 1048576 | tf_op jit(solution)/shard_map/pallas_call | solution.py:74
  35.0 1.1 convolution_bitcast_fusion.2
  36.0 1.0 copy.67
  37.0 12.3 %all-to-all-start.1 = ((f32[2,512,128]{2,0,1:T(2,128)}), f32[2,512,128]{2,0,1:T(2,128)S(1)}, u32[]{:S(2)}, u32[]{:S(2)}) async-start(f32[2,512,128]{2,0,1:T(2,128)} %copy.67), calls=%async_computation.1 | async-start | bytes 1048576 | tf_op jit(solution)/shard_map/all_to_all | solution.py:192
  49.4 0.8 convolution_bitcast_fusion.3
  50.1 0.9 multiply_add_fusion.5
  51.1 1.5 %fusion.16 = f32[2,64,8,256]{3,2,1,0:T(8,128)S(1)} fusion(f32[2,64,8,256]{3,1,2,0:T(8,128)S(1)} %pad_maximum_fusion, f32[128,128]{1,0:T(8,128)S(1)} %get-tuple-element.25, f32[128,128]{1,0:T(8,128)S(1)} %get-tuple-element.24, f32[128,128]{1,0:T(8,128)S(1)} %fusion.99), kind=kOutput, calls=%fused_computation.31 | convolution fusion | flops 805502976 | bytes 2293760 | tf_op jit(solution)/shard_map/fkaj,jm->fkam/dot_general | solution.py:120
  52.5 0.3 multiply_subtract_fusion.4
  52.9 1.2 %fusion.11 = f32[2,64,8,256]{3,1,2,0:T(8,128)S(1)} fusion(f32[2,64,8,256]{3,2,1,0:T(8,128)S(1)} %pad_maximum_fusion.1, f32[128,128]{1,0:T(8,128)S(1)} %get-tuple-element.25, f32[128,128]{1,0:T(8,128)S(1)} %fusion.99, f32[128,128]{1,0:T(8,128)S(1)} %get-tuple-element.24), kind=kOutput, calls=%fused_computation.26 | convolution fusion | flops 805502976 | bytes 2293760 | tf_op jit(solution)/shard_map/fkam,mj->fkaj/dot_general | solution.py:146
  54.1 0.8 fusion.32
  54.9 0.8 fusion.5
  55.7 0.3 copy.115
  56.0 10.4 %all-to-all-done.1 = f32[2,512,128]{2,0,1:T(2,128)S(1)} async-done(((f32[2,512,128]{2,0,1:T(2,128)}), f32[2,512,128]{2,0,1:T(2,128)S(1)}, u32[]{:S(2)}, u32[]{:S(2)}) %all-to-all-start.1) | async-done | bytes 524320 | tf_op jit(solution)/shard_map/all_to_all | solution.py:192
  66.4 0.7 convolution_bitcast_fusion.1
  67.2 0.9 multiply_add_fusion.3
  68.2 1.5 %fusion.14 = f32[2,64,8,256]{3,2,1,0:T(8,128)S(1)} fusion(f32[2,64,8,256]{3,1,2,0:T(8,128)S(1)} %pad_maximum_fusion.2, f32[128,128]{1,0:T(8,128)S(1)} %get-tuple-element.25, f32[128,128]{1,0:T(8,128)S(1)} %get-tuple-element.24, f32[128,128]{1,0:T(8,128)S(1)} %fusion.99), kind=kOutput, calls=%fused_computation.29 | convolution fusion | flops 805502976 | bytes 2293760 | tf_op jit(solution)/shard_map/fkaj,jm->fkam/dot_general | solution.py:120
  69.6 0.3 multiply_subtract_fusion.2
  70.0 1.2 %fusion.9 = f32[2,64,8,256]{3,1,2,0:T(8,128)S(1)} fusion(f32[2,64,8,256]{3,2,1,0:T(8,128)S(1)} %pad_maximum_fusion.3, f32[128,128]{1,0:T(8,128)S(1)} %get-tuple-element.25, f32[128,128]{1,0:T(8,128)S(1)} %fusion.99, f32[128,128]{1,0:T(8,128)S(1)} %get-tuple-element.24), kind=kOutput, calls=%fused_computation.24 | convolution fusion | flops 805502976 | bytes 2293760 | tf_op jit(solution)/shard_map/fkam,mj->fkaj/dot_general | solution.py:146
  71.2 1.0 fusion.25
  72.3 0.8 fusion.3
  73.0 0.3 copy.113
  73.4 0.7 copy.75
  74.1 34.8 %all_to_all.15 = f32[4,512,128]{2,0,1:T(4,128)S(1)} all-to-all(f32[4,512,128]{2,0,1:T(4,128)S(1)} %copy.75), channel_id=1, replica_groups=mesh['gx'=64,'gz'=4] {'gx'}, dimensions={1} | all-to-all | bytes 2097152 | tf_op jit(solution)/shard_map/all_to_all | solution.py:201
  108.9 2.0 %convolution_bitcast_fusion = f32[4,1,512,128]{3,2,1,0:T(8,128)} fusion(f32[512,512]{1,0:T(8,128)S(1)} %copy-done.2, f32[4,512,128]{2,0,1:T(4,128)S(1)} %all_to_all.15), kind=kOutput, calls=%fused_computation.2 | convolution fusion | flops 806092800 | bytes 3145728 | tf_op jit(solution)/shard_map/fax,ya->fyx/dot_general | solution.py:202
  (33 shorter events, 1.4 us)
Async XLA Ops:
  3.2 13.3 %copy-start.4 = (s32[4096]{0:T(1024)S(1)}, s32[4096]{0:T(1024)}, u32[]{:S(2)}) copy-start(s32[4096]{0:T(1024)} %param.10) | copy-start | bytes 49156
  3.2 13.3 %copy-start.5 = (s32[4096]{0:T(1024)S(1)}, s32[4096]{0:T(1024)}, u32[]{:S(2)}) copy-start(s32[4096]{0:T(1024)} %param.11) | copy-start | bytes 49156
  3.2 13.4 %copy-start.3 = (f32[2,4096]{1,0:T(2,128)S(1)}, f32[2,4096]{1,0:T(2,128)}, u32[]{:S(2)}) copy-start(f32[2,4096]{1,0:T(2,128)} %param.12) | copy-start | bytes 98308
  3.2 15.7 %copy-start.6 = (f32[4]{0:T(128)S(1)}, f32[4]{0:T(128)}, u32[]{:S(2)}) copy-start(f32[4]{0:T(128)} %param.13) | copy-start | bytes 52
  3.2 33.9 %all-to-all-start = ((f32[2,512,128]{2,0,1:T(2,128)}), f32[2,512,128]{2,0,1:T(2,128)S(1)}, u32[]{:S(2)}, u32[]{:S(2)}) async-start(f32[2,512,128]{2,0,1:T(2,128)} %copy.58), calls=%async_computation | async-start | bytes 1048576 | tf_op jit(solution)/shard_map/all_to_all | solution.py:190
  16.5 9.6 %copy-start = (f32[4,1,512,128]{3,2,1,0:T(8,128)S(1)}, f32[4,1,512,128]{3,2,1,0:T(8,128)}, u32[]{:S(2)}) copy-start(f32[4,1,512,128]{3,2,1,0:T(8,128)} %field_ref.1) | copy-start | bytes 3145732
  16.6 3.5 %collective-permute-start = (f32[3,4096]{1,0:T(4,128)S(1)}, f32[3,4096]{1,0:T(4,128)S(1)}, u32[]{:S(2)}, u32[]{:S(2)}) collective-permute-start(f32[3,4096]{1,0:T(4,128)S(1)} %pad_maximum_fusion.11), channel_id=1, source_target_pairs={{0,1},{1,0},{2,3},{3,2},{4,5},{5,4},{6,7},{7,6},{8,9},{9,8},{10,11... | collective-permute-start | bytes 147464 | tf_op jit(solution)/shard_map/ppermute | solution.py:183
  20.1 5.9 %collective-permute-start.1 = (f32[3,8192]{1,0:T(4,128)S(1)}, f32[3,8192]{1,0:T(4,128)S(1)}, u32[]{:S(2)}, u32[]{:S(2)}) collective-permute-start(f32[3,8192]{1,0:T(4,128)S(1)} %pad_maximum_fusion.10), channel_id=1, source_target_pairs={{0,2},{1,3},{2,0},{3,1},{4,6},{5,7},{6,4},{7,5},{8,10},{9,11},{10,... | collective-permute-start | bytes 294920 | tf_op jit(solution)/shard_map/ppermute | solution.py:183
  26.1 8.9 %copy-start.1 = (f32[512,512]{1,0:T(8,128)S(1)}, f32[512,512]{1,0:T(8,128)}, u32[]{:S(2)}) copy-start(f32[512,512]{1,0:T(8,128)} %param.16) | copy-start | bytes 3145732
  37.0 29.4 %all-to-all-start.1 = ((f32[2,512,128]{2,0,1:T(2,128)}), f32[2,512,128]{2,0,1:T(2,128)S(1)}, u32[]{:S(2)}, u32[]{:S(2)}) async-start(f32[2,512,128]{2,0,1:T(2,128)} %copy.67), calls=%async_computation.1 | async-start | bytes 1048576 | tf_op jit(solution)/shard_map/all_to_all | solution.py:192
  74.1 34.8 %copy-start.2 = (f32[512,512]{1,0:T(8,128)S(1)}, f32[512,512]{1,0:T(8,128)}, u32[]{:S(2)}) copy-start(f32[512,512]{1,0:T(8,128)} %param.15) | copy-start | bytes 3145732

commit v18 on v15

--- a/solution.py
+++ b/solution.py
@@ -99,7 +99,7 @@
     return d_index, j_index, c64, s64, ct, st, c128, s128
 
 
-def fft_filter(spread, diffusivity, eigen_here, bulk_shift, tables):
+def fft_filter(spread, diffusivity, eigen_here, bulk_shift, tables, precision):
     d_index, j_index, c64, s64, ct, st, c128, s128 = tables
     field_count, row_count, slab_width = spread.shape
     gx_count = c64.shape[0]
@@ -107,8 +107,8 @@
     total_cells = gx_count * slab_width
     spread = spread.reshape(field_count, gx_count, rows_here, slab_width)
 
-    a_real = jnp.einsum("kd,fdaj->fkaj", c64, spread, precision=EXACT)
-    a_imag = -jnp.einsum("kd,fdaj->fkaj", s64, spread, precision=EXACT)
+    a_real = jnp.einsum("kd,fdaj->fkaj", c64, spread, precision=precision)
+    a_imag = -jnp.einsum("kd,fdaj->fkaj", s64, spread, precision=precision)
     ct4 = ct[None, :, None, :]
     st4 = st[None, :, None, :]
     b_real = a_real * ct4 + a_imag * st4
@@ -117,7 +117,7 @@
     forward_table = jnp.concatenate(
         [jnp.concatenate([c128, -s128], axis=1), jnp.concatenate([s128, c128], axis=1)], axis=0
     )
-    spec = jnp.einsum("fkaj,jm->fkam", joined, forward_table, precision=EXACT)
+    spec = jnp.einsum("fkaj,jm->fkam", joined, forward_table, precision=precision)
     spec_real = spec[..., :slab_width]
     spec_imag = spec[..., slab_width:]
 
@@ -143,14 +143,14 @@
     inverse_table = jnp.concatenate(
         [jnp.concatenate([c128, s128], axis=1), jnp.concatenate([-s128, c128], axis=1)], axis=0
     )
-    back = jnp.einsum("fkam,mj->fkaj", joined, inverse_table, precision=EXACT)
+    back = jnp.einsum("fkam,mj->fkaj", joined, inverse_table, precision=precision)
     back_real = back[..., :slab_width]
     back_imag = back[..., slab_width:]
     e_real = back_real * ct4 - back_imag * st4
     e_imag = back_real * st4 + back_imag * ct4
     filtered = (
-        jnp.einsum("dk,fkaj->fdaj", c64, e_real, precision=EXACT)
-        - jnp.einsum("dk,fkaj->fdaj", s64, e_imag, precision=EXACT)
+        jnp.einsum("dk,fkaj->fdaj", c64, e_real, precision=precision)
+        - jnp.einsum("dk,fkaj->fdaj", s64, e_imag, precision=precision)
     ) / total_cells
 
     return filtered.reshape(field_count, row_count, slab_width)
@@ -193,9 +193,9 @@
     tables = dft_tables(gx_count, slab_width)
     position = lax.axis_index("gx")
     eigen_here = lax.dynamic_slice_in_dim(wall_eigen, position * rows_here, rows_here)
-    calm = fft_filter(calm, diffusivity[:2], eigen_here, bulk_shift, tables)
+    calm = fft_filter(calm, diffusivity[:2], eigen_here, bulk_shift, tables, EXACT)
     calm, fed = lax.optimization_barrier((calm, fed))
-    fed = fft_filter(fed, diffusivity[2:], eigen_here, bulk_shift, tables)
+    fed = fft_filter(fed, diffusivity[2:], eigen_here, bulk_shift, tables, HI)
     filtered = jnp.concatenate([calm, fed], axis=0)
     filtered = filtered.reshape(field_count, row_count, slab_width)
     gathered = lax.all_to_all(filtered, "gx", 1, 1, tiled=True)

time: 109 us -> 107 us (0.982)
  matrix products: 16.9 us -> 14.9 us
    dot_general x12, matrix products: 11.9 us -> 9.86 us  [the longest x2 2.55 us: fft_filter(): jnp.einsum('fkaj,jm->fkam', joined, forward_table, precision=precision)]
where the time goes in v18:
time: 107 us
  blocking collectives  34.8 us (33%)
  starting transfers between devices  25.8 us (24%)
  matrix products  14.9 us (14%)
  waiting for transfers between devices  14.2 us (13%)
  Pallas kernels  8.84 us (8%)
  local copies, waits for them, and re-layouts  4.46 us (4%)
  other arithmetic  2.76 us (3%)
    all_to_all x1, blocking collectives, per_device(): gathered = lax.all_to_all(filtered, 'gx', 1, 1, tiled=True)  34.8 us
    all_to_all x1, starting transfers between devices, per_device(): calm = lax.all_to_all(calm, 'gx', 1, 1, tiled=True)  13.3 us
    all_to_all x1, waiting for transfers between devices, per_device(): fed = lax.all_to_all(fed, 'gx', 1, 1, tiled=True)  10.4 us
    pallas_call x1, Pallas kernels, drop_source(): pl.pallas_call(source_kernel, grid=(drops // chunk,), in_specs=[pl.BlockS...  8.84 us
    all_to_all x1, starting transfers between devices, per_device(): fed = lax.all_to_all(fed, 'gx', 1, 1, tiled=True)  6.76 us
    ppermute x3, starting transfers between devices, per_device(): lax.ppermute(packed, 'gz', [(i, (i + shift) % gz_count) for i in range(gz...  5.72 us
    all_to_all x1, waiting for transfers between devices, per_device(): calm = lax.all_to_all(calm, 'gx', 1, 1, tiled=True)  3.78 us
    dot_general x2, matrix products, fft_filter(): jnp.einsum('fkaj,jm->fkam', joined, forward_table, precision=precision)  2.55 us
  transfers between devices with their start and end apart: 5, of which 2 were waited for; matrix products, arithmetic and copies ran while one was open for 13% of the time, Pallas kernels for 8%

profile of v18, /device:TPU:1, one launch (start us, length us, event | category | flops | bytes accessed | tf_op | source)
XLA Modules:
  0.0 106.7 jit_solution(7382777842819478620)
XLA Ops:
  0.0 0.7 add_convert_fusion
  0.8 2.1 %collective-permute-start = (f32[3,4096]{1,0:T(4,128)S(1)}, f32[3,4096]{1,0:T(4,128)S(1)}, u32[]{:S(2)}, u32[]{:S(2)}) collective-permute-start(f32[3,4096]{1,0:T(4,128)S(1)} %pad_maximum_fusion.10), channel_id=1, source_target_pairs={{0,1},{1,2},{2,3},{3,0},{4,5},{5,6},{6,7},{7,4},{8,9},{9,10},{10,1... | collective-permute-start | bytes 147464 | tf_op jit(solution)/shard_map/ppermute | solution.py:182
  2.9 2.5 %collective-permute-start.1 = (f32[3,4096]{1,0:T(4,128)S(1)}, f32[3,4096]{1,0:T(4,128)S(1)}, u32[]{:S(2)}, u32[]{:S(2)}) collective-permute-start(f32[3,4096]{1,0:T(4,128)S(1)} %pad_maximum_fusion.10), channel_id=1, source_target_pairs={{0,2},{1,3},{2,0},{3,1},{4,6},{5,7},{6,4},{7,5},{8,10},{9,11},{10,... | collective-permute-start | bytes 147464 | tf_op jit(solution)/shard_map/ppermute | solution.py:182
  5.4 1.2 %collective-permute-start.2 = (f32[3,4096]{1,0:T(4,128)S(1)}, f32[3,4096]{1,0:T(4,128)S(1)}, u32[]{:S(2)}, u32[]{:S(2)}) collective-permute-start(f32[3,4096]{1,0:T(4,128)S(1)} %pad_maximum_fusion.10), channel_id=1, source_target_pairs={{0,3},{1,0},{2,1},{3,2},{4,7},{5,4},{6,5},{7,6},{8,11},{9,8},{10,9... | collective-permute-start | bytes 147464 | tf_op jit(solution)/shard_map/ppermute | solution.py:182
  6.5 1.9 %convolution_bitcast_fusion.4 = f32[2,512,128]{2,1,0:T(8,128)S(1)} fusion(f32[512,512]{1,0:T(8,128)} %param.16, f32[4,1,512,128]{3,2,0,1:T(8,128)} %bitcast.87), kind=kOutput, calls=%fused_computation.10 | convolution fusion | flops 403439616 | bytes 2097152 | tf_op jit(solution)/shard_map/ay,fyx->fax/dot_general | solution.py:189
  8.5 1.2 %copy.58 = f32[2,512,128]{2,0,1:T(2,128)} copy(f32[2,512,128]{2,1,0:T(8,128)S(1)} %convolution_bitcast_fusion.4) | data formatting | bytes 1048576 | tf_op jit(solution)/shard_map/ay,fyx->fax/transpose | solution.py:189
  9.7 13.3 %all-to-all-start = ((f32[2,512,128]{2,0,1:T(2,128)}), f32[2,512,128]{2,0,1:T(2,128)S(1)}, u32[]{:S(2)}, u32[]{:S(2)}) async-start(f32[2,512,128]{2,0,1:T(2,128)} %copy.58), calls=%async_computation | async-start | bytes 1048576 | tf_op jit(solution)/shard_map/all_to_all | solution.py:190
  24.2 0.8 dynamic_slice.3
  25.6 8.8 %shard_map.91 = f32[2,512,128]{2,1,0:T(8,128)S(1)} custom-call(s32[1]{0:T(128)} %bitcast.20.plane_ref, f32[3,16384]{1,0:T(4,128)S(1)} %pad_maximum_fusion.9.packed_ref, f32[4,1,512,128]{3,2,1,0:T(8,128)S(1)} %copy-done), custom_call_target="tpu_custom_call" | custom-call | flops 8589934592 | bytes 1048576 | tf_op jit(solution)/shard_map/pallas_call | solution.py:74
  34.5 1.1 %convolution_bitcast_fusion.2 = f32[2,512,128]{1,2,0:T(8,128)S(1)} fusion(f32[2,512,128]{2,1,0:T(8,128)S(1)} %shard_map.91, f32[512,512]{1,0:T(8,128)S(1)} %copy-done.1), kind=kOutput, calls=%fused_computation.6 | convolution fusion | flops 403439616 | bytes 2097152 | tf_op jit(solution)/shard_map/ay,fyx->fax/dot_general | solution.py:191
  35.6 1.0 copy.67
  36.6 3.8 %all-to-all-done = f32[2,512,128]{2,0,1:T(2,128)S(1)} async-done(((f32[2,512,128]{2,0,1:T(2,128)}), f32[2,512,128]{2,0,1:T(2,128)S(1)}, u32[]{:S(2)}, u32[]{:S(2)}) %all-to-all-start) | async-done | bytes 524320 | tf_op jit(solution)/shard_map/all_to_all | solution.py:190
  40.3 6.8 %all-to-all-start.1 = ((f32[2,512,128]{2,0,1:T(2,128)}), f32[2,512,128]{2,0,1:T(2,128)S(1)}, u32[]{:S(2)}, u32[]{:S(2)}) async-start(f32[2,512,128]{2,0,1:T(2,128)} %copy.67), calls=%async_computation.1 | async-start | bytes 1048576 | tf_op jit(solution)/shard_map/all_to_all | solution.py:192
  47.2 0.8 convolution_bitcast_fusion.3
  47.9 0.9 multiply_add_fusion.5
  48.9 1.5 %fusion.16 = f32[2,64,8,256]{3,2,1,0:T(8,128)S(1)} fusion(f32[2,64,8,256]{3,1,2,0:T(8,128)S(1)} %pad_maximum_fusion, f32[128,128]{1,0:T(8,128)S(1)} %get-tuple-element.25, f32[128,128]{1,0:T(8,128)S(1)} %get-tuple-element.24, f32[128,128]{1,0:T(8,128)S(1)} %fusion.99), kind=kOutput, calls=%fused_computation.31 | convolution fusion | flops 805502976 | bytes 2293760 | tf_op jit(solution)/shard_map/fkaj,jm->fkam/dot_general | solution.py:120
  50.4 0.3 multiply_subtract_fusion.4
  50.8 1.2 %fusion.11 = f32[2,64,8,256]{3,1,2,0:T(8,128)S(1)} fusion(f32[2,64,8,256]{3,2,1,0:T(8,128)S(1)} %pad_maximum_fusion.1, f32[128,128]{1,0:T(8,128)S(1)} %get-tuple-element.25, f32[128,128]{1,0:T(8,128)S(1)} %fusion.99, f32[128,128]{1,0:T(8,128)S(1)} %get-tuple-element.24), kind=kOutput, calls=%fused_computation.26 | convolution fusion | flops 805502976 | bytes 2293760 | tf_op jit(solution)/shard_map/fkam,mj->fkaj/dot_general | solution.py:146
  51.9 0.8 fusion.32
  52.7 0.8 fusion.5
  53.8 10.4 %all-to-all-done.1 = f32[2,512,128]{2,0,1:T(2,128)S(1)} async-done(((f32[2,512,128]{2,0,1:T(2,128)}), f32[2,512,128]{2,0,1:T(2,128)S(1)}, u32[]{:S(2)}, u32[]{:S(2)}) %all-to-all-start.1) | async-done | bytes 524320 | tf_op jit(solution)/shard_map/all_to_all | solution.py:192
  64.3 0.5 convolution_bitcast_fusion.1
  64.8 0.6 multiply_add_fusion.3
  65.5 1.1 %fusion.14 = f32[2,64,8,256]{3,2,1,0:T(8,128)S(1)} fusion(f32[2,64,8,256]{3,1,2,0:T(8,128)S(1)} %pad_maximum_fusion.2, f32[128,128]{1,0:T(8,128)S(1)} %get-tuple-element.25, f32[128,128]{1,0:T(8,128)S(1)} %get-tuple-element.24, f32[128,128]{1,0:T(8,128)S(1)} %fusion.99), kind=kOutput, calls=%fused_computation.29 | convolution fusion | flops 402849792 | bytes 2293760 | tf_op jit(solution)/shard_map/fkaj,jm->fkam/dot_general | solution.py:120
  66.6 0.3 multiply_subtract_fusion.2
  67.0 0.8 fusion.9
  67.8 0.5 fusion.25
  68.3 0.5 fusion.3
  68.8 0.3 copy.113
  69.2 0.7 copy.75
  69.9 34.8 %all_to_all.15 = f32[4,512,128]{2,0,1:T(4,128)S(1)} all-to-all(f32[4,512,128]{2,0,1:T(4,128)S(1)} %copy.75), channel_id=1, replica_groups=mesh['gx'=64,'gz'=4] {'gx'}, dimensions={1} | all-to-all | bytes 2097152 | tf_op jit(solution)/shard_map/all_to_all | solution.py:201
  104.7 2.0 %convolution_bitcast_fusion = f32[4,1,512,128]{3,2,1,0:T(8,128)} fusion(f32[512,512]{1,0:T(8,128)S(1)} %copy-done.2, f32[4,512,128]{2,0,1:T(4,128)S(1)} %all_to_all.15), kind=kOutput, calls=%fused_computation.2 | convolution fusion | flops 806092800 | bytes 3145728 | tf_op jit(solution)/shard_map/fax,ya->fyx/dot_general | solution.py:202
  (30 shorter events, 1.9 us)
Async XLA Ops:
  0.0 0.8 copy-start.3
  0.8 24.7 %collective-permute-start = (f32[3,4096]{1,0:T(4,128)S(1)}, f32[3,4096]{1,0:T(4,128)S(1)}, u32[]{:S(2)}, u32[]{:S(2)}) collective-permute-start(f32[3,4096]{1,0:T(4,128)S(1)} %pad_maximum_fusion.10), channel_id=1, source_target_pairs={{0,1},{1,2},{2,3},{3,0},{4,5},{5,6},{6,7},{7,4},{8,9},{9,10},{10,1... | collective-permute-start | bytes 147464 | tf_op jit(solution)/shard_map/ppermute | solution.py:182
  2.9 22.6 %collective-permute-start.1 = (f32[3,4096]{1,0:T(4,128)S(1)}, f32[3,4096]{1,0:T(4,128)S(1)}, u32[]{:S(2)}, u32[]{:S(2)}) collective-permute-start(f32[3,4096]{1,0:T(4,128)S(1)} %pad_maximum_fusion.10), channel_id=1, source_target_pairs={{0,2},{1,3},{2,0},{3,1},{4,6},{5,7},{6,4},{7,5},{8,10},{9,11},{10,... | collective-permute-start | bytes 147464 | tf_op jit(solution)/shard_map/ppermute | solution.py:182
  5.4 20.1 %collective-permute-start.2 = (f32[3,4096]{1,0:T(4,128)S(1)}, f32[3,4096]{1,0:T(4,128)S(1)}, u32[]{:S(2)}, u32[]{:S(2)}) collective-permute-start(f32[3,4096]{1,0:T(4,128)S(1)} %pad_maximum_fusion.10), channel_id=1, source_target_pairs={{0,3},{1,0},{2,1},{3,2},{4,7},{5,4},{6,5},{7,6},{8,11},{9,8},{10,9... | collective-permute-start | bytes 147464 | tf_op jit(solution)/shard_map/ppermute | solution.py:182
  9.7 15.9 %copy-start = (f32[4,1,512,128]{3,2,1,0:T(8,128)S(1)}, f32[4,1,512,128]{3,2,1,0:T(8,128)}, u32[]{:S(2)}) copy-start(f32[4,1,512,128]{3,2,1,0:T(8,128)} %field_ref.1) | copy-start | bytes 3145732
  9.7 30.6 %all-to-all-start = ((f32[2,512,128]{2,0,1:T(2,128)}), f32[2,512,128]{2,0,1:T(2,128)S(1)}, u32[]{:S(2)}, u32[]{:S(2)}) async-start(f32[2,512,128]{2,0,1:T(2,128)} %copy.58), calls=%async_computation | async-start | bytes 1048576 | tf_op jit(solution)/shard_map/all_to_all | solution.py:190
  23.5 0.7 copy-start.4
  25.6 8.9 %copy-start.1 = (f32[512,512]{1,0:T(8,128)S(1)}, f32[512,512]{1,0:T(8,128)}, u32[]{:S(2)}) copy-start(f32[512,512]{1,0:T(8,128)} %param.16) | copy-start | bytes 3145732
  40.3 23.9 %all-to-all-start.1 = ((f32[2,512,128]{2,0,1:T(2,128)}), f32[2,512,128]{2,0,1:T(2,128)S(1)}, u32[]{:S(2)}, u32[]{:S(2)}) async-start(f32[2,512,128]{2,0,1:T(2,128)} %copy.67), calls=%async_computation.1 | async-start | bytes 1048576 | tf_op jit(solution)/shard_map/all_to_all | solution.py:192
  69.9 34.8 %copy-start.2 = (f32[512,512]{1,0:T(8,128)S(1)}, f32[512,512]{1,0:T(8,128)}, u32[]{:S(2)}) copy-start(f32[512,512]{1,0:T(8,128)} %param.15) | copy-start | bytes 3145732
